TPU v7x, 512 devices: a whole 4x8x8 slice. The times are simulated.
512 devices in a mesh: ep: 128 (over y, z, core), tp: 4 (over x).
Axes of the slice: x: 4, y: 8, z: 8, core: 2. Of those that a mesh axis runs over, the one named last changes fastest.
Arguments:
- tokens: bfloat16 [16384, 2048], P('ep'), may hold values from -6 to 6
- expert_ids: int32 [16384, 2], P('ep'), may hold values from 0 to 127, all different within a row; in each aligned block of 128 rows (0 to 127, 128 to 255, ...) at most 4 rows name the same one
- gate_values: float32 [16384, 2], P('ep'), may hold values from 0.2 to 1
- w_gate: bfloat16 [128, 2048, 1408], P('ep', None, 'tp'), may hold values from -0.125 to 0.125
- w_up: bfloat16 [128, 2048, 1408], P('ep', None, 'tp'), may hold values from -0.125 to 0.125
- w_down: bfloat16 [128, 1408, 2048], P('ep', 'tp'), may hold values from -0.15625 to 0.15625
Outputs:
- mixed: bfloat16 [16384, 2048], P('ep', 'tp')
Inputs may be any that keep to these rules, and one draw needn't show every extreme that they name: `expert_ids`: the two experts of a row differ. Within the 128 rows of one block, no expert is chosen more than 4 times, and in every draw some expert is chosen exactly 4 times in some block.
All inputs are finite; a program needn't handle non-finite values.
Results may differ from a plain program's by a relative error of at most 0.017.
Values may be sent and summed in bfloat16 or wider, within the bound.
No kernel may reach another device: no remote copies, remote signals or barrier semaphores. Data moves between devices by JAX's collectives and lax.ppermute only.
A program may use at most 64 MiB of HBM per device.

v0:
```python
import jax
import jax.numpy as jnp
from jax import lax
from jax.sharding import PartitionSpec as P


def shards(tokens, expert_ids, gate_values, w_gate, w_up, w_down):
    tok_rows = tokens.shape[0]
    width = tokens.shape[1]
    experts = lax.axis_size("ep")
    groups = lax.axis_size("tp")
    quarter = width // groups
    capacity = 4 * tok_rows // experts
    row_count = experts * capacity
    flat_ids = expert_ids.reshape(-1)
    onehot = (flat_ids[:, None] == jnp.arange(experts, dtype=jnp.int32)[None, :]).astype(jnp.int32)
    running = jnp.cumsum(onehot, axis=0)
    position = jnp.sum(running * onehot, axis=1) - 1
    target = (flat_ids * capacity + position).reshape(tok_rows, 2)
    slot_iota = jnp.arange(row_count, dtype=jnp.int32)
    first_hit = target[:, 0][None, :] == slot_iota[:, None]
    second_hit = target[:, 1][None, :] == slot_iota[:, None]
    placer = (first_hit | second_hit).astype(jnp.bfloat16)
    gate_mat = w_gate[0]
    up_mat = w_up[0]
    down_mat = w_down[0]
    outbound = jnp.dot(placer, tokens, preferred_element_type=jnp.float32).astype(jnp.bfloat16)
    arrived = lax.all_to_all(
        outbound.reshape(experts, capacity, width), "ep", split_axis=0, concat_axis=0, tiled=True
    )
    arrived = arrived.reshape(row_count, width)
    gate = jnp.dot(arrived, gate_mat, preferred_element_type=jnp.float32)
    up = jnp.dot(arrived, up_mat, preferred_element_type=jnp.float32)
    hidden = (jax.nn.silu(gate) * up).astype(jnp.bfloat16)
    partial_out = jnp.dot(hidden, down_mat, preferred_element_type=jnp.float32).astype(jnp.bfloat16)
    combine_w = gate_values[:, 0][:, None] * (target[:, 0][:, None] == slot_iota[None, :]).astype(
        jnp.float32
    )
    combine_w = combine_w + gate_values[:, 1][:, None] * (
        target[:, 1][:, None] == slot_iota[None, :]
    ).astype(jnp.float32)
    summed = lax.psum_scatter(
        partial_out.astype(jnp.float32).astype(jnp.bfloat16), "tp", scatter_dimension=1, tiled=True
    ).astype(jnp.float32)
    returned = lax.all_to_all(
        summed.reshape(experts, capacity, quarter).astype(jnp.bfloat16),
        "ep",
        split_axis=0,
        concat_axis=0,
        tiled=True,
    ).astype(jnp.float32)
    returned = returned.reshape(row_count, quarter)
    mixed = jnp.dot(combine_w, returned, precision=lax.Precision.HIGHEST)
    return mixed.astype(jnp.bfloat16)


def solution(mesh):
    placed = (
        P("ep", None),
        P("ep", None),
        P("ep", None),
        P("ep", None, "tp"),
        P("ep", None, "tp"),
        P("ep", "tp", None),
    )
    return jax.shard_map(
        shards, mesh=mesh, in_specs=placed, out_specs=P("ep", "tp"), check_vma=False
    )
```

profile of v0, /device:TPU:1, one launch (start us, length us, event | category | flops | bytes accessed | tf_op | source)
XLA Modules:
  0.0 170.1 jit_solution(12016268016702917788)
XLA Ops:
  6.5 0.0 copy-start
  6.5 0.0 reduce-scatter.2.cloned.1.call-start
  6.5 0.9 copy.19
  7.4 0.1 eq.85
  7.6 0.1 eq.81
  7.7 0.1 copy.21
  7.8 0.2 fusion.24
  8.1 0.2 fusion.25
  8.3 0.1 sub.7
  8.5 0.1 copy.23
  8.5 0.7 multiply_add_fusion
  9.2 3.1 %convolution_convert_fusion.1 = bf16[512,2048]{1,0:T(8,128)(2,1)} fusion(bf16[128,2048]{1,0:T(8,128)(2,1)} %param.6, s32[128]{0:T(128)S(1)} %get-tuple-element.8, s32[128]{0:T(128)S(1)} %get-tuple-element.7), kind=kOutput, calls=%fused_computation.1 | convolution fusion | flops 269680640 | bytes 2622464 | tf_op jit(solution)/shard_map/dot_general | solution.py:27
  12.3 2.7 %reshape.36 = bf16[128,4,2048]{2,1,0:T(4,128)(2,1)S(1)} reshape(bf16[512,2048]{1,0:T(8,128)(2,1)} %convolution_convert_fusion.1) | data formatting | bytes 4194304 | tf_op jit(solution)/shard_map/reshape | solution.py:29
  15.1 70.5 %all_to_all.10 = bf16[128,4,2048]{2,1,0:T(4,128)(2,1)} all-to-all(bf16[128,4,2048]{2,1,0:T(4,128)(2,1)S(1)} %reshape.36), channel_id=1, replica_groups=mesh['ep'=128,'tp'=4] {'ep'}, dimensions={0} | all-to-all | bytes 4194304 | tf_op jit(solution)/shard_map/all_to_all | solution.py:28
  85.5 2.5 %reshape.37 = bf16[512,2048]{1,0:T(8,128)(2,1)S(1)} reshape(bf16[128,4,2048]{2,1,0:T(4,128)(2,1)} %all_to_all.10) | data formatting | bytes 4194304 | tf_op jit(solution)/shard_map/reshape | solution.py:31
  88.1 3.2 %fusion.3 = f32[512,352]{0,1:T(8,128)} fusion(bf16[512,2048]{1,0:T(8,128)(2,1)S(1)} %reshape.37, bf16[1,2048,352]{1,2,0:T(8,128)(2,1)} %param.9), kind=kOutput, calls=%fused_computation.5 | convolution fusion | flops 738197504 | bytes 4259840 | tf_op jit(solution)/shard_map/dot_general | solution.py:32
  91.3 0.0 copy-done
  91.3 5.1 %convolution_convert_fusion = bf16[512,2048]{1,0:T(8,128)(2,1)} fusion(bf16[1,352,2048]{2,1,0:T(8,128)(2,1)S(1)} %copy-done, bf16[512,2048]{1,0:T(8,128)(2,1)S(1)} %reshape.37, bf16[1,2048,352]{1,2,0:T(8,128)(2,1)} %param.10, f32[512,352]{0,1:T(8,128)} %fusion.3), kind=kOutput, calls=%fused_computation | convolution fusion | flops 1478524928 | bytes 7798784 | tf_op jit(solution)/shard_map/dot_general | solution.py:35
  96.4 0.0 copy-start.1
  96.4 0.0 reduce-scatter.2.cloned.1.call-update
  96.4 29.9 %reduce-scatter.2.cloned.1.call-done = bf16[512,512]{1,0:T(8,128)(2,1)} async-done(((bf16[512,2048]{1,0:T(8,128)(2,1)}), bf16[512,512]{1,0:T(8,128)(2,1)}) %reduce-scatter.2.cloned.1.call-update) | async-done | bytes 524304 | tf_op jit(solution)/shard_map/reduce_scatter | solution.py:42
  126.3 2.0 %convert_element_type.32 = bf16[128,4,512]{2,1,0:T(4,128)(2,1)} reshape(bf16[512,512]{1,0:T(8,128)(2,1)} %reduce-scatter.2.cloned.1.call-done) | data formatting | bytes 1048576 | tf_op jit(solution)/shard_map/convert_element_type | solution.py:46
  128.3 14.4 %all-to-all-start.1 = ((bf16[128,4,512]{2,1,0:T(4,128)(2,1)}), bf16[128,4,512]{2,1,0:T(4,128)(2,1)S(1)}, u32[]{:S(2)}, u32[]{:S(2)}) async-start(bf16[128,4,512]{2,1,0:T(4,128)(2,1)} %convert_element_type.32), calls=%async_computation.2 | async-start | bytes 1048576 | tf_op jit(solution)/shard_map/all_to_all | solution.py:45
  142.6 0.0 copy-done.1
  142.7 19.4 %all-to-all-done.1 = bf16[128,4,512]{2,1,0:T(4,128)(2,1)S(1)} async-done(((bf16[128,4,512]{2,1,0:T(4,128)(2,1)}), bf16[128,4,512]{2,1,0:T(4,128)(2,1)S(1)}, u32[]{:S(2)}, u32[]{:S(2)}) %all-to-all-start.1) | async-done | bytes 524320 | tf_op jit(solution)/shard_map/all_to_all | solution.py:45
  162.1 0.1 reshape.38
  162.2 1.1 convolution_convert_fusion.2
  (9 shorter events, 0.1 us)
Async XLA Ops:
  6.5 84.8 %copy-start = (bf16[1,352,2048]{2,1,0:T(8,128)(2,1)S(1)}, bf16[1,352,2048]{2,1,0:T(8,128)(2,1)}, u32[]{:S(2)}) copy-start(bf16[1,352,2048]{2,1,0:T(8,128)(2,1)} %param.11) | copy-start | bytes 4325380
  6.5 119.8 %reduce-scatter.2.cloned.1.call-start = ((), (), s32[]{:S(2)}) async-start(), calls=%async_computation.3 | async-start | bytes 2621440 | tf_op jit(solution)/shard_map/reduce_scatter | solution.py:42
  96.4 46.2 %copy-start.1 = (f32[128,2]{0,1:T(2,128)S(1)}, f32[128,2]{0,1:T(2,128)}, u32[]{:S(2)}) copy-start(f32[128,2]{0,1:T(2,128)} %param.8) | copy-start | bytes 3076
  128.3 33.8 %all-to-all-start.1 = ((bf16[128,4,512]{2,1,0:T(4,128)(2,1)}), bf16[128,4,512]{2,1,0:T(4,128)(2,1)S(1)}, u32[]{:S(2)}, u32[]{:S(2)}) async-start(bf16[128,4,512]{2,1,0:T(4,128)(2,1)} %convert_element_type.32), calls=%async_computation.2 | async-start | bytes 1048576 | tf_op jit(solution)/shard_map/all_to_all | solution.py:45
Sparse Core Ops, SparseCore 0:
  96.5 29.7 reduce-scatter.1
where the time goes:
time: 171 us; the launch traced here: 170 us
  blocking collectives  70.5 us (41%)
  waiting for transfers between devices  49.3 us (29%)
  starting transfers between devices  14.4 us (8%)
  between operations  13.5 us (8%)
  matrix products  12.5 us (7%)
  local copies, waits for them, and re-layouts  8.87 us (5%)
    all_to_all x1, blocking collectives, shards(): lax.all_to_all(outbound.reshape(experts, capacity, width), 'ep', split_ax...  70.5 us
    reduce_scatter x1, waiting for transfers between devices, shards(): lax.psum_scatter(partial_out.astype(jnp.float32).astype(jnp.bfloat16), 't...  29.9 us
    all_to_all x1, waiting for transfers between devices, shards(): lax.all_to_all(summed.reshape(experts, capacity, quarter).astype(jnp.bflo...  19.4 us
    all_to_all x1, starting transfers between devices, shards(): lax.all_to_all(summed.reshape(experts, capacity, quarter).astype(jnp.bflo...  14.4 us
    dot_general x1, matrix products, shards(): jnp.dot(hidden, down_mat, preferred_element_type=jnp.float32)  5.11 us
  transfers between devices with their start and end apart: 2, of which 2 were waited for; matrix products, arithmetic and copies ran while one was open for 0% of the time, Pallas kernels for 0%

commit v1 on v0

--- a/solution.py
+++ b/solution.py
@@ -21,35 +21,30 @@
     first_hit = target[:, 0][None, :] == slot_iota[:, None]
     second_hit = target[:, 1][None, :] == slot_iota[:, None]
     placer = (first_hit | second_hit).astype(jnp.bfloat16)
-    gate_mat = w_gate[0]
-    up_mat = w_up[0]
-    down_mat = w_down[0]
     outbound = jnp.dot(placer, tokens, preferred_element_type=jnp.float32).astype(jnp.bfloat16)
     arrived = lax.all_to_all(
         outbound.reshape(experts, capacity, width), "ep", split_axis=0, concat_axis=0, tiled=True
     )
     arrived = arrived.reshape(row_count, width)
-    gate = jnp.dot(arrived, gate_mat, preferred_element_type=jnp.float32)
-    up = jnp.dot(arrived, up_mat, preferred_element_type=jnp.float32)
+    gate = jnp.dot(arrived, w_gate[0], preferred_element_type=jnp.float32)
+    up = jnp.dot(arrived, w_up[0], preferred_element_type=jnp.float32)
     hidden = (jax.nn.silu(gate) * up).astype(jnp.bfloat16)
-    partial_out = jnp.dot(hidden, down_mat, preferred_element_type=jnp.float32).astype(jnp.bfloat16)
+    down_q = w_down[0].reshape(w_down.shape[1], groups, quarter)
+    partial_out = jnp.einsum(
+        "rf,fqd->qrd", hidden, down_q, preferred_element_type=jnp.float32
+    ).astype(jnp.bfloat16)
+    gathered = lax.all_to_all(partial_out, "tp", split_axis=0, concat_axis=0, tiled=True)
+    summed = jnp.sum(gathered.astype(jnp.float32), axis=0).astype(jnp.bfloat16)
+    returned = lax.all_to_all(
+        summed.reshape(experts, capacity, quarter), "ep", split_axis=0, concat_axis=0, tiled=True
+    )
+    returned = returned.reshape(row_count, quarter).astype(jnp.float32)
     combine_w = gate_values[:, 0][:, None] * (target[:, 0][:, None] == slot_iota[None, :]).astype(
         jnp.float32
     )
     combine_w = combine_w + gate_values[:, 1][:, None] * (
         target[:, 1][:, None] == slot_iota[None, :]
     ).astype(jnp.float32)
-    summed = lax.psum_scatter(
-        partial_out.astype(jnp.float32).astype(jnp.bfloat16), "tp", scatter_dimension=1, tiled=True
-    ).astype(jnp.float32)
-    returned = lax.all_to_all(
-        summed.reshape(experts, capacity, quarter).astype(jnp.bfloat16),
-        "ep",
-        split_axis=0,
-        concat_axis=0,
-        tiled=True,
-    ).astype(jnp.float32)
-    returned = returned.reshape(row_count, quarter)
     mixed = jnp.dot(combine_w, returned, precision=lax.Precision.HIGHEST)
     return mixed.astype(jnp.bfloat16)
 

time: 171 us -> 151 us (0.88)
  blocking collectives: 70.5 us -> 28.8 us
  waiting for transfers between devices: 49.3 us -> 67.1 us
  starting transfers between devices: 14.4 us -> 28 us
  between operations: 13.5 us -> 0.1 us
  local copies, waits for them, and re-layouts: 8.87 us -> 12.3 us
    all_to_all x1 -> x2, waiting for transfers between devices: 19.4 us -> 67.1 us  [the longest x1 47.7 us: shards(): lax.all_to_all(outbound.reshape(experts, capacity, width), 'ep', split_ax...]
    all_to_all x1, blocking collectives: 70.5 us -> 28.8 us  [shards(): lax.all_to_all(partial_out, 'tp', split_axis=0, concat_axis=0, tiled=True)]
    reduce_scatter x1 -> x0, waiting for transfers between devices: 29.9 us -> none  [shards(): lax.psum_scatter(partial_out.astype(jnp.float32).astype(jnp.bfloat16), 't...]
    all_to_all x1 -> x2, starting transfers between devices: 14.4 us -> 28 us  [the longest x1 18.4 us: shards(): lax.all_to_all(outbound.reshape(experts, capacity, width), 'ep', split_ax...]
    another operation x3 -> x4, local copies, waits for them, and re-layouts: 0.02 us -> 4.41 us  [the longest x1 4.39 us: shards(): down_q = w_down[0].reshape(w_down.shape[1], groups, quarter)]
    reshape x1 -> x2, local copies, waits for them, and re-layouts: 0.12 us -> 2.1 us  [the longest x1 1.98 us: shards(): summed.reshape(experts, capacity, quarter)]
    convert_element_type x1 -> x0, local copies, waits for them, and re-layouts: 1.96 us -> none  [shards(): summed.reshape(experts, capacity, quarter).astype(jnp.bfloat16)]
  transfers between devices with their start and end apart: 2 -> 2, of which waited for: 2 -> 2; matrix products, arithmetic and copies ran while one was open for 0% -> 3% of each run, Pallas kernels for 0% -> 0%
where the time goes in v1:
time: 151 us
  waiting for transfers between devices  67.1 us (44%)
  blocking collectives  28.8 us (19%)
  starting transfers between devices  28 us (19%)
  local copies, waits for them, and re-layouts  12.3 us (8%)
  matrix products  12 us (8%)
  other arithmetic  2.38 us (2%)
    all_to_all x1, waiting for transfers between devices, shards(): lax.all_to_all(outbound.reshape(experts, capacity, width), 'ep', split_ax...  47.7 us
    all_to_all x1, blocking collectives, shards(): lax.all_to_all(partial_out, 'tp', split_axis=0, concat_axis=0, tiled=True)  28.8 us
    all_to_all x1, waiting for transfers between devices, shards(): lax.all_to_all(summed.reshape(experts, capacity, quarter), 'ep', split_ax...  19.4 us
    all_to_all x1, starting transfers between devices, shards(): lax.all_to_all(outbound.reshape(experts, capacity, width), 'ep', split_ax...  18.4 us
    all_to_all x1, starting transfers between devices, shards(): lax.all_to_all(summed.reshape(experts, capacity, quarter), 'ep', split_ax...  9.61 us
    dot_general x1, matrix products, shards(): jnp.einsum('rf,fqd->qrd', hidden, down_q, preferred_element_type=jnp.floa...  5.2 us
    another operation x1, local copies, waits for them, and re-layouts, shards(): down_q = w_down[0].reshape(w_down.shape[1], groups, quarter)  4.39 us
    dot_general x1, matrix products, shards(): gate = jnp.dot(arrived, w_gate[0], preferred_element_type=jnp.float32)  3.95 us
  transfers between devices with their start and end apart: 2, of which 2 were waited for; matrix products, arithmetic and copies ran while one was open for 3% of the time, Pallas kernels for 0%

profile of v1, /device:TPU:1, one launch (start us, length us, event | category | flops | bytes accessed | tf_op | source)
XLA Modules:
  0.0 150.7 jit_solution(17165572222057217435)
XLA Ops:
  0.0 0.0 copy-start
  0.0 0.9 copy.22
  0.9 0.1 eq.85
  1.0 0.1 eq.81
  1.2 0.1 copy.24
  1.3 0.2 fusion.27
  1.6 0.2 fusion.28
  1.8 0.1 sub.7
  1.9 0.1 copy.26
  2.0 0.7 multiply_add_fusion
  2.7 1.7 %convolution_convert_fusion = bf16[512,2048]{1,0:T(8,128)(2,1)S(1)} fusion(bf16[128,2048]{1,0:T(8,128)(2,1)} %param.6, s32[128]{0:T(128)S(1)} %get-tuple-element.8, s32[128]{0:T(128)S(1)} %get-tuple-element.7), kind=kOutput, calls=%fused_computation | convolution fusion | flops 269680640 | bytes 2622464 | tf_op jit(solution)/shard_map/dot_general | solution.py:24
  4.5 2.2 %reshape.37 = bf16[128,4,2048]{2,1,0:T(4,128)(2,1)} reshape(bf16[512,2048]{1,0:T(8,128)(2,1)S(1)} %convolution_convert_fusion) | data formatting | bytes 4194304 | tf_op jit(solution)/shard_map/reshape | solution.py:26
  6.7 18.4 %all-to-all-start = ((bf16[128,4,2048]{2,1,0:T(4,128)(2,1)}), bf16[128,4,2048]{2,1,0:T(4,128)(2,1)S(1)}, u32[]{:S(2)}, u32[]{:S(2)}) async-start(bf16[128,4,2048]{2,1,0:T(4,128)(2,1)} %reshape.37), calls=%async_computation | async-start | bytes 4194304 | tf_op jit(solution)/shard_map/all_to_all | solution.py:25
  25.1 4.4 %reshape_squeeze.3 = bf16[352,4,512]{2,1,0:T(4,128)(2,1)} reshape(bf16[1,352,2048]{2,1,0:T(8,128)(2,1)} %param.11) | data formatting | bytes 2883584 | tf_op jit(solution)/shard_map/reshape;squeeze | solution.py:32
  29.5 47.7 %all-to-all-done = bf16[128,4,2048]{2,1,0:T(4,128)(2,1)S(1)} async-done(((bf16[128,4,2048]{2,1,0:T(4,128)(2,1)}), bf16[128,4,2048]{2,1,0:T(4,128)(2,1)S(1)}, u32[]{:S(2)}, u32[]{:S(2)}) %all-to-all-start) | async-done | bytes 2097184 | tf_op jit(solution)/shard_map/all_to_all | solution.py:25
  77.2 2.1 %reshape.38 = bf16[512,2048]{1,0:T(8,128)(2,1)} reshape(bf16[128,4,2048]{2,1,0:T(4,128)(2,1)S(1)} %all-to-all-done) | data formatting | bytes 4194304 | tf_op jit(solution)/shard_map/reshape | solution.py:28
  79.3 0.0 copy-start.1
  79.3 3.9 %fusion.2 = f32[512,352]{0,1:T(8,128)} fusion(bf16[512,2048]{1,0:T(8,128)(2,1)} %reshape.38, bf16[1,2048,352]{1,2,0:T(8,128)(2,1)} %param.9), kind=kOutput, calls=%fused_computation.4 | convolution fusion | flops 738197504 | bytes 4259840 | tf_op jit(solution)/shard_map/dot_general | solution.py:29
  83.3 0.0 copy-done
  83.3 0.0 copy-done.1
  83.3 5.2 %convert_bitcast_fusion = bf16[4,512,512]{2,1,0:T(8,128)(2,1)} fusion(bf16[352,4,512]{2,1,0:T(4,128)(2,1)} %reshape_squeeze.3, bf16[512,2048]{1,0:T(8,128)(2,1)S(1)} %copy-done.1, bf16[1,2048,352]{1,2,0:T(8,128)(2,1)S(1)} %copy-done, f32[512,352]{0,1:T(8,128)} %fusion.2), kind=kOutput, calls=%fused_computation.1 | convolution fusion | flops 1478524928 | bytes 7798784 | tf_op jit(solution)/shard_map/rf,fqd->qrd/dot_general | solution.py:33
  88.5 28.8 %all_to_all.15 = bf16[4,512,512]{2,1,0:T(8,128)(2,1)S(1)} all-to-all(bf16[4,512,512]{2,1,0:T(8,128)(2,1)} %convert_bitcast_fusion), channel_id=1, replica_groups=mesh['ep'=128,'tp'=4] {'tp'}, dimensions={0} | all-to-all | bytes 4194304 | tf_op jit(solution)/shard_map/all_to_all | solution.py:36
  117.2 0.0 copy-start.2
  117.2 1.2 reduce_sum.22
  118.5 2.0 %reshape.39 = bf16[128,4,512]{2,1,0:T(4,128)(2,1)} reshape(bf16[512,512]{1,0:T(8,128)(2,1)} %reduce_sum.22) | data formatting | bytes 1048576 | tf_op jit(solution)/shard_map/reshape | solution.py:39
  120.5 9.6 %all-to-all-start.2 = ((bf16[128,4,512]{2,1,0:T(4,128)(2,1)}), bf16[128,4,512]{2,1,0:T(4,128)(2,1)S(1)}, u32[]{:S(2)}, u32[]{:S(2)}) async-start(bf16[128,4,512]{2,1,0:T(4,128)(2,1)} %reshape.39), calls=%async_computation.2 | async-start | bytes 1048576 | tf_op jit(solution)/shard_map/all_to_all | solution.py:38
  130.1 0.0 copy-done.2
  130.1 19.4 %all-to-all-done.2 = bf16[128,4,512]{2,1,0:T(4,128)(2,1)S(1)} async-done(((bf16[128,4,512]{2,1,0:T(4,128)(2,1)}), bf16[128,4,512]{2,1,0:T(4,128)(2,1)S(1)}, u32[]{:S(2)}, u32[]{:S(2)}) %all-to-all-start.2) | async-done | bytes 524320 | tf_op jit(solution)/shard_map/all_to_all | solution.py:38
  149.5 0.1 reshape.40
  149.6 1.1 convolution_convert_fusion.1
  (9 shorter events, 0.1 us)
Async XLA Ops:
  0.0 83.3 %copy-start = (bf16[1,2048,352]{1,2,0:T(8,128)(2,1)S(1)}, bf16[1,2048,352]{1,2,0:T(8,128)(2,1)}, u32[]{:S(2)}) copy-start(bf16[1,2048,352]{1,2,0:T(8,128)(2,1)} %param.10) | copy-start | bytes 4325380
  6.7 70.6 %all-to-all-start = ((bf16[128,4,2048]{2,1,0:T(4,128)(2,1)}), bf16[128,4,2048]{2,1,0:T(4,128)(2,1)S(1)}, u32[]{:S(2)}, u32[]{:S(2)}) async-start(bf16[128,4,2048]{2,1,0:T(4,128)(2,1)} %reshape.37), calls=%async_computation | async-start | bytes 4194304 | tf_op jit(solution)/shard_map/all_to_all | solution.py:25
  79.3 4.0 %copy-start.1 = (bf16[512,2048]{1,0:T(8,128)(2,1)S(1)}, bf16[512,2048]{1,0:T(8,128)(2,1)}, u32[]{:S(2)}) copy-start(bf16[512,2048]{1,0:T(8,128)(2,1)} %reshape.38) | copy-start | bytes 6291460
  117.2 12.8 %copy-start.2 = (f32[128,2]{0,1:T(2,128)S(1)}, f32[128,2]{0,1:T(2,128)}, u32[]{:S(2)}) copy-start(f32[128,2]{0,1:T(2,128)} %param.8) | copy-start | bytes 3076
  120.5 29.0 %all-to-all-start.2 = ((bf16[128,4,512]{2,1,0:T(4,128)(2,1)}), bf16[128,4,512]{2,1,0:T(4,128)(2,1)S(1)}, u32[]{:S(2)}, u32[]{:S(2)}) async-start(bf16[128,4,512]{2,1,0:T(4,128)(2,1)} %reshape.39), calls=%async_computation.2 | async-start | bytes 1048576 | tf_op jit(solution)/shard_map/all_to_all | solution.py:38

commit v2 on v1

--- a/solution.py
+++ b/solution.py
@@ -2,6 +2,24 @@
 import jax.numpy as jnp
 from jax import lax
 from jax.sharding import PartitionSpec as P
+
+
+def ring_reduce_scatter(quarter_of, groups, rows):
+    half = rows // 2
+    up = [(i, (i + 1) % groups) for i in range(groups)]
+    down = [(i, (i - 1) % groups) for i in range(groups)]
+    carry_a = None
+    carry_b = None
+    for step in range(1, groups):
+        own_a = quarter_of(groups - step, 0, half)
+        own_b = quarter_of(step, half, rows)
+        send_a = own_a if carry_a is None else own_a + carry_a.astype(jnp.float32)
+        send_b = own_b if carry_b is None else own_b + carry_b.astype(jnp.float32)
+        carry_a = lax.ppermute(send_a.astype(jnp.bfloat16), "tp", up)
+        carry_b = lax.ppermute(send_b.astype(jnp.bfloat16), "tp", down)
+    res_a = quarter_of(0, 0, half) + carry_a.astype(jnp.float32)
+    res_b = quarter_of(0, half, rows) + carry_b.astype(jnp.float32)
+    return jnp.concatenate([res_a, res_b], axis=0)
 
 
 def shards(tokens, expert_ids, gate_values, w_gate, w_up, w_down):
@@ -29,12 +47,15 @@
     gate = jnp.dot(arrived, w_gate[0], preferred_element_type=jnp.float32)
     up = jnp.dot(arrived, w_up[0], preferred_element_type=jnp.float32)
     hidden = (jax.nn.silu(gate) * up).astype(jnp.bfloat16)
-    down_q = w_down[0].reshape(w_down.shape[1], groups, quarter)
-    partial_out = jnp.einsum(
-        "rf,fqd->qrd", hidden, down_q, preferred_element_type=jnp.float32
-    ).astype(jnp.bfloat16)
-    gathered = lax.all_to_all(partial_out, "tp", split_axis=0, concat_axis=0, tiled=True)
-    summed = jnp.sum(gathered.astype(jnp.float32), axis=0).astype(jnp.bfloat16)
+    down = w_down[0]
+    own = lax.axis_index("tp")
+
+    def quarter_of(k, lo, hi):
+        cols = lax.dynamic_slice_in_dim(down, ((own + k) % groups) * quarter, quarter, axis=1)
+        part = jnp.dot(hidden[lo:hi], cols, preferred_element_type=jnp.float32)
+        return part.astype(jnp.bfloat16).astype(jnp.float32)
+
+    summed = ring_reduce_scatter(quarter_of, groups, row_count).astype(jnp.bfloat16)
     returned = lax.all_to_all(
         summed.reshape(experts, capacity, quarter), "ep", split_axis=0, concat_axis=0, tiled=True
     )

time: 151 us -> 150 us (level); the launches traced: 151 us -> 148 us
  blocking collectives: 28.8 us -> 0 us
  starting transfers between devices: 28 us -> 50.9 us
  waiting for transfers between devices: 67.1 us -> 78.6 us
  local copies, waits for them, and re-layouts: 12.3 us -> 6.87 us
  matrix products: 12 us -> 9.47 us
    all_to_all x1 -> x0, blocking collectives: 28.8 us -> none  [shards(): lax.all_to_all(partial_out, 'tp', split_axis=0, concat_axis=0, tiled=True)]
    ppermute x0 -> x6, starting transfers between devices: none -> 19.5 us  [the longest x3 12.5 us: ring_reduce_scatter(): carry_b = lax.ppermute(send_b.astype(jnp.bfloat16), 'tp', down)]
    ppermute x0 -> x6, waiting for transfers between devices: none -> 7.13 us  [the longest x3 5.58 us: ring_reduce_scatter(): carry_a = lax.ppermute(send_a.astype(jnp.bfloat16), 'tp', up)]
    another operation x4 -> x3, local copies, waits for them, and re-layouts: 4.41 us -> 0.02 us  [the longest x1 4.39 us: shards(): down_q = w_down[0].reshape(w_down.shape[1], groups, quarter)]
    all_to_all x1, waiting for transfers between devices: 47.7 us -> 52.1 us  [shards(): lax.all_to_all(outbound.reshape(experts, capacity, width), 'ep', split_ax...]
    all_to_all x1, starting transfers between devices: 9.61 us -> 13 us  [shards(): lax.all_to_all(summed.reshape(experts, capacity, quarter), 'ep', split_ax...]
    reshape x1 -> x0, local copies, waits for them, and re-layouts: 1.98 us -> none  [shards(): summed.reshape(experts, capacity, quarter)]
    dot_general x1 -> x9, matrix products: 5.2 us -> 3.56 us  [the longest x8 2.58 us: quarter_of(): part = jnp.dot(hidden[lo:hi], cols, preferred_element_type=jnp.float32)]
  transfers between devices with their start and end apart: 2 -> 8, of which waited for: 2 -> 7; matrix products, arithmetic and copies ran while one was open for 3% -> 2% of each run, Pallas kernels for 0% -> 0%
where the time goes in v2:
time: 150 us; the launch traced here: 148 us
  waiting for transfers between devices  78.6 us (52%)
  starting transfers between devices  50.9 us (34%)
  matrix products  9.47 us (6%)
  local copies, waits for them, and re-layouts  6.87 us (5%)
    all_to_all x1, waiting for transfers between devices, shards(): lax.all_to_all(outbound.reshape(experts, capacity, width), 'ep', split_ax...  52.1 us
    all_to_all x1, waiting for transfers between devices, shards(): lax.all_to_all(summed.reshape(experts, capacity, quarter), 'ep', split_ax...  19.4 us
    all_to_all x1, starting transfers between devices, shards(): lax.all_to_all(outbound.reshape(experts, capacity, width), 'ep', split_ax...  18.4 us
    all_to_all x1, starting transfers between devices, shards(): lax.all_to_all(summed.reshape(experts, capacity, quarter), 'ep', split_ax...  13 us
    ppermute x3, starting transfers between devices, ring_reduce_scatter(): carry_b = lax.ppermute(send_b.astype(jnp.bfloat16), 'tp', down)  12.5 us
    ppermute x3, starting transfers between devices, ring_reduce_scatter(): carry_a = lax.ppermute(send_a.astype(jnp.bfloat16), 'tp', up)  6.97 us
    ppermute x3, waiting for transfers between devices, ring_reduce_scatter(): carry_a = lax.ppermute(send_a.astype(jnp.bfloat16), 'tp', up)  5.58 us
    dot_general x1, matrix products, shards(): gate = jnp.dot(arrived, w_gate[0], preferred_element_type=jnp.float32)  3.08 us
  transfers between devices with their start and end apart: 8, of which 7 were waited for; matrix products, arithmetic and copies ran while one was open for 2% of the time, Pallas kernels for 0%

profile of v2, /device:TPU:1, one launch (start us, length us, event | category | flops | bytes accessed | tf_op | source)
XLA Modules:
  0.0 147.6 jit_solution(5738580027870705645)
XLA Ops:
  0.0 0.0 copy-start
  0.0 0.9 copy.19
  0.9 0.1 eq.94
  1.0 0.1 eq.90
  1.2 0.1 copy.21
  1.3 0.2 fusion.41
  1.6 0.2 fusion.42
  1.8 0.1 sub.7
  1.9 0.1 copy.23
  2.0 0.7 multiply_add_fusion
  2.7 1.7 %convolution_convert_fusion = bf16[512,2048]{1,0:T(8,128)(2,1)S(1)} fusion(bf16[128,2048]{1,0:T(8,128)(2,1)} %param.6, s32[128]{0:T(128)S(1)} %get-tuple-element.8, s32[128]{0:T(128)S(1)} %get-tuple-element.7), kind=kOutput, calls=%fused_computation | convolution fusion | flops 269680640 | bytes 2622464 | tf_op jit(solution)/shard_map/dot_general | solution.py:42
  4.5 2.2 %reshape.41 = bf16[128,4,2048]{2,1,0:T(4,128)(2,1)} reshape(bf16[512,2048]{1,0:T(8,128)(2,1)S(1)} %convolution_convert_fusion) | data formatting | bytes 4194304 | tf_op jit(solution)/shard_map/reshape | solution.py:44
  6.7 18.4 %all-to-all-start = ((bf16[128,4,2048]{2,1,0:T(4,128)(2,1)}), bf16[128,4,2048]{2,1,0:T(4,128)(2,1)S(1)}, u32[]{:S(2)}, u32[]{:S(2)}) async-start(bf16[128,4,2048]{2,1,0:T(4,128)(2,1)} %reshape.41), calls=%async_computation | async-start | bytes 4194304 | tf_op jit(solution)/shard_map/all_to_all | solution.py:43
  25.2 52.1 %all-to-all-done = bf16[128,4,2048]{2,1,0:T(4,128)(2,1)S(1)} async-done(((bf16[128,4,2048]{2,1,0:T(4,128)(2,1)}), bf16[128,4,2048]{2,1,0:T(4,128)(2,1)S(1)}, u32[]{:S(2)}, u32[]{:S(2)}) %all-to-all-start) | async-done | bytes 2097184 | tf_op jit(solution)/shard_map/all_to_all | solution.py:43
  77.2 2.1 %reshape.42 = bf16[512,2048]{1,0:T(8,128)(2,1)} reshape(bf16[128,4,2048]{2,1,0:T(4,128)(2,1)S(1)} %all-to-all-done) | data formatting | bytes 4194304 | tf_op jit(solution)/shard_map/reshape | solution.py:46
  79.3 0.0 copy-start.1
  79.3 0.0 copy-start.3
  79.3 3.1 %fusion.2 = f32[512,352]{0,1:T(8,128)S(1)} fusion(bf16[512,2048]{1,0:T(8,128)(2,1)} %reshape.42, bf16[1,2048,352]{1,2,0:T(8,128)(2,1)} %param.9), kind=kOutput, calls=%fused_computation.3 | convolution fusion | flops 738197504 | bytes 4259840 | tf_op jit(solution)/shard_map/dot_general | solution.py:47
  82.4 0.0 copy-done.1
  82.4 0.0 copy-done.3
  82.4 1.0 fusion.7
  83.4 0.0 copy-done
  83.4 0.3 convolution_convert_fusion.5
  83.7 3.1 %collective-permute-start = (bf16[256,512]{1,0:T(8,128)(2,1)S(1)}, bf16[256,512]{1,0:T(8,128)(2,1)S(1)}, u32[]{:S(2)}, u32[]{:S(2)}) collective-permute-start(bf16[256,512]{1,0:T(8,128)(2,1)S(1)} %convolution_convert_fusion.5), channel_id=1, source_target_pairs={{0,1},{1,2},{2,3},{3,0},{4,5},{5,6},{6,7},{7,4},{8,9},{9,10},{10,1... | collective-permute-start | bytes 786440 | tf_op jit(solution)/shard_map/ppermute | solution.py:18
  86.9 0.3 fusion.14
  87.2 0.3 convolution_convert_fusion.1
  87.5 3.4 %collective-permute-start.3 = (bf16[256,512]{1,0:T(8,128)(2,1)S(1)}, bf16[256,512]{1,0:T(8,128)(2,1)S(1)}, u32[]{:S(2)}, u32[]{:S(2)}) collective-permute-start(bf16[256,512]{1,0:T(8,128)(2,1)S(1)} %convolution_convert_fusion.1), channel_id=1, source_target_pairs={{0,3},{1,0},{2,1},{3,2},{4,7},{5,4},{6,5},{7,6},{8,11},{9,8},{10,9... | collective-permute-start | bytes 786440 | tf_op jit(solution)/shard_map/ppermute | solution.py:19
  90.9 0.3 fusion.11
  91.2 2.4 %collective-permute-done = bf16[256,512]{1,0:T(8,128)(2,1)S(1)} collective-permute-done((bf16[256,512]{1,0:T(8,128)(2,1)S(1)}, bf16[256,512]{1,0:T(8,128)(2,1)S(1)}, u32[]{:S(2)}, u32[]{:S(2)}) %collective-permute-start) | collective-permute-done | bytes 262176 | tf_op jit(solution)/shard_map/ppermute | solution.py:18
  93.6 0.3 add_convert_fusion.5
  94.0 1.9 %collective-permute-start.1 = (bf16[256,512]{1,0:T(8,128)(2,1)S(1)}, bf16[256,512]{1,0:T(8,128)(2,1)S(1)}, u32[]{:S(2)}, u32[]{:S(2)}) collective-permute-start(bf16[256,512]{1,0:T(8,128)(2,1)S(1)} %add_convert_fusion.5), channel_id=1, source_target_pairs={{0,1},{1,2},{2,3},{3,0},{4,5},{5,6},{6,7},{7,4},{8,9},{9,10},{10,1... | collective-permute-start | bytes 786440 | tf_op jit(solution)/shard_map/ppermute | solution.py:18
  95.9 0.1 collective-permute-done.3
  95.9 0.3 add_convert_fusion.2
  96.3 4.6 %collective-permute-start.4 = (bf16[256,512]{1,0:T(8,128)(2,1)S(1)}, bf16[256,512]{1,0:T(8,128)(2,1)S(1)}, u32[]{:S(2)}, u32[]{:S(2)}) collective-permute-start(bf16[256,512]{1,0:T(8,128)(2,1)S(1)} %add_convert_fusion.2), channel_id=1, source_target_pairs={{0,3},{1,0},{2,1},{3,2},{4,7},{5,4},{6,5},{7,6},{8,11},{9,8},{10,9... | collective-permute-start | bytes 786440 | tf_op jit(solution)/shard_map/ppermute | solution.py:19
  100.8 0.3 fusion.15
  101.2 1.8 %collective-permute-done.1 = bf16[256,512]{1,0:T(8,128)(2,1)S(1)} collective-permute-done((bf16[256,512]{1,0:T(8,128)(2,1)S(1)}, bf16[256,512]{1,0:T(8,128)(2,1)S(1)}, u32[]{:S(2)}, u32[]{:S(2)}) %collective-permute-start.1) | collective-permute-done | bytes 262176 | tf_op jit(solution)/shard_map/ppermute | solution.py:18
  103.0 0.1 add_convert_fusion.4
  103.0 1.9 %collective-permute-start.2 = (bf16[256,512]{1,0:T(8,128)(2,1)S(1)}, bf16[256,512]{1,0:T(8,128)(2,1)S(1)}, u32[]{:S(2)}, u32[]{:S(2)}) collective-permute-start(bf16[256,512]{1,0:T(8,128)(2,1)S(1)} %add_convert_fusion.4), channel_id=1, source_target_pairs={{0,1},{1,2},{2,3},{3,0},{4,5},{5,6},{6,7},{7,4},{8,9},{9,10},{10,1... | collective-permute-start | bytes 786440 | tf_op jit(solution)/shard_map/ppermute | solution.py:18
  105.0 0.0 collective-permute-done.4
  105.0 0.1 add_convert_fusion.1
  105.1 4.6 %collective-permute-start.5 = (bf16[256,512]{1,0:T(8,128)(2,1)S(1)}, bf16[256,512]{1,0:T(8,128)(2,1)S(1)}, u32[]{:S(2)}, u32[]{:S(2)}) collective-permute-start(bf16[256,512]{1,0:T(8,128)(2,1)S(1)} %add_convert_fusion.1), channel_id=1, source_target_pairs={{0,3},{1,0},{2,1},{3,2},{4,7},{5,4},{6,5},{7,6},{8,11},{9,8},{10,9... | collective-permute-start | bytes 786440 | tf_op jit(solution)/shard_map/ppermute | solution.py:19
  109.7 0.3 fusion.12
  110.0 1.4 collective-permute-done.2
  111.4 0.1 add_convert_fusion.3
  111.4 1.5 %collective-permute-done.5 = bf16[256,512]{1,0:T(8,128)(2,1)S(1)} collective-permute-done((bf16[256,512]{1,0:T(8,128)(2,1)S(1)}, bf16[256,512]{1,0:T(8,128)(2,1)S(1)}, u32[]{:S(2)}, u32[]{:S(2)}) %collective-permute-start.5) | collective-permute-done | bytes 262176 | tf_op jit(solution)/shard_map/ppermute | solution.py:19
  112.9 0.1 add_convert_fusion
  113.0 0.0 copy-start.2
  113.1 0.9 convert_element_type.126
  114.0 13.0 %all-to-all-start.1 = ((bf16[128,4,512]{2,1,0:T(4,128)(2,1)}), bf16[128,4,512]{2,1,0:T(4,128)(2,1)S(1)}, u32[]{:S(2)}, u32[]{:S(2)}) async-start(bf16[128,4,512]{2,1,0:T(4,128)(2,1)} %convert_element_type.126), calls=%async_computation.1 | async-start | bytes 1048576 | tf_op jit(solution)/shard_map/all_to_all | solution.py:59
  127.0 0.0 copy-done.2
  127.0 19.4 %all-to-all-done.1 = bf16[128,4,512]{2,1,0:T(4,128)(2,1)S(1)} async-done(((bf16[128,4,512]{2,1,0:T(4,128)(2,1)}), bf16[128,4,512]{2,1,0:T(4,128)(2,1)S(1)}, u32[]{:S(2)}, u32[]{:S(2)}) %all-to-all-start.1) | async-done | bytes 524320 | tf_op jit(solution)/shard_map/all_to_all | solution.py:59
  146.4 0.1 reshape.43
  146.5 1.1 convolution_convert_fusion.9
  (10 shorter events, 0.1 us)
Async XLA Ops:
  0.0 83.4 %copy-start = (bf16[1,352,2048]{2,1,0:T(8,128)(2,1)S(1)}, bf16[1,352,2048]{2,1,0:T(8,128)(2,1)}, u32[]{:S(2)}) copy-start(bf16[1,352,2048]{2,1,0:T(8,128)(2,1)} %param.11) | copy-start | bytes 4325380
  6.7 70.6 %all-to-all-start = ((bf16[128,4,2048]{2,1,0:T(4,128)(2,1)}), bf16[128,4,2048]{2,1,0:T(4,128)(2,1)S(1)}, u32[]{:S(2)}, u32[]{:S(2)}) async-start(bf16[128,4,2048]{2,1,0:T(4,128)(2,1)} %reshape.41), calls=%async_computation | async-start | bytes 4194304 | tf_op jit(solution)/shard_map/all_to_all | solution.py:43
  79.3 3.1 %copy-start.1 = (bf16[512,2048]{1,0:T(8,128)(2,1)S(1)}, bf16[512,2048]{1,0:T(8,128)(2,1)}, u32[]{:S(2)}) copy-start(bf16[512,2048]{1,0:T(8,128)(2,1)} %reshape.42) | copy-start | bytes 6291460
  79.3 3.1 %copy-start.3 = (bf16[1,2048,352]{1,2,0:T(8,128)(2,1)S(1)}, bf16[1,2048,352]{1,2,0:T(8,128)(2,1)}, u32[]{:S(2)}) copy-start(bf16[1,2048,352]{1,2,0:T(8,128)(2,1)} %param.10) | copy-start | bytes 4325380
  83.7 9.9 %collective-permute-start = (bf16[256,512]{1,0:T(8,128)(2,1)S(1)}, bf16[256,512]{1,0:T(8,128)(2,1)S(1)}, u32[]{:S(2)}, u32[]{:S(2)}) collective-permute-start(bf16[256,512]{1,0:T(8,128)(2,1)S(1)} %convolution_convert_fusion.5), channel_id=1, source_target_pairs={{0,1},{1,2},{2,3},{3,0},{4,5},{5,6},{6,7},{7,4},{8,9},{9,10},{10,1... | collective-permute-start | bytes 786440 | tf_op jit(solution)/shard_map/ppermute | solution.py:18
  87.5 8.4 %collective-permute-start.3 = (bf16[256,512]{1,0:T(8,128)(2,1)S(1)}, bf16[256,512]{1,0:T(8,128)(2,1)S(1)}, u32[]{:S(2)}, u32[]{:S(2)}) collective-permute-start(bf16[256,512]{1,0:T(8,128)(2,1)S(1)} %convolution_convert_fusion.1), channel_id=1, source_target_pairs={{0,3},{1,0},{2,1},{3,2},{4,7},{5,4},{6,5},{7,6},{8,11},{9,8},{10,9... | collective-permute-start | bytes 786440 | tf_op jit(solution)/shard_map/ppermute | solution.py:19
  94.0 9.0 %collective-permute-start.1 = (bf16[256,512]{1,0:T(8,128)(2,1)S(1)}, bf16[256,512]{1,0:T(8,128)(2,1)S(1)}, u32[]{:S(2)}, u32[]{:S(2)}) collective-permute-start(bf16[256,512]{1,0:T(8,128)(2,1)S(1)} %add_convert_fusion.5), channel_id=1, source_target_pairs={{0,1},{1,2},{2,3},{3,0},{4,5},{5,6},{6,7},{7,4},{8,9},{9,10},{10,1... | collective-permute-start | bytes 786440 | tf_op jit(solution)/shard_map/ppermute | solution.py:18
  96.3 8.7 %collective-permute-start.4 = (bf16[256,512]{1,0:T(8,128)(2,1)S(1)}, bf16[256,512]{1,0:T(8,128)(2,1)S(1)}, u32[]{:S(2)}, u32[]{:S(2)}) collective-permute-start(bf16[256,512]{1,0:T(8,128)(2,1)S(1)} %add_convert_fusion.2), channel_id=1, source_target_pairs={{0,3},{1,0},{2,1},{3,2},{4,7},{5,4},{6,5},{7,6},{8,11},{9,8},{10,9... | collective-permute-start | bytes 786440 | tf_op jit(solution)/shard_map/ppermute | solution.py:19
  103.0 8.3 %collective-permute-start.2 = (bf16[256,512]{1,0:T(8,128)(2,1)S(1)}, bf16[256,512]{1,0:T(8,128)(2,1)S(1)}, u32[]{:S(2)}, u32[]{:S(2)}) collective-permute-start(bf16[256,512]{1,0:T(8,128)(2,1)S(1)} %add_convert_fusion.4), channel_id=1, source_target_pairs={{0,1},{1,2},{2,3},{3,0},{4,5},{5,6},{6,7},{7,4},{8,9},{9,10},{10,1... | collective-permute-start | bytes 786440 | tf_op jit(solution)/shard_map/ppermute | solution.py:18
  105.1 7.9 %collective-permute-start.5 = (bf16[256,512]{1,0:T(8,128)(2,1)S(1)}, bf16[256,512]{1,0:T(8,128)(2,1)S(1)}, u32[]{:S(2)}, u32[]{:S(2)}) collective-permute-start(bf16[256,512]{1,0:T(8,128)(2,1)S(1)} %add_convert_fusion.1), channel_id=1, source_target_pairs={{0,3},{1,0},{2,1},{3,2},{4,7},{5,4},{6,5},{7,6},{8,11},{9,8},{10,9... | collective-permute-start | bytes 786440 | tf_op jit(solution)/shard_map/ppermute | solution.py:19
  113.0 14.0 %copy-start.2 = (f32[128,2]{0,1:T(2,128)S(1)}, f32[128,2]{0,1:T(2,128)}, u32[]{:S(2)}) copy-start(f32[128,2]{0,1:T(2,128)} %param.8) | copy-start | bytes 3076
  114.0 32.4 %all-to-all-start.1 = ((bf16[128,4,512]{2,1,0:T(4,128)(2,1)}), bf16[128,4,512]{2,1,0:T(4,128)(2,1)S(1)}, u32[]{:S(2)}, u32[]{:S(2)}) async-start(bf16[128,4,512]{2,1,0:T(4,128)(2,1)} %convert_element_type.126), calls=%async_computation.1 | async-start | bytes 1048576 | tf_op jit(solution)/shard_map/all_to_all | solution.py:59

commit v3 on v2

--- a/solution.py
+++ b/solution.py
@@ -8,18 +8,15 @@
     half = rows // 2
     up = [(i, (i + 1) % groups) for i in range(groups)]
     down = [(i, (i - 1) % groups) for i in range(groups)]
-    carry_a = None
-    carry_b = None
-    for step in range(1, groups):
-        own_a = quarter_of(groups - step, 0, half)
-        own_b = quarter_of(step, half, rows)
-        send_a = own_a if carry_a is None else own_a + carry_a.astype(jnp.float32)
-        send_b = own_b if carry_b is None else own_b + carry_b.astype(jnp.float32)
-        carry_a = lax.ppermute(send_a.astype(jnp.bfloat16), "tp", up)
-        carry_b = lax.ppermute(send_b.astype(jnp.bfloat16), "tp", down)
-    res_a = quarter_of(0, 0, half) + carry_a.astype(jnp.float32)
-    res_b = quarter_of(0, half, rows) + carry_b.astype(jnp.float32)
-    return jnp.concatenate([res_a, res_b], axis=0)
+    far_a = lax.ppermute(quarter_of(2, 0, half).astype(jnp.bfloat16), "tp", up)
+    far_b = lax.ppermute(quarter_of(2, half, rows).astype(jnp.bfloat16), "tp", down)
+    next_up = quarter_of(1, 0, rows)
+    next_up = next_up.at[:half].add(far_a.astype(jnp.float32))
+    prev_dn = quarter_of(groups - 1, 0, rows)
+    prev_dn = prev_dn.at[half:].add(far_b.astype(jnp.float32))
+    from_lo = lax.ppermute(next_up.astype(jnp.bfloat16), "tp", up)
+    from_hi = lax.ppermute(prev_dn.astype(jnp.bfloat16), "tp", down)
+    return quarter_of(0, 0, rows) + from_lo.astype(jnp.float32) + from_hi.astype(jnp.float32)
 
 
 def shards(tokens, expert_ids, gate_values, w_gate, w_up, w_down):

time: 150 us -> 148 us (0.987); the launches traced: 148 us -> 148 us
  starting transfers between devices: 50.9 us -> 43.4 us
  waiting for transfers between devices: 78.6 us -> 85.5 us
    ppermute x6 -> x4, waiting for transfers between devices: 7.13 us -> 14 us  [the longest x1 6.24 us: ring_reduce_scatter(): from_lo = lax.ppermute(next_up.astype(jnp.bfloat16), 'tp', up)]
    ppermute x6 -> x4, starting transfers between devices: 19.5 us -> 13.5 us  [the longest x1 5.32 us: ring_reduce_scatter(): from_hi = lax.ppermute(prev_dn.astype(jnp.bfloat16), 'tp', down)]
  transfers between devices with their start and end apart: 8 -> 6, of which waited for: 7 -> 5; matrix products, arithmetic and copies ran while one was open for 2% -> 2% of each run, Pallas kernels for 0% -> 0%
where the time goes in v3:
time: 148 us
  waiting for transfers between devices  85.5 us (58%)
  starting transfers between devices  43.4 us (29%)
  matrix products  8.92 us (6%)
  local copies, waits for them, and re-layouts  6.84 us (5%)
  other arithmetic  2.53 us (2%)
    all_to_all x1, waiting for transfers between devices, shards(): lax.all_to_all(outbound.reshape(experts, capacity, width), 'ep', split_ax...  52.1 us
    all_to_all x1, waiting for transfers between devices, shards(): lax.all_to_all(summed.reshape(experts, capacity, quarter), 'ep', split_ax...  19.4 us
    all_to_all x1, starting transfers between devices, shards(): lax.all_to_all(outbound.reshape(experts, capacity, width), 'ep', split_ax...  18.4 us
    all_to_all x1, starting transfers between devices, shards(): lax.all_to_all(summed.reshape(experts, capacity, quarter), 'ep', split_ax...  11.5 us
    ppermute x1, waiting for transfers between devices, ring_reduce_scatter(): from_lo = lax.ppermute(next_up.astype(jnp.bfloat16), 'tp', up)  6.24 us
    ppermute x1, waiting for transfers between devices, ring_reduce_scatter(): from_hi = lax.ppermute(prev_dn.astype(jnp.bfloat16), 'tp', down)  5.92 us
    ppermute x1, starting transfers between devices, ring_reduce_scatter(): from_hi = lax.ppermute(prev_dn.astype(jnp.bfloat16), 'tp', down)  5.32 us
    ppermute x1, starting transfers between devices, ring_reduce_scatter(): lax.ppermute(quarter_of(2, half, rows).astype(jnp.bfloat16), 'tp', down)  4.38 us
  transfers between devices with their start and end apart: 6, of which 5 were waited for; matrix products, arithmetic and copies ran while one was open for 2% of the time, Pallas kernels for 0%

profile of v3, /device:TPU:1, one launch (start us, length us, event | category | flops | bytes accessed | tf_op | source)
XLA Modules:
  0.0 147.5 jit_solution(10484969377435659428)
XLA Ops:
  0.0 0.0 copy-start
  0.0 0.9 copy.19
  0.9 0.1 eq.91
  1.0 0.1 eq.87
  1.2 0.1 copy.21
  1.3 0.2 fusion.32
  1.6 0.2 fusion.33
  1.8 0.1 sub.7
  1.9 0.1 copy.23
  2.0 0.7 multiply_add_fusion
  2.7 1.7 %convolution_convert_fusion = bf16[512,2048]{1,0:T(8,128)(2,1)S(1)} fusion(bf16[128,2048]{1,0:T(8,128)(2,1)} %param.10, s32[128]{0:T(128)S(1)} %get-tuple-element.32, s32[128]{0:T(128)S(1)} %get-tuple-element.31), kind=kOutput, calls=%fused_computation | convolution fusion | flops 269680640 | bytes 2622464 | tf_op jit(solution)/shard_map/dot_general | solution.py:39
  4.5 2.2 %reshape.90 = bf16[128,4,2048]{2,1,0:T(4,128)(2,1)} reshape(bf16[512,2048]{1,0:T(8,128)(2,1)S(1)} %convolution_convert_fusion) | data formatting | bytes 4194304 | tf_op jit(solution)/shard_map/reshape | solution.py:41
  6.7 18.4 %all-to-all-start = ((bf16[128,4,2048]{2,1,0:T(4,128)(2,1)}), bf16[128,4,2048]{2,1,0:T(4,128)(2,1)S(1)}, u32[]{:S(2)}, u32[]{:S(2)}) async-start(bf16[128,4,2048]{2,1,0:T(4,128)(2,1)} %reshape.90), calls=%async_computation | async-start | bytes 4194304 | tf_op jit(solution)/shard_map/all_to_all | solution.py:40
  25.1 52.1 %all-to-all-done = bf16[128,4,2048]{2,1,0:T(4,128)(2,1)S(1)} async-done(((bf16[128,4,2048]{2,1,0:T(4,128)(2,1)}), bf16[128,4,2048]{2,1,0:T(4,128)(2,1)S(1)}, u32[]{:S(2)}, u32[]{:S(2)}) %all-to-all-start) | async-done | bytes 2097184 | tf_op jit(solution)/shard_map/all_to_all | solution.py:40
  77.2 2.0 %reshape.91 = bf16[512,2048]{1,0:T(8,128)(2,1)} reshape(bf16[128,4,2048]{2,1,0:T(4,128)(2,1)S(1)} %all-to-all-done) | data formatting | bytes 4194304 | tf_op jit(solution)/shard_map/reshape | solution.py:43
  79.3 0.0 copy-start.1
  79.3 0.0 copy-start.3
  79.3 3.1 %fusion.2 = f32[512,352]{0,1:T(8,128)S(1)} fusion(bf16[512,2048]{1,0:T(8,128)(2,1)} %reshape.91, bf16[1,2048,352]{1,2,0:T(8,128)(2,1)} %param.13), kind=kOutput, calls=%fused_computation.3 | convolution fusion | flops 738197504 | bytes 4259840 | tf_op jit(solution)/shard_map/dot_general | solution.py:44
  82.4 0.0 copy-done.1
  82.4 0.0 copy-done.3
  82.4 1.0 fusion.10
  83.4 0.0 copy-done
  83.4 0.5 fusion.6
  83.9 0.3 convolution_convert_fusion.4
  84.2 4.4 %collective-permute-start.2 = (bf16[256,512]{1,0:T(8,128)(2,1)S(1)}, bf16[256,512]{1,0:T(8,128)(2,1)S(1)}, u32[]{:S(2)}, u32[]{:S(2)}) collective-permute-start(bf16[256,512]{1,0:T(8,128)(2,1)S(1)} %convolution_convert_fusion.4), channel_id=1, source_target_pairs={{0,3},{1,0},{2,1},{3,2},{4,7},{5,4},{6,5},{7,6},{8,11},{9,8},{10,9... | collective-permute-start | bytes 786440 | tf_op jit(solution)/shard_map/ppermute | solution.py:12
  88.6 0.3 convolution_convert_fusion.5
  88.9 1.9 %collective-permute-start = (bf16[256,512]{1,0:T(8,128)(2,1)S(1)}, bf16[256,512]{1,0:T(8,128)(2,1)S(1)}, u32[]{:S(2)}, u32[]{:S(2)}) collective-permute-start(bf16[256,512]{1,0:T(8,128)(2,1)S(1)} %convolution_convert_fusion.5), channel_id=1, source_target_pairs={{0,1},{1,2},{2,3},{3,0},{4,5},{5,6},{6,7},{7,4},{8,9},{9,10},{10,1... | collective-permute-start | bytes 786440 | tf_op jit(solution)/shard_map/ppermute | solution.py:11
  90.8 0.5 fusion.5
  91.3 1.8 %collective-permute-done.2 = bf16[256,512]{1,0:T(8,128)(2,1)S(1)} collective-permute-done((bf16[256,512]{1,0:T(8,128)(2,1)S(1)}, bf16[256,512]{1,0:T(8,128)(2,1)S(1)}, u32[]{:S(2)}, u32[]{:S(2)}) %collective-permute-start.2) | collective-permute-done | bytes 262176 | tf_op jit(solution)/shard_map/ppermute | solution.py:12
  93.1 0.1 fusion.13
  93.3 0.1 convert_element_type.82
  93.3 5.3 %collective-permute-start.3 = (bf16[512,512]{1,0:T(8,128)(2,1)S(1)}, bf16[512,512]{1,0:T(8,128)(2,1)S(1)}, u32[]{:S(2)}, u32[]{:S(2)}) collective-permute-start(bf16[512,512]{1,0:T(8,128)(2,1)S(1)} %convert_element_type.82), channel_id=1, source_target_pairs={{0,3},{1,0},{2,1},{3,2},{4,7},{5,4},{6,5},{7,6},{8,11},{9,8},{10,9... | collective-permute-start | bytes 1572872 | tf_op jit(solution)/shard_map/ppermute | solution.py:18
  98.7 0.0 collective-permute-done
  98.7 0.1 fusion.14
  98.8 0.9 convert_element_type.76
  99.7 1.9 %collective-permute-start.1 = (bf16[512,512]{1,0:T(8,128)(2,1)}, bf16[512,512]{1,0:T(8,128)(2,1)S(1)}, u32[]{:S(2)}, u32[]{:S(2)}) collective-permute-start(bf16[512,512]{1,0:T(8,128)(2,1)} %convert_element_type.76), channel_id=1, source_target_pairs={{0,1},{1,2},{2,3},{3,0},{4,5},{5,6},{6,7},{7,4},{8,9},{9,10},{10,1... | collective-permute-start | bytes 1572872 | tf_op jit(solution)/shard_map/ppermute | solution.py:17
  101.6 0.5 fusion.4
  102.1 5.9 %collective-permute-done.3 = bf16[512,512]{1,0:T(8,128)(2,1)S(1)} collective-permute-done((bf16[512,512]{1,0:T(8,128)(2,1)S(1)}, bf16[512,512]{1,0:T(8,128)(2,1)S(1)}, u32[]{:S(2)}, u32[]{:S(2)}) %collective-permute-start.3) | collective-permute-done | bytes 524320 | tf_op jit(solution)/shard_map/ppermute | solution.py:18
  108.0 6.2 %collective-permute-done.1 = bf16[512,512]{1,0:T(8,128)(2,1)S(1)} collective-permute-done((bf16[512,512]{1,0:T(8,128)(2,1)}, bf16[512,512]{1,0:T(8,128)(2,1)S(1)}, u32[]{:S(2)}, u32[]{:S(2)}) %collective-permute-start.1) | collective-permute-done | bytes 524320 | tf_op jit(solution)/shard_map/ppermute | solution.py:17
  114.2 0.2 add_convert_fusion
  114.4 0.0 copy-start.2
  114.5 0.9 reshape.92
  115.4 11.5 %all-to-all-start.1 = ((bf16[128,4,512]{2,1,0:T(4,128)(2,1)}), bf16[128,4,512]{2,1,0:T(4,128)(2,1)S(1)}, u32[]{:S(2)}, u32[]{:S(2)}) async-start(bf16[128,4,512]{2,1,0:T(4,128)(2,1)} %reshape.92), calls=%async_computation.1 | async-start | bytes 1048576 | tf_op jit(solution)/shard_map/all_to_all | solution.py:56
  126.9 0.0 copy-done.2
  126.9 19.4 %all-to-all-done.1 = bf16[128,4,512]{2,1,0:T(4,128)(2,1)S(1)} async-done(((bf16[128,4,512]{2,1,0:T(4,128)(2,1)}), bf16[128,4,512]{2,1,0:T(4,128)(2,1)S(1)}, u32[]{:S(2)}, u32[]{:S(2)}) %all-to-all-start.1) | async-done | bytes 524320 | tf_op jit(solution)/shard_map/all_to_all | solution.py:56
  146.3 0.1 reshape.93
  146.4 1.1 convolution_convert_fusion.6
  (9 shorter events, 0.1 us)
Async XLA Ops:
  0.0 83.4 %copy-start = (bf16[1,352,2048]{2,1,0:T(8,128)(2,1)S(1)}, bf16[1,352,2048]{2,1,0:T(8,128)(2,1)}, u32[]{:S(2)}) copy-start(bf16[1,352,2048]{2,1,0:T(8,128)(2,1)} %param.15) | copy-start | bytes 4325380
  6.7 70.6 %all-to-all-start = ((bf16[128,4,2048]{2,1,0:T(4,128)(2,1)}), bf16[128,4,2048]{2,1,0:T(4,128)(2,1)S(1)}, u32[]{:S(2)}, u32[]{:S(2)}) async-start(bf16[128,4,2048]{2,1,0:T(4,128)(2,1)} %reshape.90), calls=%async_computation | async-start | bytes 4194304 | tf_op jit(solution)/shard_map/all_to_all | solution.py:40
  79.3 3.1 %copy-start.1 = (bf16[512,2048]{1,0:T(8,128)(2,1)S(1)}, bf16[512,2048]{1,0:T(8,128)(2,1)}, u32[]{:S(2)}) copy-start(bf16[512,2048]{1,0:T(8,128)(2,1)} %reshape.91) | copy-start | bytes 6291460
  79.3 3.1 %copy-start.3 = (bf16[1,2048,352]{1,2,0:T(8,128)(2,1)S(1)}, bf16[1,2048,352]{1,2,0:T(8,128)(2,1)}, u32[]{:S(2)}) copy-start(bf16[1,2048,352]{1,2,0:T(8,128)(2,1)} %param.14) | copy-start | bytes 4325380
  84.2 8.9 %collective-permute-start.2 = (bf16[256,512]{1,0:T(8,128)(2,1)S(1)}, bf16[256,512]{1,0:T(8,128)(2,1)S(1)}, u32[]{:S(2)}, u32[]{:S(2)}) collective-permute-start(bf16[256,512]{1,0:T(8,128)(2,1)S(1)} %convolution_convert_fusion.4), channel_id=1, source_target_pairs={{0,3},{1,0},{2,1},{3,2},{4,7},{5,4},{6,5},{7,6},{8,11},{9,8},{10,9... | collective-permute-start | bytes 786440 | tf_op jit(solution)/shard_map/ppermute | solution.py:12
  88.9 9.8 %collective-permute-start = (bf16[256,512]{1,0:T(8,128)(2,1)S(1)}, bf16[256,512]{1,0:T(8,128)(2,1)S(1)}, u32[]{:S(2)}, u32[]{:S(2)}) collective-permute-start(bf16[256,512]{1,0:T(8,128)(2,1)S(1)} %convolution_convert_fusion.5), channel_id=1, source_target_pairs={{0,1},{1,2},{2,3},{3,0},{4,5},{5,6},{6,7},{7,4},{8,9},{9,10},{10,1... | collective-permute-start | bytes 786440 | tf_op jit(solution)/shard_map/ppermute | solution.py:11
  93.3 14.6 %collective-permute-start.3 = (bf16[512,512]{1,0:T(8,128)(2,1)S(1)}, bf16[512,512]{1,0:T(8,128)(2,1)S(1)}, u32[]{:S(2)}, u32[]{:S(2)}) collective-permute-start(bf16[512,512]{1,0:T(8,128)(2,1)S(1)} %convert_element_type.82), channel_id=1, source_target_pairs={{0,3},{1,0},{2,1},{3,2},{4,7},{5,4},{6,5},{7,6},{8,11},{9,8},{10,9... | collective-permute-start | bytes 1572872 | tf_op jit(solution)/shard_map/ppermute | solution.py:18
  99.7 14.6 %collective-permute-start.1 = (bf16[512,512]{1,0:T(8,128)(2,1)}, bf16[512,512]{1,0:T(8,128)(2,1)S(1)}, u32[]{:S(2)}, u32[]{:S(2)}) collective-permute-start(bf16[512,512]{1,0:T(8,128)(2,1)} %convert_element_type.76), channel_id=1, source_target_pairs={{0,1},{1,2},{2,3},{3,0},{4,5},{5,6},{6,7},{7,4},{8,9},{9,10},{10,1... | collective-permute-start | bytes 1572872 | tf_op jit(solution)/shard_map/ppermute | solution.py:17
  114.4 12.4 %copy-start.2 = (f32[128,2]{0,1:T(2,128)S(1)}, f32[128,2]{0,1:T(2,128)}, u32[]{:S(2)}) copy-start(f32[128,2]{0,1:T(2,128)} %param.12) | copy-start | bytes 3076
  115.4 30.9 %all-to-all-start.1 = ((bf16[128,4,512]{2,1,0:T(4,128)(2,1)}), bf16[128,4,512]{2,1,0:T(4,128)(2,1)S(1)}, u32[]{:S(2)}, u32[]{:S(2)}) async-start(bf16[128,4,512]{2,1,0:T(4,128)(2,1)} %reshape.92), calls=%async_computation.1 | async-start | bytes 1048576 | tf_op jit(solution)/shard_map/all_to_all | solution.py:56

commit v4 on v3

--- a/solution.py
+++ b/solution.py
@@ -19,6 +19,18 @@
     return quarter_of(0, 0, rows) + from_lo.astype(jnp.float32) + from_hi.astype(jnp.float32)
 
 
+def ring_all_gather(block, groups, rows):
+    half = rows // 2
+    up = [(i, (i + 1) % groups) for i in range(groups)]
+    down = [(i, (i - 1) % groups) for i in range(groups)]
+    from_lo = lax.ppermute(block, "tp", up)
+    from_hi = lax.ppermute(block, "tp", down)
+    far_a = lax.ppermute(from_lo[:half], "tp", up)
+    far_b = lax.ppermute(from_hi[half:], "tp", down)
+    far = jnp.concatenate([far_a, far_b], axis=0)
+    return [(0, block), (groups - 1, from_lo), (1, from_hi), (2, far)]
+
+
 def shards(tokens, expert_ids, gate_values, w_gate, w_up, w_down):
     tok_rows = tokens.shape[0]
     width = tokens.shape[1]
@@ -36,16 +48,27 @@
     first_hit = target[:, 0][None, :] == slot_iota[:, None]
     second_hit = target[:, 1][None, :] == slot_iota[:, None]
     placer = (first_hit | second_hit).astype(jnp.bfloat16)
-    outbound = jnp.dot(placer, tokens, preferred_element_type=jnp.float32).astype(jnp.bfloat16)
+    own = lax.axis_index("tp")
+    own_cols = lax.dynamic_slice_in_dim(tokens, own * quarter, quarter, axis=1)
+    outbound = jnp.dot(placer, own_cols, preferred_element_type=jnp.float32).astype(jnp.bfloat16)
     arrived = lax.all_to_all(
-        outbound.reshape(experts, capacity, width), "ep", split_axis=0, concat_axis=0, tiled=True
+        outbound.reshape(experts, capacity, quarter), "ep", split_axis=0, concat_axis=0, tiled=True
     )
-    arrived = arrived.reshape(row_count, width)
-    gate = jnp.dot(arrived, w_gate[0], preferred_element_type=jnp.float32)
-    up = jnp.dot(arrived, w_up[0], preferred_element_type=jnp.float32)
+    arrived = arrived.reshape(row_count, quarter)
+    pieces = ring_all_gather(arrived, groups, row_count)
+
+    def project(weight):
+        acc = None
+        for k, piece in pieces:
+            rows = lax.dynamic_slice_in_dim(weight, ((own + k) % groups) * quarter, quarter, axis=0)
+            term = jnp.dot(piece, rows, preferred_element_type=jnp.float32)
+            acc = term if acc is None else acc + term
+        return acc
+
+    gate = project(w_gate[0])
+    up = project(w_up[0])
     hidden = (jax.nn.silu(gate) * up).astype(jnp.bfloat16)
     down = w_down[0]
-    own = lax.axis_index("tp")
 
     def quarter_of(k, lo, hi):
         cols = lax.dynamic_slice_in_dim(down, ((own + k) % groups) * quarter, quarter, axis=1)

time: 148 us -> 131 us (0.89); the launches traced: 148 us -> 129 us
  waiting for transfers between devices: 85.5 us -> 34.6 us
  blocking collectives: 0 us -> 37.6 us
  local copies, waits for them, and re-layouts: 6.84 us -> 2.9 us
    all_to_all x1 -> x0, waiting for transfers between devices: 52.1 us -> none  [shards(): lax.all_to_all(outbound.reshape(experts, capacity, width), 'ep', split_ax...]
    all_to_all x0 -> x1, blocking collectives: none -> 37.6 us  [shards(): lax.all_to_all(outbound.reshape(experts, capacity, quarter), 'ep', split_...]
    all_to_all x1 -> x0, starting transfers between devices: 18.4 us -> none  [shards(): lax.all_to_all(outbound.reshape(experts, capacity, width), 'ep', split_ax...]
    ppermute x0 -> x4, starting transfers between devices: none -> 13 us  [the longest x1 4.57 us: ring_all_gather(): far_b = lax.ppermute(from_hi[half:], 'tp', down)]
    ppermute x0 -> x4, waiting for transfers between devices: none -> 8.5 us  [the longest x1 6.03 us: ring_all_gather(): from_lo = lax.ppermute(block, 'tp', up)]
    all_to_all x1, starting transfers between devices: 11.5 us -> 16.5 us  [shards(): lax.all_to_all(summed.reshape(experts, capacity, quarter), 'ep', split_ax...]
    ppermute x1, waiting for transfers between devices: 5.92 us -> 1.8 us  [ring_reduce_scatter(): from_hi = lax.ppermute(prev_dn.astype(jnp.bfloat16), 'tp', down)]
    reshape x2, local copies, waits for them, and re-layouts: 4.27 us -> 0.25 us  [the longest x1 0.12 us: shards(): outbound.reshape(experts, capacity, quarter)]
  transfers between devices with their start and end apart: 6 -> 9, of which waited for: 5 -> 7; matrix products, arithmetic and copies ran while one was open for 2% -> 3% of each run, Pallas kernels for 0% -> 0%
where the time goes in v4:
time: 131 us; the launch traced here: 129 us
  starting transfers between devices  43 us (33%)
  blocking collectives  37.6 us (29%)
  waiting for transfers between devices  34.6 us (26%)
  matrix products  8.57 us (7%)
  local copies, waits for them, and re-layouts  2.9 us (2%)
  other arithmetic  1.74 us (1%)
    all_to_all x1, blocking collectives, shards(): lax.all_to_all(outbound.reshape(experts, capacity, quarter), 'ep', split_...  37.6 us
    all_to_all x1, waiting for transfers between devices, shards(): lax.all_to_all(summed.reshape(experts, capacity, quarter), 'ep', split_ax...  19.4 us
    all_to_all x1, starting transfers between devices, shards(): lax.all_to_all(summed.reshape(experts, capacity, quarter), 'ep', split_ax...  16.5 us
    ppermute x1, waiting for transfers between devices, ring_all_gather(): from_lo = lax.ppermute(block, 'tp', up)  6.03 us
    ppermute x1, starting transfers between devices, ring_reduce_scatter(): from_hi = lax.ppermute(prev_dn.astype(jnp.bfloat16), 'tp', down)  4.68 us
    ppermute x1, starting transfers between devices, ring_all_gather(): far_b = lax.ppermute(from_hi[half:], 'tp', down)  4.57 us
    ppermute x1, starting transfers between devices, ring_reduce_scatter(): lax.ppermute(quarter_of(2, half, rows).astype(jnp.bfloat16), 'tp', down)  4.29 us
    dot_general x8, matrix products, project(): term = jnp.dot(piece, rows, preferred_element_type=jnp.float32)  4.25 us
  transfers between devices with their start and end apart: 9, of which 7 were waited for; matrix products, arithmetic and copies ran while one was open for 3% of the time, Pallas kernels for 0%

profile of v4, /device:TPU:1, one launch (start us, length us, event | category | flops | bytes accessed | tf_op | source)
XLA Modules:
  0.0 128.9 jit_solution(8201428754375572633)
XLA Ops:
  0.0 0.0 copy-start
  0.0 0.9 copy.19
  0.9 0.1 eq.99
  1.0 0.1 eq.95
  1.2 0.1 copy.21
  1.3 0.2 fusion.46
  1.6 0.2 fusion.47
  1.8 0.1 sub.7
  1.9 0.1 copy.23
  2.0 0.7 multiply_add_fusion
  2.7 1.2 convolution_convert_fusion.3
  3.9 0.1 reshape.98
  4.0 37.6 %all_to_all.10 = bf16[128,4,512]{2,1,0:T(4,128)(2,1)S(1)} all-to-all(bf16[128,4,512]{2,1,0:T(4,128)(2,1)S(1)} %reshape.98), channel_id=1, replica_groups=mesh['ep'=128,'tp'=4] {'ep'}, dimensions={0} | all-to-all | bytes 1048576 | tf_op jit(solution)/shard_map/all_to_all | solution.py:54
  41.7 0.1 reshape.99
  41.8 3.1 %collective-permute-start = (bf16[512,512]{1,0:T(8,128)(2,1)S(1)}, bf16[512,512]{1,0:T(8,128)(2,1)S(1)}, u32[]{:S(2)}, u32[]{:S(2)}) collective-permute-start(bf16[512,512]{1,0:T(8,128)(2,1)S(1)} %reshape.99), channel_id=1, source_target_pairs={{0,1},{1,2},{2,3},{3,0},{4,5},{5,6},{6,7},{7,4},{8,9},{9,10},{10,1... | collective-permute-start | bytes 1572872 | tf_op jit(solution)/shard_map/ppermute | solution.py:26
  44.9 3.4 %collective-permute-start.1 = (bf16[512,512]{1,0:T(8,128)(2,1)S(1)}, bf16[512,512]{1,0:T(8,128)(2,1)S(1)}, u32[]{:S(2)}, u32[]{:S(2)}) collective-permute-start(bf16[512,512]{1,0:T(8,128)(2,1)S(1)} %reshape.99), channel_id=1, source_target_pairs={{0,3},{1,0},{2,1},{3,2},{4,7},{5,4},{6,5},{7,6},{8,11},{9,8},{10,9... | collective-permute-start | bytes 1572872 | tf_op jit(solution)/shard_map/ppermute | solution.py:27
  48.4 0.0 copy-start.2
  48.4 1.5 %fusion.24 = f32[512,352]{0,1:T(8,128)S(1)} fusion(bf16[512,512]{1,0:T(8,128)(2,1)S(1)} %reshape.99, bf16[1,2048,352]{1,2,0:T(8,128)(2,1)} %param.13, s32[]{:T(128)S(6)} %select_n.63), kind=kOutput, calls=%fused_computation.37 | convolution fusion | flops 184549376 | bytes 1605636 | tf_op jit(solution)/shard_map/dot_general | solution.py:64
  49.9 0.0 copy-done.2
  49.9 0.0 copy-start.1
  49.9 0.4 fusion.18
  50.3 6.0 %collective-permute-done = bf16[512,512]{1,0:T(8,128)(2,1)S(1)} collective-permute-done((bf16[512,512]{1,0:T(8,128)(2,1)S(1)}, bf16[512,512]{1,0:T(8,128)(2,1)S(1)}, u32[]{:S(2)}, u32[]{:S(2)}) %collective-permute-start) | collective-permute-done | bytes 524320 | tf_op jit(solution)/shard_map/ppermute | solution.py:26
  56.3 1.9 %collective-permute-start.2 = (bf16[256,512]{1,0:T(8,128)(2,1)S(1)}, bf16[256,512]{1,0:T(8,128)(2,1)S(1)}, u32[]{:S(2)}, u32[]{:S(2)}) collective-permute-start(bf16[256,512]{1,0:T(8,128)(2,1)S(1)} %slice.83), channel_id=1, source_target_pairs={{0,1},{1,2},{2,3},{3,0},{4,5},{5,6},{6,7},{7,4},{8,9},{9,10},{10,1... | collective-permute-start | bytes 786440 | tf_op jit(solution)/shard_map/ppermute | solution.py:28
  58.3 0.0 collective-permute-done.1
  58.3 4.6 %collective-permute-start.3 = (bf16[256,512]{1,0:T(8,128)(2,1)S(1)}, bf16[256,512]{1,0:T(8,128)(2,1)S(1)}, u32[]{:S(2)}, u32[]{:S(2)}) collective-permute-start(bf16[256,512]{1,0:T(8,128)(2,1)S(1)} %slice.84), channel_id=1, source_target_pairs={{0,3},{1,0},{2,1},{3,2},{4,7},{5,4},{6,5},{7,6},{8,11},{9,8},{10,9... | collective-permute-start | bytes 786440 | tf_op jit(solution)/shard_map/ppermute | solution.py:29
  62.9 0.0 copy-done.1
  62.9 0.4 convolution_add_fusion.3
  63.3 0.4 convolution_add_fusion.1
  63.7 1.0 collective-permute-done.2
  64.7 1.5 %collective-permute-done.3 = bf16[256,512]{1,0:T(8,128)(2,1)S(1)} collective-permute-done((bf16[256,512]{1,0:T(8,128)(2,1)S(1)}, bf16[256,512]{1,0:T(8,128)(2,1)S(1)}, u32[]{:S(2)}, u32[]{:S(2)}) %collective-permute-start.3) | collective-permute-done | bytes 262176 | tf_op jit(solution)/shard_map/ppermute | solution.py:29
  66.2 0.4 fusion.20
  66.6 0.4 fusion.12
  67.0 0.4 fusion.3
  67.4 0.5 multiply_convert_fusion
  67.8 0.0 copy-done
  67.9 0.5 fusion.1
  68.3 0.3 convolution_convert_fusion.5
  68.7 2.6 %collective-permute-start.4 = (bf16[256,512]{1,0:T(8,128)(2,1)S(1)}, bf16[256,512]{1,0:T(8,128)(2,1)S(1)}, u32[]{:S(2)}, u32[]{:S(2)}) collective-permute-start(bf16[256,512]{1,0:T(8,128)(2,1)S(1)} %convolution_convert_fusion.5), channel_id=1, source_target_pairs={{0,1},{1,2},{2,3},{3,0},{4,5},{5,6},{6,7},{7,4},{8,9},{9,10},{10,1... | collective-permute-start | bytes 786440 | tf_op jit(solution)/shard_map/ppermute | solution.py:11
  71.3 0.3 convolution_convert_fusion.4
  71.6 4.3 %collective-permute-start.6 = (bf16[256,512]{1,0:T(8,128)(2,1)S(1)}, bf16[256,512]{1,0:T(8,128)(2,1)S(1)}, u32[]{:S(2)}, u32[]{:S(2)}) collective-permute-start(bf16[256,512]{1,0:T(8,128)(2,1)S(1)} %convolution_convert_fusion.4), channel_id=1, source_target_pairs={{0,3},{1,0},{2,1},{3,2},{4,7},{5,4},{6,5},{7,6},{8,11},{9,8},{10,9... | collective-permute-start | bytes 786440 | tf_op jit(solution)/shard_map/ppermute | solution.py:12
  75.9 0.5 fusion.2
  76.4 1.0 collective-permute-done.4
  77.4 0.1 fusion.6
  77.6 0.1 convert_element_type.76
  77.6 1.9 %collective-permute-start.5 = (bf16[512,512]{1,0:T(8,128)(2,1)S(1)}, bf16[512,512]{1,0:T(8,128)(2,1)S(1)}, u32[]{:S(2)}, u32[]{:S(2)}) collective-permute-start(bf16[512,512]{1,0:T(8,128)(2,1)S(1)} %convert_element_type.76), channel_id=1, source_target_pairs={{0,1},{1,2},{2,3},{3,0},{4,5},{5,6},{6,7},{7,4},{8,9},{9,10},{10,1... | collective-permute-start | bytes 1572872 | tf_op jit(solution)/shard_map/ppermute | solution.py:17
  79.6 0.0 collective-permute-done.6
  79.6 0.1 fusion.5
  79.7 0.1 convert_element_type.82
  79.8 4.7 %collective-permute-start.7 = (bf16[512,512]{1,0:T(8,128)(2,1)S(1)}, bf16[512,512]{1,0:T(8,128)(2,1)S(1)}, u32[]{:S(2)}, u32[]{:S(2)}) collective-permute-start(bf16[512,512]{1,0:T(8,128)(2,1)S(1)} %convert_element_type.82), channel_id=1, source_target_pairs={{0,3},{1,0},{2,1},{3,2},{4,7},{5,4},{6,5},{7,6},{8,11},{9,8},{10,9... | collective-permute-start | bytes 1572872 | tf_op jit(solution)/shard_map/ppermute | solution.py:18
  84.5 0.5 fusion
  84.9 3.8 %collective-permute-done.5 = bf16[512,512]{1,0:T(8,128)(2,1)S(1)} collective-permute-done((bf16[512,512]{1,0:T(8,128)(2,1)S(1)}, bf16[512,512]{1,0:T(8,128)(2,1)S(1)}, u32[]{:S(2)}, u32[]{:S(2)}) %collective-permute-start.5) | collective-permute-done | bytes 524320 | tf_op jit(solution)/shard_map/ppermute | solution.py:17
  88.8 1.8 %collective-permute-done.7 = bf16[512,512]{1,0:T(8,128)(2,1)S(1)} collective-permute-done((bf16[512,512]{1,0:T(8,128)(2,1)S(1)}, bf16[512,512]{1,0:T(8,128)(2,1)S(1)}, u32[]{:S(2)}, u32[]{:S(2)}) %collective-permute-start.7) | collective-permute-done | bytes 524320 | tf_op jit(solution)/shard_map/ppermute | solution.py:18
  90.6 0.2 add_convert_fusion
  90.8 0.0 copy-start.3
  90.8 0.9 reshape.100
  91.7 16.5 %all-to-all-start.1 = ((bf16[128,4,512]{2,1,0:T(4,128)(2,1)}), bf16[128,4,512]{2,1,0:T(4,128)(2,1)S(1)}, u32[]{:S(2)}, u32[]{:S(2)}) async-start(bf16[128,4,512]{2,1,0:T(4,128)(2,1)} %reshape.100), calls=%async_computation.1 | async-start | bytes 1048576 | tf_op jit(solution)/shard_map/all_to_all | solution.py:79
  108.2 0.0 copy-done.3
  108.3 19.4 %all-to-all-done.1 = bf16[128,4,512]{2,1,0:T(4,128)(2,1)S(1)} async-done(((bf16[128,4,512]{2,1,0:T(4,128)(2,1)}), bf16[128,4,512]{2,1,0:T(4,128)(2,1)S(1)}, u32[]{:S(2)}, u32[]{:S(2)}) %all-to-all-start.1) | async-done | bytes 524320 | tf_op jit(solution)/shard_map/all_to_all | solution.py:79
  127.7 0.1 reshape.101
  127.8 1.1 convolution_convert_fusion.6
  (13 shorter events, 0.2 us)
Async XLA Ops:
  0.0 67.9 %copy-start = (bf16[1,352,2048]{2,1,0:T(8,128)(2,1)S(1)}, bf16[1,352,2048]{2,1,0:T(8,128)(2,1)}, u32[]{:S(2)}) copy-start(bf16[1,352,2048]{2,1,0:T(8,128)(2,1)} %param.15) | copy-start | bytes 4325380
  41.8 14.5 %collective-permute-start = (bf16[512,512]{1,0:T(8,128)(2,1)S(1)}, bf16[512,512]{1,0:T(8,128)(2,1)S(1)}, u32[]{:S(2)}, u32[]{:S(2)}) collective-permute-start(bf16[512,512]{1,0:T(8,128)(2,1)S(1)} %reshape.99), channel_id=1, source_target_pairs={{0,1},{1,2},{2,3},{3,0},{4,5},{5,6},{6,7},{7,4},{8,9},{9,10},{10,1... | collective-permute-start | bytes 1572872 | tf_op jit(solution)/shard_map/ppermute | solution.py:26
  44.9 13.3 %collective-permute-start.1 = (bf16[512,512]{1,0:T(8,128)(2,1)S(1)}, bf16[512,512]{1,0:T(8,128)(2,1)S(1)}, u32[]{:S(2)}, u32[]{:S(2)}) collective-permute-start(bf16[512,512]{1,0:T(8,128)(2,1)S(1)} %reshape.99), channel_id=1, source_target_pairs={{0,3},{1,0},{2,1},{3,2},{4,7},{5,4},{6,5},{7,6},{8,11},{9,8},{10,9... | collective-permute-start | bytes 1572872 | tf_op jit(solution)/shard_map/ppermute | solution.py:27
  48.4 1.5 %copy-start.2 = (bf16[1,2048,352]{1,2,0:T(8,128)(2,1)S(1)}, bf16[1,2048,352]{1,2,0:T(8,128)(2,1)}, u32[]{:S(2)}) copy-start(bf16[1,2048,352]{1,2,0:T(8,128)(2,1)} %param.14) | copy-start | bytes 4325380
  49.9 13.0 %copy-start.1 = (bf16[1,2048,352]{1,2,0:T(8,128)(2,1)S(1)}, bf16[1,2048,352]{1,2,0:T(8,128)(2,1)}, u32[]{:S(2)}) copy-start(bf16[1,2048,352]{1,2,0:T(8,128)(2,1)} %param.13) | copy-start | bytes 4325380
  56.3 8.3 %collective-permute-start.2 = (bf16[256,512]{1,0:T(8,128)(2,1)S(1)}, bf16[256,512]{1,0:T(8,128)(2,1)S(1)}, u32[]{:S(2)}, u32[]{:S(2)}) collective-permute-start(bf16[256,512]{1,0:T(8,128)(2,1)S(1)} %slice.83), channel_id=1, source_target_pairs={{0,1},{1,2},{2,3},{3,0},{4,5},{5,6},{6,7},{7,4},{8,9},{9,10},{10,1... | collective-permute-start | bytes 786440 | tf_op jit(solution)/shard_map/ppermute | solution.py:28
  58.3 7.9 %collective-permute-start.3 = (bf16[256,512]{1,0:T(8,128)(2,1)S(1)}, bf16[256,512]{1,0:T(8,128)(2,1)S(1)}, u32[]{:S(2)}, u32[]{:S(2)}) collective-permute-start(bf16[256,512]{1,0:T(8,128)(2,1)S(1)} %slice.84), channel_id=1, source_target_pairs={{0,3},{1,0},{2,1},{3,2},{4,7},{5,4},{6,5},{7,6},{8,11},{9,8},{10,9... | collective-permute-start | bytes 786440 | tf_op jit(solution)/shard_map/ppermute | solution.py:29
  68.7 8.8 %collective-permute-start.4 = (bf16[256,512]{1,0:T(8,128)(2,1)S(1)}, bf16[256,512]{1,0:T(8,128)(2,1)S(1)}, u32[]{:S(2)}, u32[]{:S(2)}) collective-permute-start(bf16[256,512]{1,0:T(8,128)(2,1)S(1)} %convolution_convert_fusion.5), channel_id=1, source_target_pairs={{0,1},{1,2},{2,3},{3,0},{4,5},{5,6},{6,7},{7,4},{8,9},{9,10},{10,1... | collective-permute-start | bytes 786440 | tf_op jit(solution)/shard_map/ppermute | solution.py:11
  71.6 7.9 %collective-permute-start.6 = (bf16[256,512]{1,0:T(8,128)(2,1)S(1)}, bf16[256,512]{1,0:T(8,128)(2,1)S(1)}, u32[]{:S(2)}, u32[]{:S(2)}) collective-permute-start(bf16[256,512]{1,0:T(8,128)(2,1)S(1)} %convolution_convert_fusion.4), channel_id=1, source_target_pairs={{0,3},{1,0},{2,1},{3,2},{4,7},{5,4},{6,5},{7,6},{8,11},{9,8},{10,9... | collective-permute-start | bytes 786440 | tf_op jit(solution)/shard_map/ppermute | solution.py:12
  77.6 11.1 %collective-permute-start.5 = (bf16[512,512]{1,0:T(8,128)(2,1)S(1)}, bf16[512,512]{1,0:T(8,128)(2,1)S(1)}, u32[]{:S(2)}, u32[]{:S(2)}) collective-permute-start(bf16[512,512]{1,0:T(8,128)(2,1)S(1)} %convert_element_type.76), channel_id=1, source_target_pairs={{0,1},{1,2},{2,3},{3,0},{4,5},{5,6},{6,7},{7,4},{8,9},{9,10},{10,1... | collective-permute-start | bytes 1572872 | tf_op jit(solution)/shard_map/ppermute | solution.py:17
  79.8 10.8 %collective-permute-start.7 = (bf16[512,512]{1,0:T(8,128)(2,1)S(1)}, bf16[512,512]{1,0:T(8,128)(2,1)S(1)}, u32[]{:S(2)}, u32[]{:S(2)}) collective-permute-start(bf16[512,512]{1,0:T(8,128)(2,1)S(1)} %convert_element_type.82), channel_id=1, source_target_pairs={{0,3},{1,0},{2,1},{3,2},{4,7},{5,4},{6,5},{7,6},{8,11},{9,8},{10,9... | collective-permute-start | bytes 1572872 | tf_op jit(solution)/shard_map/ppermute | solution.py:18
  90.8 17.4 %copy-start.3 = (f32[128,2]{0,1:T(2,128)S(1)}, f32[128,2]{0,1:T(2,128)}, u32[]{:S(2)}) copy-start(f32[128,2]{0,1:T(2,128)} %param.12) | copy-start | bytes 3076
  91.7 35.9 %all-to-all-start.1 = ((bf16[128,4,512]{2,1,0:T(4,128)(2,1)}), bf16[128,4,512]{2,1,0:T(4,128)(2,1)S(1)}, u32[]{:S(2)}, u32[]{:S(2)}) async-start(bf16[128,4,512]{2,1,0:T(4,128)(2,1)} %reshape.100), calls=%async_computation.1 | async-start | bytes 1048576 | tf_op jit(solution)/shard_map/all_to_all | solution.py:79

commit v5 on v4

--- a/solution.py
+++ b/solution.py
@@ -4,29 +4,27 @@
 from jax.sharding import PartitionSpec as P
 
 
+def shifted(value, groups, shift):
+    return lax.ppermute(value, "tp", [(i, (i + shift) % groups) for i in range(groups)])
+
+
 def ring_reduce_scatter(quarter_of, groups, rows):
     half = rows // 2
-    up = [(i, (i + 1) % groups) for i in range(groups)]
-    down = [(i, (i - 1) % groups) for i in range(groups)]
-    far_a = lax.ppermute(quarter_of(2, 0, half).astype(jnp.bfloat16), "tp", up)
-    far_b = lax.ppermute(quarter_of(2, half, rows).astype(jnp.bfloat16), "tp", down)
-    next_up = quarter_of(1, 0, rows)
-    next_up = next_up.at[:half].add(far_a.astype(jnp.float32))
-    prev_dn = quarter_of(groups - 1, 0, rows)
-    prev_dn = prev_dn.at[half:].add(far_b.astype(jnp.float32))
-    from_lo = lax.ppermute(next_up.astype(jnp.bfloat16), "tp", up)
-    from_hi = lax.ppermute(prev_dn.astype(jnp.bfloat16), "tp", down)
-    return quarter_of(0, 0, rows) + from_lo.astype(jnp.float32) + from_hi.astype(jnp.float32)
+    send = lambda k, lo, hi: quarter_of(k, lo, hi).astype(jnp.bfloat16)
+    from_lo = shifted(send(1, 0, rows), groups, 1)
+    from_hi = shifted(send(groups - 1, 0, rows), groups, -1)
+    far_a = shifted(send(2, 0, half), groups, 2)
+    far_b = shifted(send(2, half, rows), groups, -2)
+    far = jnp.concatenate([far_a, far_b], axis=0).astype(jnp.float32)
+    return quarter_of(0, 0, rows) + from_lo.astype(jnp.float32) + from_hi.astype(jnp.float32) + far
 
 
 def ring_all_gather(block, groups, rows):
     half = rows // 2
-    up = [(i, (i + 1) % groups) for i in range(groups)]
-    down = [(i, (i - 1) % groups) for i in range(groups)]
-    from_lo = lax.ppermute(block, "tp", up)
-    from_hi = lax.ppermute(block, "tp", down)
-    far_a = lax.ppermute(from_lo[:half], "tp", up)
-    far_b = lax.ppermute(from_hi[half:], "tp", down)
+    from_lo = shifted(block, groups, 1)
+    from_hi = shifted(block, groups, -1)
+    far_a = shifted(block[:half], groups, 2)
+    far_b = shifted(block[half:], groups, -2)
     far = jnp.concatenate([far_a, far_b], axis=0)
     return [(0, block), (groups - 1, from_lo), (1, from_hi), (2, far)]
 

time: 131 us -> 138 us (1.053)
  the two profiles are of different devices: /device:TPU:1 before, /device:TPU:2 now
where the time goes in v5:
time: 138 us; the launch traced here: 137 us
  waiting for transfers between devices  68.2 us (49%)
  starting transfers between devices  52.9 us (38%)
  matrix products  10.6 us (8%)
  local copies, waits for them, and re-layouts  3.98 us (3%)
    ppermute x8, waiting for transfers between devices, shifted(): lax.ppermute(value, 'tp', [(i, (i + shift) % groups) for i in range(group...  27.1 us
    ppermute x8, starting transfers between devices, shifted(): lax.ppermute(value, 'tp', [(i, (i + shift) % groups) for i in range(group...  26.5 us
    all_to_all x1, waiting for transfers between devices, shards(): lax.all_to_all(summed.reshape(experts, capacity, quarter), 'ep', split_ax...  20.6 us
    all_to_all x1, waiting for transfers between devices, shards(): lax.all_to_all(outbound.reshape(experts, capacity, quarter), 'ep', split_...  20.6 us
    all_to_all x1, starting transfers between devices, shards(): lax.all_to_all(outbound.reshape(experts, capacity, quarter), 'ep', split_...  17.8 us
    all_to_all x1, starting transfers between devices, shards(): lax.all_to_all(summed.reshape(experts, capacity, quarter), 'ep', split_ax...  8.57 us
    dot_general x8, matrix products, project(): term = jnp.dot(piece, rows, preferred_element_type=jnp.float32)  6.23 us
  transfers between devices with their start and end apart: 10, of which 6 were waited for; matrix products, arithmetic and copies ran while one was open for 3% of the time, Pallas kernels for 0%

profile of v5, /device:TPU:2, one launch (start us, length us, event | category | flops | bytes accessed | tf_op | source)
XLA Modules:
  0.0 137.3 jit_solution(13325212426117259639)
XLA Ops:
  0.0 0.0 copy-start
  0.0 0.9 copy.19
  0.9 0.1 eq.99
  1.0 0.1 eq.95
  1.2 0.1 copy.21
  1.3 0.2 fusion.44
  1.6 0.2 fusion.45
  1.8 0.1 sub.7
  1.9 0.1 copy.23
  2.0 0.7 multiply_add_fusion
  2.7 1.2 convolution_convert_fusion.3
  3.9 0.9 reshape.51
  4.8 17.8 %all-to-all-start = ((bf16[128,4,512]{2,1,0:T(4,128)(2,1)}), bf16[128,4,512]{2,1,0:T(4,128)(2,1)S(1)}, u32[]{:S(2)}, u32[]{:S(2)}) async-start(bf16[128,4,512]{2,1,0:T(4,128)(2,1)} %reshape.51), calls=%async_computation | async-start | bytes 1048576 | tf_op jit(solution)/shard_map/all_to_all | solution.py:52
  22.7 20.6 %all-to-all-done = bf16[128,4,512]{2,1,0:T(4,128)(2,1)S(1)} async-done(((bf16[128,4,512]{2,1,0:T(4,128)(2,1)}), bf16[128,4,512]{2,1,0:T(4,128)(2,1)S(1)}, u32[]{:S(2)}, u32[]{:S(2)}) %all-to-all-start) | async-done | bytes 524320 | tf_op jit(solution)/shard_map/all_to_all | solution.py:52
  43.3 0.1 reshape.52
  43.4 3.4 %collective-permute-start = (bf16[512,512]{1,0:T(8,128)(2,1)S(1)}, bf16[512,512]{1,0:T(8,128)(2,1)S(1)}, u32[]{:S(2)}, u32[]{:S(2)}) collective-permute-start(bf16[512,512]{1,0:T(8,128)(2,1)S(1)} %reshape.52), channel_id=1, source_target_pairs={{0,1},{1,2},{2,3},{3,0},{4,5},{5,6},{6,7},{7,4},{8,9},{9,10},{10,1... | collective-permute-start | bytes 1572872 | tf_op jit(solution)/shard_map/ppermute | solution.py:8
  46.8 2.4 %collective-permute-start.1 = (bf16[512,512]{1,0:T(8,128)(2,1)S(1)}, bf16[512,512]{1,0:T(8,128)(2,1)}, u32[]{:S(2)}, u32[]{:S(2)}) collective-permute-start(bf16[512,512]{1,0:T(8,128)(2,1)S(1)} %reshape.52), channel_id=1, source_target_pairs={{0,3},{1,0},{2,1},{3,2},{4,7},{5,4},{6,5},{7,6},{8,11},{9,8},{10,9... | collective-permute-start | bytes 1572872 | tf_op jit(solution)/shard_map/ppermute | solution.py:8
  49.3 0.2 fusion.71
  49.4 0.1 slice.45
  49.5 4.0 %collective-permute-start.2 = (bf16[256,512]{1,0:T(8,128)(2,1)S(1)}, bf16[256,512]{1,0:T(8,128)(2,1)S(1)}, u32[]{:S(2)}, u32[]{:S(2)}) collective-permute-start(bf16[256,512]{1,0:T(8,128)(2,1)S(1)} %slice.45), channel_id=1, source_target_pairs={{0,2},{1,3},{2,0},{3,1},{4,6},{5,7},{6,4},{7,5},{8,10},{9,11},{10,... | collective-permute-start | bytes 786440 | tf_op jit(solution)/shard_map/ppermute | solution.py:8
  53.6 0.1 slice.47
  53.6 0.0 copy-start.2
  53.6 3.4 %collective-permute-start.3 = (bf16[256,512]{1,0:T(8,128)(2,1)S(1)}, bf16[256,512]{1,0:T(8,128)(2,1)S(1)}, u32[]{:S(2)}, u32[]{:S(2)}) collective-permute-start(bf16[256,512]{1,0:T(8,128)(2,1)S(1)} %slice.47), channel_id=1, source_target_pairs={{0,2},{1,3},{2,0},{3,1},{4,6},{5,7},{6,4},{7,5},{8,10},{9,11},{10,... | collective-permute-start | bytes 786440 | tf_op jit(solution)/shard_map/ppermute | solution.py:8
  57.1 1.4 fusion.22
  58.5 0.0 copy-done.2
  58.5 0.0 copy-start.1
  58.5 0.4 fusion.16
  58.9 10.9 %collective-permute-done.2 = bf16[256,512]{1,0:T(8,128)(2,1)S(1)} collective-permute-done((bf16[256,512]{1,0:T(8,128)(2,1)S(1)}, bf16[256,512]{1,0:T(8,128)(2,1)S(1)}, u32[]{:S(2)}, u32[]{:S(2)}) %collective-permute-start.2) | collective-permute-done | bytes 262176 | tf_op jit(solution)/shard_map/ppermute | solution.py:8
  69.8 2.8 %collective-permute-done.3 = bf16[256,512]{1,0:T(8,128)(2,1)S(1)} collective-permute-done((bf16[256,512]{1,0:T(8,128)(2,1)S(1)}, bf16[256,512]{1,0:T(8,128)(2,1)S(1)}, u32[]{:S(2)}, u32[]{:S(2)}) %collective-permute-start.3) | collective-permute-done | bytes 262176 | tf_op jit(solution)/shard_map/ppermute | solution.py:8
  72.6 0.0 copy-done.1
  72.6 0.4 fusion.18
  73.0 0.4 fusion.10
  73.4 0.0 collective-permute-done
  73.4 0.4 convolution_add_fusion.3
  73.8 0.4 convolution_add_fusion.1
  74.2 0.0 collective-permute-done.1
  74.2 1.4 %fusion.1 = f32[512,352]{0,1:T(8,128)S(1)} fusion(f32[512,352]{0,1:T(8,128)S(1)} %fusion.18, f32[512,352]{0,1:T(8,128)S(1)} %convolution_add_fusion.3, bf16[512,512]{1,0:T(8,128)(2,1)} %collective-permute-done.1, bf16[1,2048,352]{1,2,0:T(8,128)(2,1)S(1)} %copy-done.1, s32[]{:T(128)S(6)} %select_n.67), kind=kOutput, calls=%fused_computation.9 | convolution fusion | flops 184909824 | bytes 3047428 | tf_op jit(solution)/shard_map/dot_general | solution.py:62
  75.6 1.5 %multiply_convert_fusion = bf16[512,352]{0,1:T(8,128)(2,1)S(1)} fusion(f32[512,352]{0,1:T(8,128)S(1)} %fusion.1, f32[512,352]{0,1:T(8,128)S(1)} %fusion.10, f32[512,352]{0,1:T(8,128)S(1)} %convolution_add_fusion.1, bf16[512,512]{1,0:T(8,128)(2,1)} %collective-permute-done.1, bf16[1,2048,352]{1,2,0:T(8,128)(2,1)S(1)} %copy-done.2, s32[]{:T(128)S(6)} %select_n.67), kind=kOutput, calls=%fused_computation.15 | convolution fusion | flops 185991168 | bytes 3407876 | tf_op jit(solution)/shard_map/dot_general | solution.py:62
  77.1 0.0 copy-done
  77.1 0.5 convolution_convert_fusion.1
  77.6 0.5 convolution_convert_fusion
  78.1 1.9 %collective-permute-start.4 = (bf16[512,512]{1,0:T(8,128)(2,1)S(1)}, bf16[512,512]{1,0:T(8,128)(2,1)S(1)}, u32[]{:S(2)}, u32[]{:S(2)}) collective-permute-start(bf16[512,512]{1,0:T(8,128)(2,1)S(1)} %convolution_convert_fusion.1), channel_id=1, source_target_pairs={{0,1},{1,2},{2,3},{3,0},{4,5},{5,6},{6,7},{7,4},{8,9},{9,10},{10,1... | collective-permute-start | bytes 1572872 | tf_op jit(solution)/shard_map/ppermute | solution.py:8
  80.0 3.9 %collective-permute-start.5 = (bf16[512,512]{1,0:T(8,128)(2,1)S(1)}, bf16[512,512]{1,0:T(8,128)(2,1)S(1)}, u32[]{:S(2)}, u32[]{:S(2)}) collective-permute-start(bf16[512,512]{1,0:T(8,128)(2,1)S(1)} %convolution_convert_fusion), channel_id=1, source_target_pairs={{0,3},{1,0},{2,1},{3,2},{4,7},{5,4},{6,5},{7,6},{8,11},{9,8},{10,9... | collective-permute-start | bytes 1572872 | tf_op jit(solution)/shard_map/ppermute | solution.py:8
  83.9 0.3 convolution_convert_fusion.5
  84.3 0.3 convolution_convert_fusion.4
  84.6 3.4 %collective-permute-start.6 = (bf16[256,512]{1,0:T(8,128)(2,1)S(1)}, bf16[256,512]{1,0:T(8,128)(2,1)S(1)}, u32[]{:S(2)}, u32[]{:S(2)}) collective-permute-start(bf16[256,512]{1,0:T(8,128)(2,1)S(1)} %convolution_convert_fusion.5), channel_id=1, source_target_pairs={{0,2},{1,3},{2,0},{3,1},{4,6},{5,7},{6,4},{7,5},{8,10},{9,11},{10,... | collective-permute-start | bytes 786440 | tf_op jit(solution)/shard_map/ppermute | solution.py:8
  88.0 3.9 %collective-permute-start.7 = (bf16[256,512]{1,0:T(8,128)(2,1)S(1)}, bf16[256,512]{1,0:T(8,128)(2,1)S(1)}, u32[]{:S(2)}, u32[]{:S(2)}) collective-permute-start(bf16[256,512]{1,0:T(8,128)(2,1)S(1)} %convolution_convert_fusion.4), channel_id=1, source_target_pairs={{0,2},{1,3},{2,0},{3,1},{4,6},{5,7},{6,4},{7,5},{8,10},{9,11},{10,... | collective-permute-start | bytes 786440 | tf_op jit(solution)/shard_map/ppermute | solution.py:8
  91.9 10.6 %collective-permute-done.6 = bf16[256,512]{1,0:T(8,128)(2,1)S(1)} collective-permute-done((bf16[256,512]{1,0:T(8,128)(2,1)S(1)}, bf16[256,512]{1,0:T(8,128)(2,1)S(1)}, u32[]{:S(2)}, u32[]{:S(2)}) %collective-permute-start.6) | collective-permute-done | bytes 262176 | tf_op jit(solution)/shard_map/ppermute | solution.py:8
  102.6 2.8 %collective-permute-done.7 = bf16[256,512]{1,0:T(8,128)(2,1)S(1)} collective-permute-done((bf16[256,512]{1,0:T(8,128)(2,1)S(1)}, bf16[256,512]{1,0:T(8,128)(2,1)S(1)}, u32[]{:S(2)}, u32[]{:S(2)}) %collective-permute-start.7) | collective-permute-done | bytes 262176 | tf_op jit(solution)/shard_map/ppermute | solution.py:8
  105.4 0.0 collective-permute-done.4
  105.4 0.0 collective-permute-done.5
  105.4 0.6 add_convert_fusion
  106.0 0.0 copy-start.3
  106.0 0.9 reshape.53
  106.9 8.6 %all-to-all-start.1 = ((bf16[128,4,512]{2,1,0:T(4,128)(2,1)}), bf16[128,4,512]{2,1,0:T(4,128)(2,1)S(1)}, u32[]{:S(2)}, u32[]{:S(2)}) async-start(bf16[128,4,512]{2,1,0:T(4,128)(2,1)} %reshape.53), calls=%async_computation.1 | async-start | bytes 1048576 | tf_op jit(solution)/shard_map/all_to_all | solution.py:77
  115.5 0.0 copy-done.3
  115.5 20.6 %all-to-all-done.1 = bf16[128,4,512]{2,1,0:T(4,128)(2,1)S(1)} async-done(((bf16[128,4,512]{2,1,0:T(4,128)(2,1)}), bf16[128,4,512]{2,1,0:T(4,128)(2,1)S(1)}, u32[]{:S(2)}, u32[]{:S(2)}) %all-to-all-start.1) | async-done | bytes 524320 | tf_op jit(solution)/shard_map/all_to_all | solution.py:77
  136.1 0.1 reshape.54
  136.2 1.1 convolution_convert_fusion.6
  (11 shorter events, 0.1 us)
Async XLA Ops:
  0.0 77.1 %copy-start = (bf16[1,352,2048]{2,1,0:T(8,128)(2,1)S(1)}, bf16[1,352,2048]{2,1,0:T(8,128)(2,1)}, u32[]{:S(2)}) copy-start(bf16[1,352,2048]{2,1,0:T(8,128)(2,1)} %param.11) | copy-start | bytes 4325380
  4.8 38.4 %all-to-all-start = ((bf16[128,4,512]{2,1,0:T(4,128)(2,1)}), bf16[128,4,512]{2,1,0:T(4,128)(2,1)S(1)}, u32[]{:S(2)}, u32[]{:S(2)}) async-start(bf16[128,4,512]{2,1,0:T(4,128)(2,1)} %reshape.51), calls=%async_computation | async-start | bytes 1048576 | tf_op jit(solution)/shard_map/all_to_all | solution.py:52
  43.4 30.0 %collective-permute-start = (bf16[512,512]{1,0:T(8,128)(2,1)S(1)}, bf16[512,512]{1,0:T(8,128)(2,1)S(1)}, u32[]{:S(2)}, u32[]{:S(2)}) collective-permute-start(bf16[512,512]{1,0:T(8,128)(2,1)S(1)} %reshape.52), channel_id=1, source_target_pairs={{0,1},{1,2},{2,3},{3,0},{4,5},{5,6},{6,7},{7,4},{8,9},{9,10},{10,1... | collective-permute-start | bytes 1572872 | tf_op jit(solution)/shard_map/ppermute | solution.py:8
  46.8 27.4 %collective-permute-start.1 = (bf16[512,512]{1,0:T(8,128)(2,1)S(1)}, bf16[512,512]{1,0:T(8,128)(2,1)}, u32[]{:S(2)}, u32[]{:S(2)}) collective-permute-start(bf16[512,512]{1,0:T(8,128)(2,1)S(1)} %reshape.52), channel_id=1, source_target_pairs={{0,3},{1,0},{2,1},{3,2},{4,7},{5,4},{6,5},{7,6},{8,11},{9,8},{10,9... | collective-permute-start | bytes 1572872 | tf_op jit(solution)/shard_map/ppermute | solution.py:8
  49.5 20.2 %collective-permute-start.2 = (bf16[256,512]{1,0:T(8,128)(2,1)S(1)}, bf16[256,512]{1,0:T(8,128)(2,1)S(1)}, u32[]{:S(2)}, u32[]{:S(2)}) collective-permute-start(bf16[256,512]{1,0:T(8,128)(2,1)S(1)} %slice.45), channel_id=1, source_target_pairs={{0,2},{1,3},{2,0},{3,1},{4,6},{5,7},{6,4},{7,5},{8,10},{9,11},{10,... | collective-permute-start | bytes 786440 | tf_op jit(solution)/shard_map/ppermute | solution.py:8
  53.6 4.8 %copy-start.2 = (bf16[1,2048,352]{1,2,0:T(8,128)(2,1)S(1)}, bf16[1,2048,352]{1,2,0:T(8,128)(2,1)}, u32[]{:S(2)}) copy-start(bf16[1,2048,352]{1,2,0:T(8,128)(2,1)} %param.10) | copy-start | bytes 4325380
  53.6 18.9 %collective-permute-start.3 = (bf16[256,512]{1,0:T(8,128)(2,1)S(1)}, bf16[256,512]{1,0:T(8,128)(2,1)S(1)}, u32[]{:S(2)}, u32[]{:S(2)}) collective-permute-start(bf16[256,512]{1,0:T(8,128)(2,1)S(1)} %slice.47), channel_id=1, source_target_pairs={{0,2},{1,3},{2,0},{3,1},{4,6},{5,7},{6,4},{7,5},{8,10},{9,11},{10,... | collective-permute-start | bytes 786440 | tf_op jit(solution)/shard_map/ppermute | solution.py:8
  58.5 14.1 %copy-start.1 = (bf16[1,2048,352]{1,2,0:T(8,128)(2,1)S(1)}, bf16[1,2048,352]{1,2,0:T(8,128)(2,1)}, u32[]{:S(2)}) copy-start(bf16[1,2048,352]{1,2,0:T(8,128)(2,1)} %param.9) | copy-start | bytes 4325380
  78.1 27.3 %collective-permute-start.4 = (bf16[512,512]{1,0:T(8,128)(2,1)S(1)}, bf16[512,512]{1,0:T(8,128)(2,1)S(1)}, u32[]{:S(2)}, u32[]{:S(2)}) collective-permute-start(bf16[512,512]{1,0:T(8,128)(2,1)S(1)} %convolution_convert_fusion.1), channel_id=1, source_target_pairs={{0,1},{1,2},{2,3},{3,0},{4,5},{5,6},{6,7},{7,4},{8,9},{9,10},{10,1... | collective-permute-start | bytes 1572872 | tf_op jit(solution)/shard_map/ppermute | solution.py:8
  80.0 25.4 %collective-permute-start.5 = (bf16[512,512]{1,0:T(8,128)(2,1)S(1)}, bf16[512,512]{1,0:T(8,128)(2,1)S(1)}, u32[]{:S(2)}, u32[]{:S(2)}) collective-permute-start(bf16[512,512]{1,0:T(8,128)(2,1)S(1)} %convolution_convert_fusion), channel_id=1, source_target_pairs={{0,3},{1,0},{2,1},{3,2},{4,7},{5,4},{6,5},{7,6},{8,11},{9,8},{10,9... | collective-permute-start | bytes 1572872 | tf_op jit(solution)/shard_map/ppermute | solution.py:8
  84.6 18.0 %collective-permute-start.6 = (bf16[256,512]{1,0:T(8,128)(2,1)S(1)}, bf16[256,512]{1,0:T(8,128)(2,1)S(1)}, u32[]{:S(2)}, u32[]{:S(2)}) collective-permute-start(bf16[256,512]{1,0:T(8,128)(2,1)S(1)} %convolution_convert_fusion.5), channel_id=1, source_target_pairs={{0,2},{1,3},{2,0},{3,1},{4,6},{5,7},{6,4},{7,5},{8,10},{9,11},{10,... | collective-permute-start | bytes 786440 | tf_op jit(solution)/shard_map/ppermute | solution.py:8
  88.0 17.4 %collective-permute-start.7 = (bf16[256,512]{1,0:T(8,128)(2,1)S(1)}, bf16[256,512]{1,0:T(8,128)(2,1)S(1)}, u32[]{:S(2)}, u32[]{:S(2)}) collective-permute-start(bf16[256,512]{1,0:T(8,128)(2,1)S(1)} %convolution_convert_fusion.4), channel_id=1, source_target_pairs={{0,2},{1,3},{2,0},{3,1},{4,6},{5,7},{6,4},{7,5},{8,10},{9,11},{10,... | collective-permute-start | bytes 786440 | tf_op jit(solution)/shard_map/ppermute | solution.py:8
  106.0 9.5 %copy-start.3 = (f32[128,2]{0,1:T(2,128)S(1)}, f32[128,2]{0,1:T(2,128)}, u32[]{:S(2)}) copy-start(f32[128,2]{0,1:T(2,128)} %param.8) | copy-start | bytes 3076
  106.9 29.2 %all-to-all-start.1 = ((bf16[128,4,512]{2,1,0:T(4,128)(2,1)}), bf16[128,4,512]{2,1,0:T(4,128)(2,1)S(1)}, u32[]{:S(2)}, u32[]{:S(2)}) async-start(bf16[128,4,512]{2,1,0:T(4,128)(2,1)} %reshape.53), calls=%async_computation.1 | async-start | bytes 1048576 | tf_op jit(solution)/shard_map/all_to_all | solution.py:77

commit v6 on v4

--- a/solution.py
+++ b/solution.py
@@ -49,18 +49,28 @@
     second_hit = target[:, 1][None, :] == slot_iota[:, None]
     placer = (first_hit | second_hit).astype(jnp.bfloat16)
     own = lax.axis_index("tp")
-    own_cols = lax.dynamic_slice_in_dim(tokens, own * quarter, quarter, axis=1)
+    half_cols = width // 2
+    side = own % 2
+    own_cols = lax.dynamic_slice_in_dim(tokens, side * half_cols, half_cols, axis=1)
     outbound = jnp.dot(placer, own_cols, preferred_element_type=jnp.float32).astype(jnp.bfloat16)
     arrived = lax.all_to_all(
-        outbound.reshape(experts, capacity, quarter), "ep", split_axis=0, concat_axis=0, tiled=True
+        outbound.reshape(experts, capacity, half_cols), "ep", split_axis=0, concat_axis=0, tiled=True
     )
-    arrived = arrived.reshape(row_count, quarter)
-    pieces = ring_all_gather(arrived, groups, row_count)
+    arrived = arrived.reshape(row_count, half_cols)
+    half_rows = row_count // 2
+    other = jnp.concatenate(
+        [
+            lax.ppermute(arrived[:half_rows], "tp", [(i, (i - 1) % groups) for i in range(groups)]),
+            lax.ppermute(arrived[half_rows:], "tp", [(i, (i + 1) % groups) for i in range(groups)]),
+        ],
+        axis=0,
+    )
+    pieces = [(side, arrived), (1 - side, other)]
 
     def project(weight):
         acc = None
-        for k, piece in pieces:
-            rows = lax.dynamic_slice_in_dim(weight, ((own + k) % groups) * quarter, quarter, axis=0)
+        for h, piece in pieces:
+            rows = lax.dynamic_slice_in_dim(weight, h * half_cols, half_cols, axis=0)
             term = jnp.dot(piece, rows, preferred_element_type=jnp.float32)
             acc = term if acc is None else acc + term
         return acc

time: 131 us -> 140 us (1.069)
  blocking collectives: 37.6 us -> 0 us
  waiting for transfers between devices: 34.6 us -> 66.7 us
  starting transfers between devices: 43 us -> 53.3 us
  local copies, waits for them, and re-layouts: 2.9 us -> 8.49 us
  matrix products: 8.57 us -> 7.1 us
    all_to_all x1 -> x0, blocking collectives: 37.6 us -> none  [shards(): lax.all_to_all(outbound.reshape(experts, capacity, quarter), 'ep', split_...]
    all_to_all x0 -> x1, waiting for transfers between devices: none -> 30.4 us  [shards(): lax.all_to_all(outbound.reshape(experts, capacity, half_cols), 'ep', spli...]
    all_to_all x0 -> x1, starting transfers between devices: none -> 18.4 us  [shards(): lax.all_to_all(outbound.reshape(experts, capacity, half_cols), 'ep', spli...]
    ppermute x4 -> x2, starting transfers between devices: 13 us -> 6.29 us  [the longest x1 4.38 us: shards(): lax.ppermute(arrived[:half_rows], 'tp', [(i, (i - 1) % groups) for i in r...]
    slice x2 -> x3, local copies, waits for them, and re-layouts: 0.04 us -> 2.23 us  [the longest x2 1.31 us: shards(): arrived[half_rows:]]
    dot_general x8 -> x4, matrix products: 4.25 us -> 3.56 us  [project(): term = jnp.dot(piece, rows, preferred_element_type=jnp.float32)]
    ppermute x4 -> x2, waiting for transfers between devices: 8.5 us -> 9.1 us  [the longest x1 4.9 us: shards(): lax.ppermute(arrived[half_rows:], 'tp', [(i, (i + 1) % groups) for i in r...]
  transfers between devices with their start and end apart: 9 -> 8, of which waited for: 7 -> 7; matrix products, arithmetic and copies ran while one was open for 3% -> 5% of each run, Pallas kernels for 0% -> 0%
where the time goes in v6:
time: 140 us; the launch traced here: 138 us
  waiting for transfers between devices  66.7 us (48%)
  starting transfers between devices  53.3 us (38%)
  local copies, waits for them, and re-layouts  8.49 us (6%)
  matrix products  7.1 us (5%)
  other arithmetic  2.54 us (2%)
    all_to_all x1, waiting for transfers between devices, shards(): lax.all_to_all(outbound.reshape(experts, capacity, half_cols), 'ep', spli...  30.4 us
    all_to_all x1, waiting for transfers between devices, shards(): lax.all_to_all(summed.reshape(experts, capacity, quarter), 'ep', split_ax...  19.4 us
    all_to_all x1, starting transfers between devices, shards(): lax.all_to_all(outbound.reshape(experts, capacity, half_cols), 'ep', spli...  18.4 us
    all_to_all x1, starting transfers between devices, shards(): lax.all_to_all(summed.reshape(experts, capacity, quarter), 'ep', split_ax...  15.5 us
    ppermute x1, waiting for transfers between devices, shards(): lax.ppermute(arrived[half_rows:], 'tp', [(i, (i + 1) % groups) for i in r...  4.9 us
    ppermute x1, starting transfers between devices, ring_reduce_scatter(): from_hi = lax.ppermute(prev_dn.astype(jnp.bfloat16), 'tp', down)  4.67 us
    ppermute x1, starting transfers between devices, ring_reduce_scatter(): lax.ppermute(quarter_of(2, half, rows).astype(jnp.bfloat16), 'tp', down)  4.57 us
    ppermute x1, waiting for transfers between devices, ring_reduce_scatter(): from_lo = lax.ppermute(next_up.astype(jnp.bfloat16), 'tp', up)  4.4 us
  transfers between devices with their start and end apart: 8, of which 7 were waited for; matrix products, arithmetic and copies ran while one was open for 5% of the time, Pallas kernels for 0%

profile of v6, /device:TPU:1, one launch (start us, length us, event | category | flops | bytes accessed | tf_op | source)
XLA Modules:
  0.0 138.5 jit_solution(9453537553904063124)
XLA Ops:
  0.0 0.0 copy-start
  0.0 0.0 copy-start.3
  0.0 0.9 copy.19
  0.9 0.1 eq.92
  1.1 0.1 eq.88
  1.2 0.1 copy.21
  1.3 0.2 fusion.35
  1.6 0.2 fusion.36
  1.8 0.1 sub.10
  2.0 0.1 copy.23
  2.0 0.7 multiply_add_fusion
  2.8 0.0 copy-done.3
  2.8 0.4 convolution_convert_fusion
  3.2 1.2 reshape.96
  4.4 18.4 %all-to-all-start = ((bf16[128,4,1024]{2,1,0:T(4,128)(2,1)}), bf16[128,4,1024]{2,1,0:T(4,128)(2,1)S(1)}, u32[]{:S(2)}, u32[]{:S(2)}) async-start(bf16[128,4,1024]{2,1,0:T(4,128)(2,1)} %reshape.96), calls=%async_computation | async-start | bytes 2097152 | tf_op jit(solution)/shard_map/all_to_all | solution.py:56
  22.9 30.4 %all-to-all-done = bf16[128,4,1024]{2,1,0:T(4,128)(2,1)S(1)} async-done(((bf16[128,4,1024]{2,1,0:T(4,128)(2,1)}), bf16[128,4,1024]{2,1,0:T(4,128)(2,1)S(1)}, u32[]{:S(2)}, u32[]{:S(2)}) %all-to-all-start) | async-done | bytes 1048608 | tf_op jit(solution)/shard_map/all_to_all | solution.py:56
  53.3 0.4 fusion.57
  53.6 0.9 slice.83
  54.6 4.4 %collective-permute-start = (bf16[256,1024]{1,0:T(8,128)(2,1)}, bf16[256,1024]{1,0:T(8,128)(2,1)}, u32[]{:S(2)}, u32[]{:S(2)}) collective-permute-start(bf16[256,1024]{1,0:T(8,128)(2,1)} %slice.83), channel_id=1, source_target_pairs={{0,3},{1,0},{2,1},{3,2},{4,7},{5,4},{6,5},{7,6},{8,11},{9,8},{10,9... | collective-permute-start | bytes 1572872 | tf_op jit(solution)/shard_map/ppermute | solution.py:63
  59.0 0.9 slice.85
  59.9 1.9 %collective-permute-start.1 = (bf16[256,1024]{1,0:T(8,128)(2,1)}, bf16[256,1024]{1,0:T(8,128)(2,1)}, u32[]{:S(2)}, u32[]{:S(2)}) collective-permute-start(bf16[256,1024]{1,0:T(8,128)(2,1)} %slice.85), channel_id=1, source_target_pairs={{0,1},{1,2},{2,3},{3,0},{4,5},{5,6},{6,7},{7,4},{8,9},{9,10},{10,1... | collective-permute-start | bytes 1572872 | tf_op jit(solution)/shard_map/ppermute | solution.py:64
  61.8 0.3 reshape.97
  62.1 0.0 copy-start.2
  62.1 1.8 %fusion.9 = f32[512,352]{0,1:T(8,128)S(1)} fusion(bf16[512,1024]{1,0:T(8,128)(2,1)S(1)} %reshape.97, bf16[1,2048,352]{1,2,0:T(8,128)(2,1)} %param.13, s32[]{:T(128)S(6)} %select_n.48), kind=kOutput, calls=%fused_computation.19 | convolution fusion | flops 369098752 | bytes 2490372 | tf_op jit(solution)/shard_map/dot_general | solution.py:74
  63.9 0.0 copy-done.2
  63.9 0.6 fusion.6
  64.5 0.0 copy-start.1
  64.5 4.2 %collective-permute-done = bf16[256,1024]{1,0:T(8,128)(2,1)} collective-permute-done((bf16[256,1024]{1,0:T(8,128)(2,1)}, bf16[256,1024]{1,0:T(8,128)(2,1)}, u32[]{:S(2)}, u32[]{:S(2)}) %collective-permute-start) | collective-permute-done | bytes 524320 | tf_op jit(solution)/shard_map/ppermute | solution.py:63
  68.7 1.1 constant_dynamic-update-slice_fusion.1
  69.8 4.9 %collective-permute-done.1 = bf16[256,1024]{1,0:T(8,128)(2,1)} collective-permute-done((bf16[256,1024]{1,0:T(8,128)(2,1)}, bf16[256,1024]{1,0:T(8,128)(2,1)}, u32[]{:S(2)}, u32[]{:S(2)}) %collective-permute-start.1) | collective-permute-done | bytes 524320 | tf_op jit(solution)/shard_map/ppermute | solution.py:64
  74.7 1.1 constant_dynamic-update-slice_fusion
  75.8 0.0 copy-done.1
  75.8 0.6 convolution_add_fusion.1
  76.4 0.6 fusion.4
  77.0 0.0 copy-done
  77.0 0.5 fusion.1
  77.5 0.3 convolution_convert_fusion.5
  77.8 1.9 %collective-permute-start.2 = (bf16[256,512]{1,0:T(8,128)(2,1)S(1)}, bf16[256,512]{1,0:T(8,128)(2,1)S(1)}, u32[]{:S(2)}, u32[]{:S(2)}) collective-permute-start(bf16[256,512]{1,0:T(8,128)(2,1)S(1)} %convolution_convert_fusion.5), channel_id=1, source_target_pairs={{0,1},{1,2},{2,3},{3,0},{4,5},{5,6},{6,7},{7,4},{8,9},{9,10},{10,1... | collective-permute-start | bytes 786440 | tf_op jit(solution)/shard_map/ppermute | solution.py:11
  79.7 0.3 convolution_convert_fusion.4
  80.1 4.6 %collective-permute-start.4 = (bf16[256,512]{1,0:T(8,128)(2,1)S(1)}, bf16[256,512]{1,0:T(8,128)(2,1)S(1)}, u32[]{:S(2)}, u32[]{:S(2)}) collective-permute-start(bf16[256,512]{1,0:T(8,128)(2,1)S(1)} %convolution_convert_fusion.4), channel_id=1, source_target_pairs={{0,3},{1,0},{2,1},{3,2},{4,7},{5,4},{6,5},{7,6},{8,11},{9,8},{10,9... | collective-permute-start | bytes 786440 | tf_op jit(solution)/shard_map/ppermute | solution.py:12
  84.6 0.5 fusion.2
  85.1 1.0 collective-permute-done.2
  86.1 0.1 fusion.16
  86.3 0.1 convert_element_type.76
  86.3 1.9 %collective-permute-start.3 = (bf16[512,512]{1,0:T(8,128)(2,1)S(1)}, bf16[512,512]{1,0:T(8,128)(2,1)S(1)}, u32[]{:S(2)}, u32[]{:S(2)}) collective-permute-start(bf16[512,512]{1,0:T(8,128)(2,1)S(1)} %convert_element_type.76), channel_id=1, source_target_pairs={{0,1},{1,2},{2,3},{3,0},{4,5},{5,6},{6,7},{7,4},{8,9},{9,10},{10,1... | collective-permute-start | bytes 1572872 | tf_op jit(solution)/shard_map/ppermute | solution.py:17
  88.3 0.0 collective-permute-done.4
  88.3 0.1 fusion.15
  88.4 0.9 convert_element_type.82
  89.3 4.7 %collective-permute-start.5 = (bf16[512,512]{1,0:T(8,128)(2,1)}, bf16[512,512]{1,0:T(8,128)(2,1)S(1)}, u32[]{:S(2)}, u32[]{:S(2)}) collective-permute-start(bf16[512,512]{1,0:T(8,128)(2,1)} %convert_element_type.82), channel_id=1, source_target_pairs={{0,3},{1,0},{2,1},{3,2},{4,7},{5,4},{6,5},{7,6},{8,11},{9,8},{10,9... | collective-permute-start | bytes 1572872 | tf_op jit(solution)/shard_map/ppermute | solution.py:18
  94.0 0.5 fusion
  94.4 4.4 %collective-permute-done.3 = bf16[512,512]{1,0:T(8,128)(2,1)S(1)} collective-permute-done((bf16[512,512]{1,0:T(8,128)(2,1)S(1)}, bf16[512,512]{1,0:T(8,128)(2,1)S(1)}, u32[]{:S(2)}, u32[]{:S(2)}) %collective-permute-start.3) | collective-permute-done | bytes 524320 | tf_op jit(solution)/shard_map/ppermute | solution.py:17
  98.8 2.3 %collective-permute-done.5 = bf16[512,512]{1,0:T(8,128)(2,1)S(1)} collective-permute-done((bf16[512,512]{1,0:T(8,128)(2,1)}, bf16[512,512]{1,0:T(8,128)(2,1)S(1)}, u32[]{:S(2)}, u32[]{:S(2)}) %collective-permute-start.5) | collective-permute-done | bytes 524320 | tf_op jit(solution)/shard_map/ppermute | solution.py:18
  101.1 0.2 add_convert_fusion
  101.4 0.0 copy-start.4
  101.4 0.9 reshape.98
  102.3 15.5 %all-to-all-start.1 = ((bf16[128,4,512]{2,1,0:T(4,128)(2,1)}), bf16[128,4,512]{2,1,0:T(4,128)(2,1)S(1)}, u32[]{:S(2)}, u32[]{:S(2)}) async-start(bf16[128,4,512]{2,1,0:T(4,128)(2,1)} %reshape.98), calls=%async_computation.1 | async-start | bytes 1048576 | tf_op jit(solution)/shard_map/all_to_all | solution.py:89
  117.8 0.0 copy-done.4
  117.9 19.4 %all-to-all-done.1 = bf16[128,4,512]{2,1,0:T(4,128)(2,1)S(1)} async-done(((bf16[128,4,512]{2,1,0:T(4,128)(2,1)}), bf16[128,4,512]{2,1,0:T(4,128)(2,1)S(1)}, u32[]{:S(2)}, u32[]{:S(2)}) %all-to-all-start.1) | async-done | bytes 524320 | tf_op jit(solution)/shard_map/all_to_all | solution.py:89
  137.3 0.1 reshape.99
  137.4 1.1 convolution_convert_fusion.6
  (9 shorter events, 0.1 us)
Async XLA Ops:
  0.0 77.0 %copy-start = (bf16[1,352,2048]{2,1,0:T(8,128)(2,1)S(1)}, bf16[1,352,2048]{2,1,0:T(8,128)(2,1)}, u32[]{:S(2)}) copy-start(bf16[1,352,2048]{2,1,0:T(8,128)(2,1)} %param.15) | copy-start | bytes 4325380
  0.0 2.8 %copy-start.3 = (bf16[128,2048]{1,0:T(8,128)(2,1)S(1)}, bf16[128,2048]{1,0:T(8,128)(2,1)}, u32[]{:S(2)}) copy-start(bf16[128,2048]{1,0:T(8,128)(2,1)} %param.10) | copy-start | bytes 1572868
  4.4 48.9 %all-to-all-start = ((bf16[128,4,1024]{2,1,0:T(4,128)(2,1)}), bf16[128,4,1024]{2,1,0:T(4,128)(2,1)S(1)}, u32[]{:S(2)}, u32[]{:S(2)}) async-start(bf16[128,4,1024]{2,1,0:T(4,128)(2,1)} %reshape.96), calls=%async_computation | async-start | bytes 2097152 | tf_op jit(solution)/shard_map/all_to_all | solution.py:56
  54.6 14.1 %collective-permute-start = (bf16[256,1024]{1,0:T(8,128)(2,1)}, bf16[256,1024]{1,0:T(8,128)(2,1)}, u32[]{:S(2)}, u32[]{:S(2)}) collective-permute-start(bf16[256,1024]{1,0:T(8,128)(2,1)} %slice.83), channel_id=1, source_target_pairs={{0,3},{1,0},{2,1},{3,2},{4,7},{5,4},{6,5},{7,6},{8,11},{9,8},{10,9... | collective-permute-start | bytes 1572872 | tf_op jit(solution)/shard_map/ppermute | solution.py:63
  59.9 14.8 %collective-permute-start.1 = (bf16[256,1024]{1,0:T(8,128)(2,1)}, bf16[256,1024]{1,0:T(8,128)(2,1)}, u32[]{:S(2)}, u32[]{:S(2)}) collective-permute-start(bf16[256,1024]{1,0:T(8,128)(2,1)} %slice.85), channel_id=1, source_target_pairs={{0,1},{1,2},{2,3},{3,0},{4,5},{5,6},{6,7},{7,4},{8,9},{9,10},{10,1... | collective-permute-start | bytes 1572872 | tf_op jit(solution)/shard_map/ppermute | solution.py:64
  62.1 1.8 %copy-start.2 = (bf16[1,2048,352]{1,2,0:T(8,128)(2,1)S(1)}, bf16[1,2048,352]{1,2,0:T(8,128)(2,1)}, u32[]{:S(2)}) copy-start(bf16[1,2048,352]{1,2,0:T(8,128)(2,1)} %param.14) | copy-start | bytes 4325380
  64.5 11.3 %copy-start.1 = (bf16[1,2048,352]{1,2,0:T(8,128)(2,1)S(1)}, bf16[1,2048,352]{1,2,0:T(8,128)(2,1)}, u32[]{:S(2)}) copy-start(bf16[1,2048,352]{1,2,0:T(8,128)(2,1)} %param.13) | copy-start | bytes 4325380
  77.8 8.3 %collective-permute-start.2 = (bf16[256,512]{1,0:T(8,128)(2,1)S(1)}, bf16[256,512]{1,0:T(8,128)(2,1)S(1)}, u32[]{:S(2)}, u32[]{:S(2)}) collective-permute-start(bf16[256,512]{1,0:T(8,128)(2,1)S(1)} %convolution_convert_fusion.5), channel_id=1, source_target_pairs={{0,1},{1,2},{2,3},{3,0},{4,5},{5,6},{6,7},{7,4},{8,9},{9,10},{10,1... | collective-permute-start | bytes 786440 | tf_op jit(solution)/shard_map/ppermute | solution.py:11
  80.1 8.2 %collective-permute-start.4 = (bf16[256,512]{1,0:T(8,128)(2,1)S(1)}, bf16[256,512]{1,0:T(8,128)(2,1)S(1)}, u32[]{:S(2)}, u32[]{:S(2)}) collective-permute-start(bf16[256,512]{1,0:T(8,128)(2,1)S(1)} %convolution_convert_fusion.4), channel_id=1, source_target_pairs={{0,3},{1,0},{2,1},{3,2},{4,7},{5,4},{6,5},{7,6},{8,11},{9,8},{10,9... | collective-permute-start | bytes 786440 | tf_op jit(solution)/shard_map/ppermute | solution.py:12
  86.3 12.5 %collective-permute-start.3 = (bf16[512,512]{1,0:T(8,128)(2,1)S(1)}, bf16[512,512]{1,0:T(8,128)(2,1)S(1)}, u32[]{:S(2)}, u32[]{:S(2)}) collective-permute-start(bf16[512,512]{1,0:T(8,128)(2,1)S(1)} %convert_element_type.76), channel_id=1, source_target_pairs={{0,1},{1,2},{2,3},{3,0},{4,5},{5,6},{6,7},{7,4},{8,9},{9,10},{10,1... | collective-permute-start | bytes 1572872 | tf_op jit(solution)/shard_map/ppermute | solution.py:17
  89.3 11.9 %collective-permute-start.5 = (bf16[512,512]{1,0:T(8,128)(2,1)}, bf16[512,512]{1,0:T(8,128)(2,1)S(1)}, u32[]{:S(2)}, u32[]{:S(2)}) collective-permute-start(bf16[512,512]{1,0:T(8,128)(2,1)} %convert_element_type.82), channel_id=1, source_target_pairs={{0,3},{1,0},{2,1},{3,2},{4,7},{5,4},{6,5},{7,6},{8,11},{9,8},{10,9... | collective-permute-start | bytes 1572872 | tf_op jit(solution)/shard_map/ppermute | solution.py:18
  101.4 16.5 %copy-start.4 = (f32[128,2]{0,1:T(2,128)S(1)}, f32[128,2]{0,1:T(2,128)}, u32[]{:S(2)}) copy-start(f32[128,2]{0,1:T(2,128)} %param.12) | copy-start | bytes 3076
  102.3 35.0 %all-to-all-start.1 = ((bf16[128,4,512]{2,1,0:T(4,128)(2,1)}), bf16[128,4,512]{2,1,0:T(4,128)(2,1)S(1)}, u32[]{:S(2)}, u32[]{:S(2)}) async-start(bf16[128,4,512]{2,1,0:T(4,128)(2,1)} %reshape.98), calls=%async_computation.1 | async-start | bytes 1048576 | tf_op jit(solution)/shard_map/all_to_all | solution.py:89

commit v7 on v4

--- a/solution.py
+++ b/solution.py
@@ -27,8 +27,7 @@
     from_hi = lax.ppermute(block, "tp", down)
     far_a = lax.ppermute(from_lo[:half], "tp", up)
     far_b = lax.ppermute(from_hi[half:], "tp", down)
-    far = jnp.concatenate([far_a, far_b], axis=0)
-    return [(0, block), (groups - 1, from_lo), (1, from_hi), (2, far)]
+    return block, from_lo, from_hi, far_a, far_b
 
 
 def shards(tokens, expert_ids, gate_values, w_gate, w_up, w_down):
@@ -40,9 +39,9 @@
     capacity = 4 * tok_rows // experts
     row_count = experts * capacity
     flat_ids = expert_ids.reshape(-1)
-    onehot = (flat_ids[:, None] == jnp.arange(experts, dtype=jnp.int32)[None, :]).astype(jnp.int32)
-    running = jnp.cumsum(onehot, axis=0)
-    position = jnp.sum(running * onehot, axis=1) - 1
+    pair_iota = jnp.arange(flat_ids.shape[0], dtype=jnp.int32)
+    earlier_same = (flat_ids[:, None] == flat_ids[None, :]) & (pair_iota[None, :] < pair_iota[:, None])
+    position = jnp.sum(earlier_same.astype(jnp.int32), axis=1)
     target = (flat_ids * capacity + position).reshape(tok_rows, 2)
     slot_iota = jnp.arange(row_count, dtype=jnp.int32)
     first_hit = target[:, 0][None, :] == slot_iota[:, None]
@@ -55,19 +54,26 @@
         outbound.reshape(experts, capacity, quarter), "ep", split_axis=0, concat_axis=0, tiled=True
     )
     arrived = arrived.reshape(row_count, quarter)
-    pieces = ring_all_gather(arrived, groups, row_count)
+    block, from_lo, from_hi, far_a, far_b = ring_all_gather(arrived, groups, row_count)
+    half = row_count // 2
 
-    def project(weight):
+    def project(weight, lo, hi, far):
         acc = None
-        for k, piece in pieces:
+        for k, piece in ((0, block[lo:hi]), (groups - 1, from_lo[lo:hi]), (1, from_hi[lo:hi]), (2, far)):
             rows = lax.dynamic_slice_in_dim(weight, ((own + k) % groups) * quarter, quarter, axis=0)
             term = jnp.dot(piece, rows, preferred_element_type=jnp.float32)
             acc = term if acc is None else acc + term
         return acc
 
-    gate = project(w_gate[0])
-    up = project(w_up[0])
-    hidden = (jax.nn.silu(gate) * up).astype(jnp.bfloat16)
+    hidden = jnp.concatenate(
+        [
+            (
+                jax.nn.silu(project(w_gate[0], lo, hi, far)) * project(w_up[0], lo, hi, far)
+            ).astype(jnp.bfloat16)
+            for lo, hi, far in ((0, half, far_a), (half, row_count, far_b))
+        ],
+        axis=0,
+    )
     down = w_down[0]
 
     def quarter_of(k, lo, hi):

time: 131 us -> 143 us (1.092)
  blocking collectives: 37.6 us -> 0 us
  starting transfers between devices: 43 us -> 60.1 us
  waiting for transfers between devices: 34.6 us -> 50.7 us
  matrix products: 8.57 us -> 20.1 us
  local copies, waits for them, and re-layouts: 2.9 us -> 8.23 us
    all_to_all x1 -> x0, blocking collectives: 37.6 us -> none  [shards(): lax.all_to_all(outbound.reshape(experts, capacity, quarter), 'ep', split_...]
    all_to_all x0 -> x1, waiting for transfers between devices: none -> 19.4 us  [shards(): lax.all_to_all(outbound.reshape(experts, capacity, quarter), 'ep', split_...]
    all_to_all x0 -> x1, starting transfers between devices: none -> 18.4 us  [shards(): lax.all_to_all(outbound.reshape(experts, capacity, quarter), 'ep', split_...]
    dot_general x8 -> x16, matrix products: 4.25 us -> 15.8 us  [project(): term = jnp.dot(piece, rows, preferred_element_type=jnp.float32)]
    ppermute x1, waiting for transfers between devices: 6.03 us -> 0.01 us  [ring_all_gather(): from_lo = lax.ppermute(block, 'tp', up)]
    ppermute x1, waiting for transfers between devices: 1.03 us -> 5.46 us  [ring_reduce_scatter(): far_a = lax.ppermute(quarter_of(2, 0, half).astype(jnp.bfloat16), 'tp', up)]
    slice x2 -> x5, local copies, waits for them, and re-layouts: 0.04 us -> 4.04 us  [the longest x3 2.11 us: project(): block[lo:hi]]
    all_to_all x1, starting transfers between devices: 16.5 us -> 14.9 us  [shards(): lax.all_to_all(summed.reshape(experts, capacity, quarter), 'ep', split_ax...]
  transfers between devices with their start and end apart: 9 -> 10, of which waited for: 7 -> 6; matrix products, arithmetic and copies ran while one was open for 3% -> 16% of each run, Pallas kernels for 0% -> 0%
where the time goes in v7:
time: 143 us; the launch traced here: 141 us
  starting transfers between devices  60.1 us (42%)
  waiting for transfers between devices  50.7 us (35%)
  matrix products  20.1 us (14%)
  local copies, waits for them, and re-layouts  8.23 us (6%)
  other arithmetic  1.49 us (1%)
    all_to_all x1, waiting for transfers between devices, shards(): lax.all_to_all(summed.reshape(experts, capacity, quarter), 'ep', split_ax...  19.4 us
    all_to_all x1, waiting for transfers between devices, shards(): lax.all_to_all(outbound.reshape(experts, capacity, quarter), 'ep', split_...  19.4 us
    all_to_all x1, starting transfers between devices, shards(): lax.all_to_all(outbound.reshape(experts, capacity, quarter), 'ep', split_...  18.4 us
    dot_general x16, matrix products, project(): term = jnp.dot(piece, rows, preferred_element_type=jnp.float32)  15.8 us
    all_to_all x1, starting transfers between devices, shards(): lax.all_to_all(summed.reshape(experts, capacity, quarter), 'ep', split_ax...  14.9 us
    ppermute x1, waiting for transfers between devices, ring_reduce_scatter(): far_a = lax.ppermute(quarter_of(2, 0, half).astype(jnp.bfloat16), 'tp', up)  5.46 us
    ppermute x1, starting transfers between devices, ring_all_gather(): far_b = lax.ppermute(from_hi[half:], 'tp', down)  5.32 us
    ppermute x1, starting transfers between devices, ring_reduce_scatter(): lax.ppermute(quarter_of(2, half, rows).astype(jnp.bfloat16), 'tp', down)  4.57 us
  transfers between devices with their start and end apart: 10, of which 6 were waited for; matrix products, arithmetic and copies ran while one was open for 16% of the time, Pallas kernels for 0%

profile of v7, /device:TPU:1, one launch (start us, length us, event | category | flops | bytes accessed | tf_op | source)
XLA Modules:
  0.0 141.1 jit_solution(14046342221794542535)
XLA Ops:
  0.0 0.9 copy.16
  0.9 0.1 eq.93
  1.0 0.2 convert_reduce_fusion
  1.2 0.1 reduce_sum.12
  1.4 0.1 copy.17
  1.4 0.7 multiply_add_fusion
  2.1 1.2 convolution_convert_fusion.3
  3.4 0.9 reshape.82
  4.3 18.4 %all-to-all-start = ((bf16[128,4,512]{2,1,0:T(4,128)(2,1)}), bf16[128,4,512]{2,1,0:T(4,128)(2,1)S(1)}, u32[]{:S(2)}, u32[]{:S(2)}) async-start(bf16[128,4,512]{2,1,0:T(4,128)(2,1)} %reshape.82), calls=%async_computation | async-start | bytes 1048576 | tf_op jit(solution)/shard_map/all_to_all | solution.py:53
  22.8 19.4 %all-to-all-done = bf16[128,4,512]{2,1,0:T(4,128)(2,1)S(1)} async-done(((bf16[128,4,512]{2,1,0:T(4,128)(2,1)}), bf16[128,4,512]{2,1,0:T(4,128)(2,1)S(1)}, u32[]{:S(2)}, u32[]{:S(2)}) %all-to-all-start) | async-done | bytes 524320 | tf_op jit(solution)/shard_map/all_to_all | solution.py:53
  42.1 0.9 reshape.83
  43.1 4.5 %collective-permute-start.1 = (bf16[512,512]{1,0:T(8,128)(2,1)}, bf16[512,512]{1,0:T(8,128)(2,1)}, u32[]{:S(2)}, u32[]{:S(2)}) collective-permute-start(bf16[512,512]{1,0:T(8,128)(2,1)} %reshape.83), channel_id=1, source_target_pairs={{0,3},{1,0},{2,1},{3,2},{4,7},{5,4},{6,5},{7,6},{8,11},{9,8},{10,9... | collective-permute-start | bytes 1572872 | tf_op jit(solution)/shard_map/ppermute | solution.py:27
  47.6 1.9 %collective-permute-start = (bf16[512,512]{1,0:T(8,128)(2,1)}, bf16[512,512]{1,0:T(8,128)(2,1)}, u32[]{:S(2)}, u32[]{:S(2)}) collective-permute-start(bf16[512,512]{1,0:T(8,128)(2,1)} %reshape.83), channel_id=1, source_target_pairs={{0,1},{1,2},{2,3},{3,0},{4,5},{5,6},{6,7},{7,4},{8,9},{9,10},{10,1... | collective-permute-start | bytes 1572872 | tf_op jit(solution)/shard_map/ppermute | solution.py:26
  49.5 1.0 fusion.111
  50.5 1.1 slice.93
  51.5 2.0 %fusion.22 = f32[256,352]{0,1:T(8,128)} fusion(bf16[256,512]{1,0:T(8,128)(2,1)S(1)} %slice.93, bf16[1,2048,352]{1,2,0:T(8,128)(2,1)} %param.14, s32[]{:T(128)S(6)} %select_n.87), kind=kOutput, calls=%fused_computation.41 | convolution fusion | flops 92274688 | bytes 983044 | tf_op jit(solution)/shard_map/dot_general | solution.py:64
  53.6 1.0 fusion.34
  54.6 0.1 slice.89
  54.7 1.3 fusion.24
  55.9 0.3 fusion.36
  56.2 0.0 copy-start.2
  56.2 0.8 collective-permute-done.1
  57.1 1.0 slice.103
  58.0 5.3 %collective-permute-start.3 = (bf16[256,512]{1,0:T(8,128)(2,1)S(1)}, bf16[256,512]{1,0:T(8,128)(2,1)S(1)}, u32[]{:S(2)}, u32[]{:S(2)}) collective-permute-start(bf16[256,512]{1,0:T(8,128)(2,1)S(1)} %slice.103), channel_id=1, source_target_pairs={{0,3},{1,0},{2,1},{3,2},{4,7},{5,4},{6,5},{7,6},{8,11},{9,8},{10,9... | collective-permute-start | bytes 786440 | tf_op jit(solution)/shard_map/ppermute | solution.py:29
  63.4 0.0 collective-permute-done
  63.4 1.0 slice.99
  64.4 2.1 %collective-permute-start.2 = (bf16[256,512]{1,0:T(8,128)(2,1)S(1)}, bf16[256,512]{1,0:T(8,128)(2,1)S(1)}, u32[]{:S(2)}, u32[]{:S(2)}) collective-permute-start(bf16[256,512]{1,0:T(8,128)(2,1)S(1)} %slice.99), channel_id=1, source_target_pairs={{0,1},{1,2},{2,3},{3,0},{4,5},{5,6},{6,7},{7,4},{8,9},{9,10},{10,1... | collective-permute-start | bytes 786440 | tf_op jit(solution)/shard_map/ppermute | solution.py:28
  66.4 1.2 convolution_add_fusion.7
  67.7 1.3 convolution_add_fusion.5
  69.0 1.2 convolution_add_fusion.1
  70.3 1.2 convolution_add_fusion.3
  71.5 0.3 fusion.14
  71.8 0.3 fusion.26
  72.1 1.2 fusion.5
  73.4 1.3 multiply_convert_fusion
  74.6 0.3 convolution_convert_fusion.4
  75.0 4.6 %collective-permute-start.6 = (bf16[256,512]{1,0:T(8,128)(2,1)S(1)}, bf16[256,512]{1,0:T(8,128)(2,1)S(1)}, u32[]{:S(2)}, u32[]{:S(2)}) collective-permute-start(bf16[256,512]{1,0:T(8,128)(2,1)S(1)} %convolution_convert_fusion.4), channel_id=1, source_target_pairs={{0,3},{1,0},{2,1},{3,2},{4,7},{5,4},{6,5},{7,6},{8,11},{9,8},{10,9... | collective-permute-start | bytes 786440 | tf_op jit(solution)/shard_map/ppermute | solution.py:12
  79.5 0.0 collective-permute-done.2
  79.6 0.3 fusion.16
  79.8 0.3 fusion.28
  80.1 1.3 fusion.3
  81.4 1.3 multiply_convert_fusion.1
  82.7 0.3 convolution_convert_fusion.5
  83.0 1.9 %collective-permute-start.4 = (bf16[256,512]{1,0:T(8,128)(2,1)S(1)}, bf16[256,512]{1,0:T(8,128)(2,1)S(1)}, u32[]{:S(2)}, u32[]{:S(2)}) collective-permute-start(bf16[256,512]{1,0:T(8,128)(2,1)S(1)} %convolution_convert_fusion.5), channel_id=1, source_target_pairs={{0,1},{1,2},{2,3},{3,0},{4,5},{5,6},{6,7},{7,4},{8,9},{9,10},{10,1... | collective-permute-start | bytes 786440 | tf_op jit(solution)/shard_map/ppermute | solution.py:11
  84.9 0.5 fusion.1
  85.4 0.5 fusion.2
  85.9 5.5 %collective-permute-done.4 = bf16[256,512]{1,0:T(8,128)(2,1)S(1)} collective-permute-done((bf16[256,512]{1,0:T(8,128)(2,1)S(1)}, bf16[256,512]{1,0:T(8,128)(2,1)S(1)}, u32[]{:S(2)}, u32[]{:S(2)}) %collective-permute-start.4) | collective-permute-done | bytes 262176 | tf_op jit(solution)/shard_map/ppermute | solution.py:11
  91.3 0.1 fusion.8
  91.5 0.1 convert_element_type.78
  91.5 1.9 %collective-permute-start.5 = (bf16[512,512]{1,0:T(8,128)(2,1)S(1)}, bf16[512,512]{1,0:T(8,128)(2,1)S(1)}, u32[]{:S(2)}, u32[]{:S(2)}) collective-permute-start(bf16[512,512]{1,0:T(8,128)(2,1)S(1)} %convert_element_type.78), channel_id=1, source_target_pairs={{0,1},{1,2},{2,3},{3,0},{4,5},{5,6},{6,7},{7,4},{8,9},{9,10},{10,1... | collective-permute-start | bytes 1572872 | tf_op jit(solution)/shard_map/ppermute | solution.py:17
  93.5 0.0 collective-permute-done.6
  93.5 0.1 fusion.7
  93.6 0.1 convert_element_type.84
  93.7 4.6 %collective-permute-start.7 = (bf16[512,512]{1,0:T(8,128)(2,1)S(1)}, bf16[512,512]{1,0:T(8,128)(2,1)S(1)}, u32[]{:S(2)}, u32[]{:S(2)}) collective-permute-start(bf16[512,512]{1,0:T(8,128)(2,1)S(1)} %convert_element_type.84), channel_id=1, source_target_pairs={{0,3},{1,0},{2,1},{3,2},{4,7},{5,4},{6,5},{7,6},{8,11},{9,8},{10,9... | collective-permute-start | bytes 1572872 | tf_op jit(solution)/shard_map/ppermute | solution.py:18
  98.3 0.5 fusion
  98.7 4.5 %collective-permute-done.5 = bf16[512,512]{1,0:T(8,128)(2,1)S(1)} collective-permute-done((bf16[512,512]{1,0:T(8,128)(2,1)S(1)}, bf16[512,512]{1,0:T(8,128)(2,1)S(1)}, u32[]{:S(2)}, u32[]{:S(2)}) %collective-permute-start.5) | collective-permute-done | bytes 524320 | tf_op jit(solution)/shard_map/ppermute | solution.py:17
  103.2 1.2 collective-permute-done.7
  104.4 0.2 add_convert_fusion
  104.6 0.0 copy-start.6
  104.6 0.9 reshape.84
  105.5 14.9 %all-to-all-start.1 = ((bf16[128,4,512]{2,1,0:T(4,128)(2,1)}), bf16[128,4,512]{2,1,0:T(4,128)(2,1)S(1)}, u32[]{:S(2)}, u32[]{:S(2)}) async-start(bf16[128,4,512]{2,1,0:T(4,128)(2,1)} %reshape.84), calls=%async_computation.1 | async-start | bytes 1048576 | tf_op jit(solution)/shard_map/all_to_all | solution.py:85
  120.4 19.4 %all-to-all-done.1 = bf16[128,4,512]{2,1,0:T(4,128)(2,1)S(1)} async-done(((bf16[128,4,512]{2,1,0:T(4,128)(2,1)}), bf16[128,4,512]{2,1,0:T(4,128)(2,1)S(1)}, u32[]{:S(2)}, u32[]{:S(2)}) %all-to-all-start.1) | async-done | bytes 524320 | tf_op jit(solution)/shard_map/all_to_all | solution.py:85
  139.8 0.1 reshape.85
  140.0 1.1 convolution_convert_fusion.6
  (15 shorter events, 0.0 us)
Async XLA Ops:
  0.0 74.6 %copy-start = (bf16[1,352,2048]{2,1,0:T(8,128)(2,1)S(1)}, bf16[1,352,2048]{2,1,0:T(8,128)(2,1)}, u32[]{:S(2)}) copy-start(bf16[1,352,2048]{2,1,0:T(8,128)(2,1)} %param.15) | copy-start | bytes 4325380
  4.3 37.8 %all-to-all-start = ((bf16[128,4,512]{2,1,0:T(4,128)(2,1)}), bf16[128,4,512]{2,1,0:T(4,128)(2,1)S(1)}, u32[]{:S(2)}, u32[]{:S(2)}) async-start(bf16[128,4,512]{2,1,0:T(4,128)(2,1)} %reshape.82), calls=%async_computation | async-start | bytes 1048576 | tf_op jit(solution)/shard_map/all_to_all | solution.py:53
  43.1 10.5 %copy-start.1 = (bf16[1,2048,352]{1,2,0:T(8,128)(2,1)S(1)}, bf16[1,2048,352]{1,2,0:T(8,128)(2,1)}, u32[]{:S(2)}) copy-start(bf16[1,2048,352]{1,2,0:T(8,128)(2,1)} %param.13) | copy-start | bytes 4325380
  43.1 14.0 %collective-permute-start.1 = (bf16[512,512]{1,0:T(8,128)(2,1)}, bf16[512,512]{1,0:T(8,128)(2,1)}, u32[]{:S(2)}, u32[]{:S(2)}) collective-permute-start(bf16[512,512]{1,0:T(8,128)(2,1)} %reshape.83), channel_id=1, source_target_pairs={{0,3},{1,0},{2,1},{3,2},{4,7},{5,4},{6,5},{7,6},{8,11},{9,8},{10,9... | collective-permute-start | bytes 1572872 | tf_op jit(solution)/shard_map/ppermute | solution.py:27
  47.6 15.8 %collective-permute-start = (bf16[512,512]{1,0:T(8,128)(2,1)}, bf16[512,512]{1,0:T(8,128)(2,1)}, u32[]{:S(2)}, u32[]{:S(2)}) collective-permute-start(bf16[512,512]{1,0:T(8,128)(2,1)} %reshape.83), channel_id=1, source_target_pairs={{0,1},{1,2},{2,3},{3,0},{4,5},{5,6},{6,7},{7,4},{8,9},{9,10},{10,1... | collective-permute-start | bytes 1572872 | tf_op jit(solution)/shard_map/ppermute | solution.py:26
  50.5 4.1 %copy-start.5 = (bf16[64,4,512]{2,1,0:T(4,128)(2,1)S(1)}, bf16[64,4,512]{2,1,0:T(4,128)(2,1)}, u32[]{:S(2)}) copy-start(bf16[64,4,512]{2,1,0:T(4,128)(2,1)} %get-tuple-element.29) | copy-start | bytes 786436
  56.2 11.4 %copy-start.2 = (bf16[1,2048,352]{1,2,0:T(8,128)(2,1)S(1)}, bf16[1,2048,352]{1,2,0:T(8,128)(2,1)}, u32[]{:S(2)}) copy-start(bf16[1,2048,352]{1,2,0:T(8,128)(2,1)} %param.14) | copy-start | bytes 4325380
  58.0 13.5 %collective-permute-start.3 = (bf16[256,512]{1,0:T(8,128)(2,1)S(1)}, bf16[256,512]{1,0:T(8,128)(2,1)S(1)}, u32[]{:S(2)}, u32[]{:S(2)}) collective-permute-start(bf16[256,512]{1,0:T(8,128)(2,1)S(1)} %slice.103), channel_id=1, source_target_pairs={{0,3},{1,0},{2,1},{3,2},{4,7},{5,4},{6,5},{7,6},{8,11},{9,8},{10,9... | collective-permute-start | bytes 786440 | tf_op jit(solution)/shard_map/ppermute | solution.py:29
  64.3 4.6 %copy-start.4 = (f32[256,352]{0,1:T(8,128)S(1)}, f32[256,352]{0,1:T(8,128)}, u32[]{:S(2)}) copy-start(f32[256,352]{0,1:T(8,128)} %fusion.22) | copy-start | bytes 1081348
  64.4 15.2 %collective-permute-start.2 = (bf16[256,512]{1,0:T(8,128)(2,1)S(1)}, bf16[256,512]{1,0:T(8,128)(2,1)S(1)}, u32[]{:S(2)}, u32[]{:S(2)}) collective-permute-start(bf16[256,512]{1,0:T(8,128)(2,1)S(1)} %slice.99), channel_id=1, source_target_pairs={{0,1},{1,2},{2,3},{3,0},{4,5},{5,6},{6,7},{7,4},{8,9},{9,10},{10,1... | collective-permute-start | bytes 786440 | tf_op jit(solution)/shard_map/ppermute | solution.py:28
  67.7 2.6 %copy-start.3 = (f32[256,352]{0,1:T(8,128)S(1)}, f32[256,352]{0,1:T(8,128)}, u32[]{:S(2)}) copy-start(f32[256,352]{0,1:T(8,128)} %fusion.34) | copy-start | bytes 1081348
  75.0 18.5 %collective-permute-start.6 = (bf16[256,512]{1,0:T(8,128)(2,1)S(1)}, bf16[256,512]{1,0:T(8,128)(2,1)S(1)}, u32[]{:S(2)}, u32[]{:S(2)}) collective-permute-start(bf16[256,512]{1,0:T(8,128)(2,1)S(1)} %convolution_convert_fusion.4), channel_id=1, source_target_pairs={{0,3},{1,0},{2,1},{3,2},{4,7},{5,4},{6,5},{7,6},{8,11},{9,8},{10,9... | collective-permute-start | bytes 786440 | tf_op jit(solution)/shard_map/ppermute | solution.py:12
  83.0 8.3 %collective-permute-start.4 = (bf16[256,512]{1,0:T(8,128)(2,1)S(1)}, bf16[256,512]{1,0:T(8,128)(2,1)S(1)}, u32[]{:S(2)}, u32[]{:S(2)}) collective-permute-start(bf16[256,512]{1,0:T(8,128)(2,1)S(1)} %convolution_convert_fusion.5), channel_id=1, source_target_pairs={{0,1},{1,2},{2,3},{3,0},{4,5},{5,6},{6,7},{7,4},{8,9},{9,10},{10,1... | collective-permute-start | bytes 786440 | tf_op jit(solution)/shard_map/ppermute | solution.py:11
  91.5 11.7 %collective-permute-start.5 = (bf16[512,512]{1,0:T(8,128)(2,1)S(1)}, bf16[512,512]{1,0:T(8,128)(2,1)S(1)}, u32[]{:S(2)}, u32[]{:S(2)}) collective-permute-start(bf16[512,512]{1,0:T(8,128)(2,1)S(1)} %convert_element_type.78), channel_id=1, source_target_pairs={{0,1},{1,2},{2,3},{3,0},{4,5},{5,6},{6,7},{7,4},{8,9},{9,10},{10,1... | collective-permute-start | bytes 1572872 | tf_op jit(solution)/shard_map/ppermute | solution.py:17
  93.7 10.7 %collective-permute-start.7 = (bf16[512,512]{1,0:T(8,128)(2,1)S(1)}, bf16[512,512]{1,0:T(8,128)(2,1)S(1)}, u32[]{:S(2)}, u32[]{:S(2)}) collective-permute-start(bf16[512,512]{1,0:T(8,128)(2,1)S(1)} %convert_element_type.84), channel_id=1, source_target_pairs={{0,3},{1,0},{2,1},{3,2},{4,7},{5,4},{6,5},{7,6},{8,11},{9,8},{10,9... | collective-permute-start | bytes 1572872 | tf_op jit(solution)/shard_map/ppermute | solution.py:18
  104.6 15.8 %copy-start.6 = (f32[128,2]{0,1:T(2,128)S(1)}, f32[128,2]{0,1:T(2,128)}, u32[]{:S(2)}) copy-start(f32[128,2]{0,1:T(2,128)} %param.12) | copy-start | bytes 3076
  105.5 34.3 %all-to-all-start.1 = ((bf16[128,4,512]{2,1,0:T(4,128)(2,1)}), bf16[128,4,512]{2,1,0:T(4,128)(2,1)S(1)}, u32[]{:S(2)}, u32[]{:S(2)}) async-start(bf16[128,4,512]{2,1,0:T(4,128)(2,1)} %reshape.84), calls=%async_computation.1 | async-start | bytes 1048576 | tf_op jit(solution)/shard_map/all_to_all | solution.py:85

commit v8 on v4

--- a/solution.py
+++ b/solution.py
@@ -5,29 +5,21 @@
 
 
 def ring_reduce_scatter(quarter_of, groups, rows):
-    half = rows // 2
     up = [(i, (i + 1) % groups) for i in range(groups)]
     down = [(i, (i - 1) % groups) for i in range(groups)]
-    far_a = lax.ppermute(quarter_of(2, 0, half).astype(jnp.bfloat16), "tp", up)
-    far_b = lax.ppermute(quarter_of(2, half, rows).astype(jnp.bfloat16), "tp", down)
-    next_up = quarter_of(1, 0, rows)
-    next_up = next_up.at[:half].add(far_a.astype(jnp.float32))
-    prev_dn = quarter_of(groups - 1, 0, rows)
-    prev_dn = prev_dn.at[half:].add(far_b.astype(jnp.float32))
+    far = lax.ppermute(quarter_of(2, 0, rows).astype(jnp.bfloat16), "tp", up)
+    next_up = quarter_of(1, 0, rows) + far.astype(jnp.float32)
     from_lo = lax.ppermute(next_up.astype(jnp.bfloat16), "tp", up)
-    from_hi = lax.ppermute(prev_dn.astype(jnp.bfloat16), "tp", down)
+    from_hi = lax.ppermute(quarter_of(groups - 1, 0, rows).astype(jnp.bfloat16), "tp", down)
     return quarter_of(0, 0, rows) + from_lo.astype(jnp.float32) + from_hi.astype(jnp.float32)
 
 
 def ring_all_gather(block, groups, rows):
-    half = rows // 2
     up = [(i, (i + 1) % groups) for i in range(groups)]
     down = [(i, (i - 1) % groups) for i in range(groups)]
     from_lo = lax.ppermute(block, "tp", up)
     from_hi = lax.ppermute(block, "tp", down)
-    far_a = lax.ppermute(from_lo[:half], "tp", up)
-    far_b = lax.ppermute(from_hi[half:], "tp", down)
-    far = jnp.concatenate([far_a, far_b], axis=0)
+    far = lax.ppermute(from_lo, "tp", up)
     return [(0, block), (groups - 1, from_lo), (1, from_hi), (2, far)]
 
 

time: 131 us -> 137 us (1.046)
  waiting for transfers between devices: 34.6 us -> 50.8 us
  starting transfers between devices: 43 us -> 34.9 us
    ppermute x5 -> x3, waiting for transfers between devices: 5.3 us -> 15.9 us  [the longest x1 10.1 us: ring_all_gather(): far = lax.ppermute(from_lo, 'tp', up)]
    ppermute x5 -> x3, starting transfers between devices: 18.1 us -> 8.4 us  [the longest x1 4.57 us: ring_reduce_scatter(): lax.ppermute(quarter_of(groups - 1, 0, rows).astype(jnp.bfloat16), 'tp',...]
    ppermute x1, waiting for transfers between devices: 3.84 us -> 9.54 us  [ring_reduce_scatter(): from_lo = lax.ppermute(next_up.astype(jnp.bfloat16), 'tp', up)]
  transfers between devices with their start and end apart: 9 -> 7, of which waited for: 7 -> 5; matrix products, arithmetic and copies ran while one was open for 3% -> 3% of each run, Pallas kernels for 0% -> 0%
where the time goes in v8:
time: 137 us; the launch traced here: 136 us
  waiting for transfers between devices  50.8 us (37%)
  blocking collectives  37.6 us (27%)
  starting transfers between devices  34.9 us (25%)
  matrix products  8.25 us (6%)
  local copies, waits for them, and re-layouts  2.83 us (2%)
    all_to_all x1, blocking collectives, shards(): lax.all_to_all(outbound.reshape(experts, capacity, quarter), 'ep', split_...  37.6 us
    all_to_all x1, waiting for transfers between devices, shards(): lax.all_to_all(summed.reshape(experts, capacity, quarter), 'ep', split_ax...  19.4 us
    all_to_all x1, starting transfers between devices, shards(): lax.all_to_all(summed.reshape(experts, capacity, quarter), 'ep', split_ax...  17.8 us
    ppermute x1, waiting for transfers between devices, ring_all_gather(): far = lax.ppermute(from_lo, 'tp', up)  10.1 us
    ppermute x1, waiting for transfers between devices, ring_reduce_scatter(): from_lo = lax.ppermute(next_up.astype(jnp.bfloat16), 'tp', up)  9.54 us
    ppermute x1, waiting for transfers between devices, ring_all_gather(): from_lo = lax.ppermute(block, 'tp', up)  5.88 us
    ppermute x1, waiting for transfers between devices, ring_reduce_scatter(): far = lax.ppermute(quarter_of(2, 0, rows).astype(jnp.bfloat16), 'tp', up)  5.82 us
    ppermute x1, starting transfers between devices, ring_reduce_scatter(): lax.ppermute(quarter_of(groups - 1, 0, rows).astype(jnp.bfloat16), 'tp',...  4.57 us
  transfers between devices with their start and end apart: 7, of which 5 were waited for; matrix products, arithmetic and copies ran while one was open for 3% of the time, Pallas kernels for 0%

profile of v8, /device:TPU:1, one launch (start us, length us, event | category | flops | bytes accessed | tf_op | source)
XLA Modules:
  0.0 136.1 jit_solution(11003479734343146311)
XLA Ops:
  0.0 0.0 copy-start
  0.0 0.9 copy.19
  0.9 0.1 eq.98
  1.0 0.1 eq.94
  1.2 0.1 copy.21
  1.3 0.2 fusion.37
  1.6 0.2 fusion.38
  1.8 0.1 sub.7
  1.9 0.1 copy.23
  2.0 0.7 multiply_add_fusion
  2.7 1.2 convolution_convert_fusion.4
  3.9 0.1 reshape.49
  4.1 37.6 %all_to_all.10 = bf16[128,4,512]{2,1,0:T(4,128)(2,1)S(1)} all-to-all(bf16[128,4,512]{2,1,0:T(4,128)(2,1)S(1)} %reshape.49), channel_id=1, replica_groups=mesh['ep'=128,'tp'=4] {'ep'}, dimensions={0} | all-to-all | bytes 1048576 | tf_op jit(solution)/shard_map/all_to_all | solution.py:46
  41.7 0.1 reshape.50
  41.8 3.1 %collective-permute-start = (bf16[512,512]{1,0:T(8,128)(2,1)S(1)}, bf16[512,512]{1,0:T(8,128)(2,1)S(1)}, u32[]{:S(2)}, u32[]{:S(2)}) collective-permute-start(bf16[512,512]{1,0:T(8,128)(2,1)S(1)} %reshape.50), channel_id=1, source_target_pairs={{0,1},{1,2},{2,3},{3,0},{4,5},{5,6},{6,7},{7,4},{8,9},{9,10},{10,1... | collective-permute-start | bytes 1572872 | tf_op jit(solution)/shard_map/ppermute | solution.py:20
  45.0 0.0 copy-start.1
  45.0 0.0 copy-start.2
  45.0 3.6 %collective-permute-start.1 = (bf16[512,512]{1,0:T(8,128)(2,1)S(1)}, bf16[512,512]{1,0:T(8,128)(2,1)S(1)}, u32[]{:S(2)}, u32[]{:S(2)}) collective-permute-start(bf16[512,512]{1,0:T(8,128)(2,1)S(1)} %reshape.50), channel_id=1, source_target_pairs={{0,3},{1,0},{2,1},{3,2},{4,7},{5,4},{6,5},{7,6},{8,11},{9,8},{10,9... | collective-permute-start | bytes 1572872 | tf_op jit(solution)/shard_map/ppermute | solution.py:21
  48.7 1.4 %fusion.13 = f32[512,352]{0,1:T(8,128)S(1)} fusion(bf16[512,512]{1,0:T(8,128)(2,1)S(1)} %reshape.50, bf16[1,2048,352]{1,2,0:T(8,128)(2,1)} %param.10, s32[]{:T(128)S(6)} %select_n.60), kind=kOutput, calls=%fused_computation.24 | convolution fusion | flops 184549376 | bytes 1605636 | tf_op jit(solution)/shard_map/dot_general | solution.py:56
  50.0 0.0 copy-done.1
  50.0 0.4 fusion.18
  50.4 5.9 %collective-permute-done = bf16[512,512]{1,0:T(8,128)(2,1)S(1)} collective-permute-done((bf16[512,512]{1,0:T(8,128)(2,1)S(1)}, bf16[512,512]{1,0:T(8,128)(2,1)S(1)}, u32[]{:S(2)}, u32[]{:S(2)}) %collective-permute-start) | collective-permute-done | bytes 524320 | tf_op jit(solution)/shard_map/ppermute | solution.py:20
  56.3 1.9 %collective-permute-start.2 = (bf16[512,512]{1,0:T(8,128)(2,1)S(1)}, bf16[512,512]{1,0:T(8,128)(2,1)S(1)}, u32[]{:S(2)}, u32[]{:S(2)}) collective-permute-start(bf16[512,512]{1,0:T(8,128)(2,1)S(1)} %collective-permute-done), channel_id=1, source_target_pairs={{0,1},{1,2},{2,3},{3,0},{4,5},{5,6},{6,7},{7,4},{8,9},{9,10},{10,1... | collective-permute-start | bytes 1572872 | tf_op jit(solution)/shard_map/ppermute | solution.py:22
  58.2 0.0 copy-done.2
  58.2 0.4 convolution_add_fusion.2
  58.6 0.4 convolution_add_fusion.5
  59.0 0.0 collective-permute-done.1
  59.0 0.4 convolution_add_fusion.1
  59.4 0.4 convolution_add_fusion.4
  59.8 10.1 %collective-permute-done.2 = bf16[512,512]{1,0:T(8,128)(2,1)S(1)} collective-permute-done((bf16[512,512]{1,0:T(8,128)(2,1)S(1)}, bf16[512,512]{1,0:T(8,128)(2,1)S(1)}, u32[]{:S(2)}, u32[]{:S(2)}) %collective-permute-start.2) | collective-permute-done | bytes 524320 | tf_op jit(solution)/shard_map/ppermute | solution.py:22
  70.0 0.4 convolution_add_fusion.3
  70.3 0.4 multiply_convert_fusion
  70.8 0.0 copy-done
  70.8 0.5 convolution_convert_fusion.1
  71.3 1.9 %collective-permute-start.3 = (bf16[512,512]{1,0:T(8,128)(2,1)S(1)}, bf16[512,512]{1,0:T(8,128)(2,1)S(1)}, u32[]{:S(2)}, u32[]{:S(2)}) collective-permute-start(bf16[512,512]{1,0:T(8,128)(2,1)S(1)} %convolution_convert_fusion.1), channel_id=1, source_target_pairs={{0,1},{1,2},{2,3},{3,0},{4,5},{5,6},{6,7},{7,4},{8,9},{9,10},{10,1... | collective-permute-start | bytes 1572872 | tf_op jit(solution)/shard_map/ppermute | solution.py:10
  73.2 0.5 convolution_convert_fusion
  73.7 4.6 %collective-permute-start.5 = (bf16[512,512]{1,0:T(8,128)(2,1)S(1)}, bf16[512,512]{1,0:T(8,128)(2,1)S(1)}, u32[]{:S(2)}, u32[]{:S(2)}) collective-permute-start(bf16[512,512]{1,0:T(8,128)(2,1)S(1)} %convolution_convert_fusion), channel_id=1, source_target_pairs={{0,3},{1,0},{2,1},{3,2},{4,7},{5,4},{6,5},{7,6},{8,11},{9,8},{10,9... | collective-permute-start | bytes 1572872 | tf_op jit(solution)/shard_map/ppermute | solution.py:13
  78.2 5.8 %collective-permute-done.3 = bf16[512,512]{1,0:T(8,128)(2,1)S(1)} collective-permute-done((bf16[512,512]{1,0:T(8,128)(2,1)S(1)}, bf16[512,512]{1,0:T(8,128)(2,1)S(1)}, u32[]{:S(2)}, u32[]{:S(2)}) %collective-permute-start.3) | collective-permute-done | bytes 524320 | tf_op jit(solution)/shard_map/ppermute | solution.py:10
  84.1 0.5 add_convert_fusion.1
  84.5 1.9 %collective-permute-start.4 = (bf16[512,512]{1,0:T(8,128)(2,1)S(1)}, bf16[512,512]{1,0:T(8,128)(2,1)S(1)}, u32[]{:S(2)}, u32[]{:S(2)}) collective-permute-start(bf16[512,512]{1,0:T(8,128)(2,1)S(1)} %add_convert_fusion.1), channel_id=1, source_target_pairs={{0,1},{1,2},{2,3},{3,0},{4,5},{5,6},{6,7},{7,4},{8,9},{9,10},{10,1... | collective-permute-start | bytes 1572872 | tf_op jit(solution)/shard_map/ppermute | solution.py:12
  86.5 0.5 fusion
  86.9 0.0 collective-permute-done.5
  86.9 9.5 %collective-permute-done.4 = bf16[512,512]{1,0:T(8,128)(2,1)S(1)} collective-permute-done((bf16[512,512]{1,0:T(8,128)(2,1)S(1)}, bf16[512,512]{1,0:T(8,128)(2,1)S(1)}, u32[]{:S(2)}, u32[]{:S(2)}) %collective-permute-start.4) | collective-permute-done | bytes 524320 | tf_op jit(solution)/shard_map/ppermute | solution.py:12
  96.5 0.2 add_convert_fusion
  96.7 0.0 copy-start.3
  96.7 0.9 reshape.51
  97.6 17.8 %all-to-all-start.1 = ((bf16[128,4,512]{2,1,0:T(4,128)(2,1)}), bf16[128,4,512]{2,1,0:T(4,128)(2,1)S(1)}, u32[]{:S(2)}, u32[]{:S(2)}) async-start(bf16[128,4,512]{2,1,0:T(4,128)(2,1)} %reshape.51), calls=%async_computation.1 | async-start | bytes 1048576 | tf_op jit(solution)/shard_map/all_to_all | solution.py:71
  115.4 0.0 copy-done.3
  115.5 19.4 %all-to-all-done.1 = bf16[128,4,512]{2,1,0:T(4,128)(2,1)S(1)} async-done(((bf16[128,4,512]{2,1,0:T(4,128)(2,1)}), bf16[128,4,512]{2,1,0:T(4,128)(2,1)S(1)}, u32[]{:S(2)}, u32[]{:S(2)}) %all-to-all-start.1) | async-done | bytes 524320 | tf_op jit(solution)/shard_map/all_to_all | solution.py:71
  134.9 0.1 reshape.52
  135.0 1.1 convolution_convert_fusion.5
  (9 shorter events, 0.1 us)
Async XLA Ops:
  0.0 70.8 %copy-start = (bf16[1,352,2048]{2,1,0:T(8,128)(2,1)S(1)}, bf16[1,352,2048]{2,1,0:T(8,128)(2,1)}, u32[]{:S(2)}) copy-start(bf16[1,352,2048]{2,1,0:T(8,128)(2,1)} %param.11) | copy-start | bytes 4325380
  41.8 14.5 %collective-permute-start = (bf16[512,512]{1,0:T(8,128)(2,1)S(1)}, bf16[512,512]{1,0:T(8,128)(2,1)S(1)}, u32[]{:S(2)}, u32[]{:S(2)}) collective-permute-start(bf16[512,512]{1,0:T(8,128)(2,1)S(1)} %reshape.50), channel_id=1, source_target_pairs={{0,1},{1,2},{2,3},{3,0},{4,5},{5,6},{6,7},{7,4},{8,9},{9,10},{10,1... | collective-permute-start | bytes 1572872 | tf_op jit(solution)/shard_map/ppermute | solution.py:20
  45.0 5.0 %copy-start.1 = (bf16[1,2048,352]{1,2,0:T(8,128)(2,1)S(1)}, bf16[1,2048,352]{1,2,0:T(8,128)(2,1)}, u32[]{:S(2)}) copy-start(bf16[1,2048,352]{1,2,0:T(8,128)(2,1)} %param.9) | copy-start | bytes 4325380
  45.0 13.2 %copy-start.2 = (bf16[1,2048,352]{1,2,0:T(8,128)(2,1)S(1)}, bf16[1,2048,352]{1,2,0:T(8,128)(2,1)}, u32[]{:S(2)}) copy-start(bf16[1,2048,352]{1,2,0:T(8,128)(2,1)} %param.10) | copy-start | bytes 4325380
  45.0 14.0 %collective-permute-start.1 = (bf16[512,512]{1,0:T(8,128)(2,1)S(1)}, bf16[512,512]{1,0:T(8,128)(2,1)S(1)}, u32[]{:S(2)}, u32[]{:S(2)}) collective-permute-start(bf16[512,512]{1,0:T(8,128)(2,1)S(1)} %reshape.50), channel_id=1, source_target_pairs={{0,3},{1,0},{2,1},{3,2},{4,7},{5,4},{6,5},{7,6},{8,11},{9,8},{10,9... | collective-permute-start | bytes 1572872 | tf_op jit(solution)/shard_map/ppermute | solution.py:21
  56.3 13.6 %collective-permute-start.2 = (bf16[512,512]{1,0:T(8,128)(2,1)S(1)}, bf16[512,512]{1,0:T(8,128)(2,1)S(1)}, u32[]{:S(2)}, u32[]{:S(2)}) collective-permute-start(bf16[512,512]{1,0:T(8,128)(2,1)S(1)} %collective-permute-done), channel_id=1, source_target_pairs={{0,1},{1,2},{2,3},{3,0},{4,5},{5,6},{6,7},{7,4},{8,9},{9,10},{10,1... | collective-permute-start | bytes 1572872 | tf_op jit(solution)/shard_map/ppermute | solution.py:22
  71.3 12.8 %collective-permute-start.3 = (bf16[512,512]{1,0:T(8,128)(2,1)S(1)}, bf16[512,512]{1,0:T(8,128)(2,1)S(1)}, u32[]{:S(2)}, u32[]{:S(2)}) collective-permute-start(bf16[512,512]{1,0:T(8,128)(2,1)S(1)} %convolution_convert_fusion.1), channel_id=1, source_target_pairs={{0,1},{1,2},{2,3},{3,0},{4,5},{5,6},{6,7},{7,4},{8,9},{9,10},{10,1... | collective-permute-start | bytes 1572872 | tf_op jit(solution)/shard_map/ppermute | solution.py:10
  73.7 13.3 %collective-permute-start.5 = (bf16[512,512]{1,0:T(8,128)(2,1)S(1)}, bf16[512,512]{1,0:T(8,128)(2,1)S(1)}, u32[]{:S(2)}, u32[]{:S(2)}) collective-permute-start(bf16[512,512]{1,0:T(8,128)(2,1)S(1)} %convolution_convert_fusion), channel_id=1, source_target_pairs={{0,3},{1,0},{2,1},{3,2},{4,7},{5,4},{6,5},{7,6},{8,11},{9,8},{10,9... | collective-permute-start | bytes 1572872 | tf_op jit(solution)/shard_map/ppermute | solution.py:13
  84.5 11.9 %collective-permute-start.4 = (bf16[512,512]{1,0:T(8,128)(2,1)S(1)}, bf16[512,512]{1,0:T(8,128)(2,1)S(1)}, u32[]{:S(2)}, u32[]{:S(2)}) collective-permute-start(bf16[512,512]{1,0:T(8,128)(2,1)S(1)} %add_convert_fusion.1), channel_id=1, source_target_pairs={{0,1},{1,2},{2,3},{3,0},{4,5},{5,6},{6,7},{7,4},{8,9},{9,10},{10,1... | collective-permute-start | bytes 1572872 | tf_op jit(solution)/shard_map/ppermute | solution.py:12
  96.7 18.8 %copy-start.3 = (f32[128,2]{0,1:T(2,128)S(1)}, f32[128,2]{0,1:T(2,128)}, u32[]{:S(2)}) copy-start(f32[128,2]{0,1:T(2,128)} %param.8) | copy-start | bytes 3076
  97.6 37.3 %all-to-all-start.1 = ((bf16[128,4,512]{2,1,0:T(4,128)(2,1)}), bf16[128,4,512]{2,1,0:T(4,128)(2,1)S(1)}, u32[]{:S(2)}, u32[]{:S(2)}) async-start(bf16[128,4,512]{2,1,0:T(4,128)(2,1)} %reshape.51), calls=%async_computation.1 | async-start | bytes 1048576 | tf_op jit(solution)/shard_map/all_to_all | solution.py:71

commit v9 on v4

--- a/solution.py
+++ b/solution.py
@@ -79,14 +79,13 @@
     returned = lax.all_to_all(
         summed.reshape(experts, capacity, quarter), "ep", split_axis=0, concat_axis=0, tiled=True
     )
-    returned = returned.reshape(row_count, quarter).astype(jnp.float32)
-    combine_w = gate_values[:, 0][:, None] * (target[:, 0][:, None] == slot_iota[None, :]).astype(
-        jnp.float32
-    )
-    combine_w = combine_w + gate_values[:, 1][:, None] * (
-        target[:, 1][:, None] == slot_iota[None, :]
-    ).astype(jnp.float32)
-    mixed = jnp.dot(combine_w, returned, precision=lax.Precision.HIGHEST)
+    returned = returned.reshape(row_count, quarter)
+    mixed = None
+    for k in range(2):
+        pick = (target[:, k][:, None] == slot_iota[None, :]).astype(jnp.bfloat16)
+        chosen = jnp.dot(pick, returned, preferred_element_type=jnp.float32)
+        term = gate_values[:, k][:, None] * chosen
+        mixed = term if mixed is None else mixed + term
     return mixed.astype(jnp.bfloat16)
 
 

time: 131 us -> 131 us (level)
  no operation moved by 1% of the time
where the time goes in v9:
time: 131 us; the launch traced here: 129 us
  starting transfers between devices  43 us (33%)
  blocking collectives  37.6 us (29%)
  waiting for transfers between devices  34.6 us (26%)
  matrix products  8.69 us (7%)
  local copies, waits for them, and re-layouts  2.9 us (2%)
  other arithmetic  1.74 us (1%)
    all_to_all x1, blocking collectives, shards(): lax.all_to_all(outbound.reshape(experts, capacity, quarter), 'ep', split_...  37.6 us
    all_to_all x1, waiting for transfers between devices, shards(): lax.all_to_all(summed.reshape(experts, capacity, quarter), 'ep', split_ax...  19.4 us
    all_to_all x1, starting transfers between devices, shards(): lax.all_to_all(summed.reshape(experts, capacity, quarter), 'ep', split_ax...  16.5 us
    ppermute x1, waiting for transfers between devices, ring_all_gather(): from_lo = lax.ppermute(block, 'tp', up)  6.02 us
    ppermute x1, starting transfers between devices, ring_reduce_scatter(): from_hi = lax.ppermute(prev_dn.astype(jnp.bfloat16), 'tp', down)  4.68 us
    ppermute x1, starting transfers between devices, ring_all_gather(): far_b = lax.ppermute(from_hi[half:], 'tp', down)  4.57 us
    ppermute x1, starting transfers between devices, ring_reduce_scatter(): lax.ppermute(quarter_of(2, half, rows).astype(jnp.bfloat16), 'tp', down)  4.29 us
    dot_general x8, matrix products, project(): term = jnp.dot(piece, rows, preferred_element_type=jnp.float32)  4.26 us
  transfers between devices with their start and end apart: 9, of which 7 were waited for; matrix products, arithmetic and copies ran while one was open for 3% of the time, Pallas kernels for 0%

profile of v9, /device:TPU:1, one launch (start us, length us, event | category | flops | bytes accessed | tf_op | source)
XLA Modules:
  0.0 129.0 jit_solution(14094490646033331974)
XLA Ops:
  0.0 0.0 copy-start
  0.0 0.9 copy.19
  0.9 0.1 eq.99
  1.0 0.1 eq.95
  1.2 0.1 copy.21
  1.3 0.2 fusion.45
  1.6 0.2 fusion.46
  1.8 0.1 sub.7
  1.9 0.1 copy.23
  2.0 0.7 multiply_add_fusion
  2.7 1.2 convolution_convert_fusion.3
  3.9 0.1 reshape.98
  4.0 37.6 %all_to_all.10 = bf16[128,4,512]{2,1,0:T(4,128)(2,1)S(1)} all-to-all(bf16[128,4,512]{2,1,0:T(4,128)(2,1)S(1)} %reshape.98), channel_id=1, replica_groups=mesh['ep'=128,'tp'=4] {'ep'}, dimensions={0} | all-to-all | bytes 1048576 | tf_op jit(solution)/shard_map/all_to_all | solution.py:54
  41.7 0.1 reshape.99
  41.8 3.1 %collective-permute-start = (bf16[512,512]{1,0:T(8,128)(2,1)S(1)}, bf16[512,512]{1,0:T(8,128)(2,1)S(1)}, u32[]{:S(2)}, u32[]{:S(2)}) collective-permute-start(bf16[512,512]{1,0:T(8,128)(2,1)S(1)} %reshape.99), channel_id=1, source_target_pairs={{0,1},{1,2},{2,3},{3,0},{4,5},{5,6},{6,7},{7,4},{8,9},{9,10},{10,1... | collective-permute-start | bytes 1572872 | tf_op jit(solution)/shard_map/ppermute | solution.py:26
  44.9 3.4 %collective-permute-start.1 = (bf16[512,512]{1,0:T(8,128)(2,1)S(1)}, bf16[512,512]{1,0:T(8,128)(2,1)S(1)}, u32[]{:S(2)}, u32[]{:S(2)}) collective-permute-start(bf16[512,512]{1,0:T(8,128)(2,1)S(1)} %reshape.99), channel_id=1, source_target_pairs={{0,3},{1,0},{2,1},{3,2},{4,7},{5,4},{6,5},{7,6},{8,11},{9,8},{10,9... | collective-permute-start | bytes 1572872 | tf_op jit(solution)/shard_map/ppermute | solution.py:27
  48.4 0.0 copy-start.2
  48.4 1.5 %fusion.26 = f32[512,352]{0,1:T(8,128)S(1)} fusion(bf16[512,512]{1,0:T(8,128)(2,1)S(1)} %reshape.99, bf16[1,2048,352]{1,2,0:T(8,128)(2,1)} %param.13, s32[]{:T(128)S(6)} %select_n.63), kind=kOutput, calls=%fused_computation.40 | convolution fusion | flops 184549376 | bytes 1605636 | tf_op jit(solution)/shard_map/dot_general | solution.py:64
  49.9 0.0 copy-done.2
  49.9 0.0 copy-start.1
  49.9 0.4 fusion.20
  50.3 6.0 %collective-permute-done = bf16[512,512]{1,0:T(8,128)(2,1)S(1)} collective-permute-done((bf16[512,512]{1,0:T(8,128)(2,1)S(1)}, bf16[512,512]{1,0:T(8,128)(2,1)S(1)}, u32[]{:S(2)}, u32[]{:S(2)}) %collective-permute-start) | collective-permute-done | bytes 524320 | tf_op jit(solution)/shard_map/ppermute | solution.py:26
  56.3 1.9 %collective-permute-start.2 = (bf16[256,512]{1,0:T(8,128)(2,1)S(1)}, bf16[256,512]{1,0:T(8,128)(2,1)S(1)}, u32[]{:S(2)}, u32[]{:S(2)}) collective-permute-start(bf16[256,512]{1,0:T(8,128)(2,1)S(1)} %slice.83), channel_id=1, source_target_pairs={{0,1},{1,2},{2,3},{3,0},{4,5},{5,6},{6,7},{7,4},{8,9},{9,10},{10,1... | collective-permute-start | bytes 786440 | tf_op jit(solution)/shard_map/ppermute | solution.py:28
  58.3 0.0 collective-permute-done.1
  58.3 4.6 %collective-permute-start.3 = (bf16[256,512]{1,0:T(8,128)(2,1)S(1)}, bf16[256,512]{1,0:T(8,128)(2,1)S(1)}, u32[]{:S(2)}, u32[]{:S(2)}) collective-permute-start(bf16[256,512]{1,0:T(8,128)(2,1)S(1)} %slice.84), channel_id=1, source_target_pairs={{0,3},{1,0},{2,1},{3,2},{4,7},{5,4},{6,5},{7,6},{8,11},{9,8},{10,9... | collective-permute-start | bytes 786440 | tf_op jit(solution)/shard_map/ppermute | solution.py:29
  62.9 0.0 copy-done.1
  62.9 0.4 convolution_add_fusion.3
  63.3 0.4 convolution_add_fusion.1
  63.7 1.0 collective-permute-done.2
  64.7 1.5 %collective-permute-done.3 = bf16[256,512]{1,0:T(8,128)(2,1)S(1)} collective-permute-done((bf16[256,512]{1,0:T(8,128)(2,1)S(1)}, bf16[256,512]{1,0:T(8,128)(2,1)S(1)}, u32[]{:S(2)}, u32[]{:S(2)}) %collective-permute-start.3) | collective-permute-done | bytes 262176 | tf_op jit(solution)/shard_map/ppermute | solution.py:29
  66.2 0.4 fusion.22
  66.6 0.4 fusion.14
  67.0 0.4 fusion.3
  67.4 0.5 multiply_convert_fusion
  67.8 0.0 copy-done
  67.9 0.5 fusion.1
  68.3 0.3 convolution_convert_fusion.5
  68.7 2.6 %collective-permute-start.4 = (bf16[256,512]{1,0:T(8,128)(2,1)S(1)}, bf16[256,512]{1,0:T(8,128)(2,1)S(1)}, u32[]{:S(2)}, u32[]{:S(2)}) collective-permute-start(bf16[256,512]{1,0:T(8,128)(2,1)S(1)} %convolution_convert_fusion.5), channel_id=1, source_target_pairs={{0,1},{1,2},{2,3},{3,0},{4,5},{5,6},{6,7},{7,4},{8,9},{9,10},{10,1... | collective-permute-start | bytes 786440 | tf_op jit(solution)/shard_map/ppermute | solution.py:11
  71.3 0.3 convolution_convert_fusion.4
  71.6 4.3 %collective-permute-start.6 = (bf16[256,512]{1,0:T(8,128)(2,1)S(1)}, bf16[256,512]{1,0:T(8,128)(2,1)S(1)}, u32[]{:S(2)}, u32[]{:S(2)}) collective-permute-start(bf16[256,512]{1,0:T(8,128)(2,1)S(1)} %convolution_convert_fusion.4), channel_id=1, source_target_pairs={{0,3},{1,0},{2,1},{3,2},{4,7},{5,4},{6,5},{7,6},{8,11},{9,8},{10,9... | collective-permute-start | bytes 786440 | tf_op jit(solution)/shard_map/ppermute | solution.py:12
  75.9 0.5 fusion.2
  76.4 1.0 collective-permute-done.4
  77.4 0.1 fusion.8
  77.6 0.1 convert_element_type.75
  77.6 1.9 %collective-permute-start.5 = (bf16[512,512]{1,0:T(8,128)(2,1)S(1)}, bf16[512,512]{1,0:T(8,128)(2,1)S(1)}, u32[]{:S(2)}, u32[]{:S(2)}) collective-permute-start(bf16[512,512]{1,0:T(8,128)(2,1)S(1)} %convert_element_type.75), channel_id=1, source_target_pairs={{0,1},{1,2},{2,3},{3,0},{4,5},{5,6},{6,7},{7,4},{8,9},{9,10},{10,1... | collective-permute-start | bytes 1572872 | tf_op jit(solution)/shard_map/ppermute | solution.py:17
  79.6 0.0 collective-permute-done.6
  79.6 0.1 fusion.7
  79.7 0.1 convert_element_type.81
  79.8 4.7 %collective-permute-start.7 = (bf16[512,512]{1,0:T(8,128)(2,1)S(1)}, bf16[512,512]{1,0:T(8,128)(2,1)S(1)}, u32[]{:S(2)}, u32[]{:S(2)}) collective-permute-start(bf16[512,512]{1,0:T(8,128)(2,1)S(1)} %convert_element_type.81), channel_id=1, source_target_pairs={{0,3},{1,0},{2,1},{3,2},{4,7},{5,4},{6,5},{7,6},{8,11},{9,8},{10,9... | collective-permute-start | bytes 1572872 | tf_op jit(solution)/shard_map/ppermute | solution.py:18
  84.5 0.5 fusion
  84.9 3.8 %collective-permute-done.5 = bf16[512,512]{1,0:T(8,128)(2,1)S(1)} collective-permute-done((bf16[512,512]{1,0:T(8,128)(2,1)S(1)}, bf16[512,512]{1,0:T(8,128)(2,1)S(1)}, u32[]{:S(2)}, u32[]{:S(2)}) %collective-permute-start.5) | collective-permute-done | bytes 524320 | tf_op jit(solution)/shard_map/ppermute | solution.py:17
  88.8 1.8 %collective-permute-done.7 = bf16[512,512]{1,0:T(8,128)(2,1)S(1)} collective-permute-done((bf16[512,512]{1,0:T(8,128)(2,1)S(1)}, bf16[512,512]{1,0:T(8,128)(2,1)S(1)}, u32[]{:S(2)}, u32[]{:S(2)}) %collective-permute-start.7) | collective-permute-done | bytes 524320 | tf_op jit(solution)/shard_map/ppermute | solution.py:18
  90.6 0.2 add_convert_fusion
  90.8 0.0 copy-start.3
  90.8 0.9 reshape.100
  91.7 16.5 %all-to-all-start.1 = ((bf16[128,4,512]{2,1,0:T(4,128)(2,1)}), bf16[128,4,512]{2,1,0:T(4,128)(2,1)S(1)}, u32[]{:S(2)}, u32[]{:S(2)}) async-start(bf16[128,4,512]{2,1,0:T(4,128)(2,1)} %reshape.100), calls=%async_computation.1 | async-start | bytes 1048576 | tf_op jit(solution)/shard_map/all_to_all | solution.py:79
  108.2 0.0 copy-done.3
  108.2 19.4 %all-to-all-done.1 = bf16[128,4,512]{2,1,0:T(4,128)(2,1)S(1)} async-done(((bf16[128,4,512]{2,1,0:T(4,128)(2,1)}), bf16[128,4,512]{2,1,0:T(4,128)(2,1)S(1)}, u32[]{:S(2)}, u32[]{:S(2)}) %all-to-all-start.1) | async-done | bytes 524320 | tf_op jit(solution)/shard_map/all_to_all | solution.py:79
  127.6 0.1 reshape.101
  127.8 0.3 convolution_multiply_fusion.1
  128.0 0.9 fusion.6
  (13 shorter events, 0.2 us)
Async XLA Ops:
  0.0 67.9 %copy-start = (bf16[1,352,2048]{2,1,0:T(8,128)(2,1)S(1)}, bf16[1,352,2048]{2,1,0:T(8,128)(2,1)}, u32[]{:S(2)}) copy-start(bf16[1,352,2048]{2,1,0:T(8,128)(2,1)} %param.15) | copy-start | bytes 4325380
  41.8 14.5 %collective-permute-start = (bf16[512,512]{1,0:T(8,128)(2,1)S(1)}, bf16[512,512]{1,0:T(8,128)(2,1)S(1)}, u32[]{:S(2)}, u32[]{:S(2)}) collective-permute-start(bf16[512,512]{1,0:T(8,128)(2,1)S(1)} %reshape.99), channel_id=1, source_target_pairs={{0,1},{1,2},{2,3},{3,0},{4,5},{5,6},{6,7},{7,4},{8,9},{9,10},{10,1... | collective-permute-start | bytes 1572872 | tf_op jit(solution)/shard_map/ppermute | solution.py:26
  44.9 13.3 %collective-permute-start.1 = (bf16[512,512]{1,0:T(8,128)(2,1)S(1)}, bf16[512,512]{1,0:T(8,128)(2,1)S(1)}, u32[]{:S(2)}, u32[]{:S(2)}) collective-permute-start(bf16[512,512]{1,0:T(8,128)(2,1)S(1)} %reshape.99), channel_id=1, source_target_pairs={{0,3},{1,0},{2,1},{3,2},{4,7},{5,4},{6,5},{7,6},{8,11},{9,8},{10,9... | collective-permute-start | bytes 1572872 | tf_op jit(solution)/shard_map/ppermute | solution.py:27
  48.4 1.5 %copy-start.2 = (bf16[1,2048,352]{1,2,0:T(8,128)(2,1)S(1)}, bf16[1,2048,352]{1,2,0:T(8,128)(2,1)}, u32[]{:S(2)}) copy-start(bf16[1,2048,352]{1,2,0:T(8,128)(2,1)} %param.14) | copy-start | bytes 4325380
  49.9 13.0 %copy-start.1 = (bf16[1,2048,352]{1,2,0:T(8,128)(2,1)S(1)}, bf16[1,2048,352]{1,2,0:T(8,128)(2,1)}, u32[]{:S(2)}) copy-start(bf16[1,2048,352]{1,2,0:T(8,128)(2,1)} %param.13) | copy-start | bytes 4325380
  56.3 8.3 %collective-permute-start.2 = (bf16[256,512]{1,0:T(8,128)(2,1)S(1)}, bf16[256,512]{1,0:T(8,128)(2,1)S(1)}, u32[]{:S(2)}, u32[]{:S(2)}) collective-permute-start(bf16[256,512]{1,0:T(8,128)(2,1)S(1)} %slice.83), channel_id=1, source_target_pairs={{0,1},{1,2},{2,3},{3,0},{4,5},{5,6},{6,7},{7,4},{8,9},{9,10},{10,1... | collective-permute-start | bytes 786440 | tf_op jit(solution)/shard_map/ppermute | solution.py:28
  58.3 7.9 %collective-permute-start.3 = (bf16[256,512]{1,0:T(8,128)(2,1)S(1)}, bf16[256,512]{1,0:T(8,128)(2,1)S(1)}, u32[]{:S(2)}, u32[]{:S(2)}) collective-permute-start(bf16[256,512]{1,0:T(8,128)(2,1)S(1)} %slice.84), channel_id=1, source_target_pairs={{0,3},{1,0},{2,1},{3,2},{4,7},{5,4},{6,5},{7,6},{8,11},{9,8},{10,9... | collective-permute-start | bytes 786440 | tf_op jit(solution)/shard_map/ppermute | solution.py:29
  68.7 8.8 %collective-permute-start.4 = (bf16[256,512]{1,0:T(8,128)(2,1)S(1)}, bf16[256,512]{1,0:T(8,128)(2,1)S(1)}, u32[]{:S(2)}, u32[]{:S(2)}) collective-permute-start(bf16[256,512]{1,0:T(8,128)(2,1)S(1)} %convolution_convert_fusion.5), channel_id=1, source_target_pairs={{0,1},{1,2},{2,3},{3,0},{4,5},{5,6},{6,7},{7,4},{8,9},{9,10},{10,1... | collective-permute-start | bytes 786440 | tf_op jit(solution)/shard_map/ppermute | solution.py:11
  71.6 7.9 %collective-permute-start.6 = (bf16[256,512]{1,0:T(8,128)(2,1)S(1)}, bf16[256,512]{1,0:T(8,128)(2,1)S(1)}, u32[]{:S(2)}, u32[]{:S(2)}) collective-permute-start(bf16[256,512]{1,0:T(8,128)(2,1)S(1)} %convolution_convert_fusion.4), channel_id=1, source_target_pairs={{0,3},{1,0},{2,1},{3,2},{4,7},{5,4},{6,5},{7,6},{8,11},{9,8},{10,9... | collective-permute-start | bytes 786440 | tf_op jit(solution)/shard_map/ppermute | solution.py:12
  77.6 11.1 %collective-permute-start.5 = (bf16[512,512]{1,0:T(8,128)(2,1)S(1)}, bf16[512,512]{1,0:T(8,128)(2,1)S(1)}, u32[]{:S(2)}, u32[]{:S(2)}) collective-permute-start(bf16[512,512]{1,0:T(8,128)(2,1)S(1)} %convert_element_type.75), channel_id=1, source_target_pairs={{0,1},{1,2},{2,3},{3,0},{4,5},{5,6},{6,7},{7,4},{8,9},{9,10},{10,1... | collective-permute-start | bytes 1572872 | tf_op jit(solution)/shard_map/ppermute | solution.py:17
  79.8 10.8 %collective-permute-start.7 = (bf16[512,512]{1,0:T(8,128)(2,1)S(1)}, bf16[512,512]{1,0:T(8,128)(2,1)S(1)}, u32[]{:S(2)}, u32[]{:S(2)}) collective-permute-start(bf16[512,512]{1,0:T(8,128)(2,1)S(1)} %convert_element_type.81), channel_id=1, source_target_pairs={{0,3},{1,0},{2,1},{3,2},{4,7},{5,4},{6,5},{7,6},{8,11},{9,8},{10,9... | collective-permute-start | bytes 1572872 | tf_op jit(solution)/shard_map/ppermute | solution.py:18
  90.8 17.4 %copy-start.3 = (f32[128,2]{0,1:T(2,128)S(1)}, f32[128,2]{0,1:T(2,128)}, u32[]{:S(2)}) copy-start(f32[128,2]{0,1:T(2,128)} %param.12) | copy-start | bytes 3076
  91.7 35.9 %all-to-all-start.1 = ((bf16[128,4,512]{2,1,0:T(4,128)(2,1)}), bf16[128,4,512]{2,1,0:T(4,128)(2,1)S(1)}, u32[]{:S(2)}, u32[]{:S(2)}) async-start(bf16[128,4,512]{2,1,0:T(4,128)(2,1)} %reshape.100), calls=%async_computation.1 | async-start | bytes 1048576 | tf_op jit(solution)/shard_map/all_to_all | solution.py:79

commit v10 on v9

--- a/solution.py
+++ b/solution.py
@@ -39,11 +39,18 @@
     quarter = width // groups
     capacity = 4 * tok_rows // experts
     row_count = experts * capacity
-    flat_ids = expert_ids.reshape(-1)
-    onehot = (flat_ids[:, None] == jnp.arange(experts, dtype=jnp.int32)[None, :]).astype(jnp.int32)
-    running = jnp.cumsum(onehot, axis=0)
-    position = jnp.sum(running * onehot, axis=1) - 1
-    target = (flat_ids * capacity + position).reshape(tok_rows, 2)
+    row_iota = jnp.arange(tok_rows, dtype=jnp.int32)
+    earlier = (row_iota[None, :] < row_iota[:, None]).astype(jnp.int32)
+    first, second = expert_ids[:, 0], expert_ids[:, 1]
+    same_row = (first == second).astype(jnp.int32)
+    targets = []
+    for k, ids in enumerate((first, second)):
+        hits = (ids[:, None] == first[None, :]).astype(jnp.int32) + (
+            ids[:, None] == second[None, :]
+        ).astype(jnp.int32)
+        position = jnp.sum(hits * earlier, axis=1) + (same_row if k == 1 else 0)
+        targets.append(ids * capacity + position)
+    target = jnp.stack(targets, axis=1)
     slot_iota = jnp.arange(row_count, dtype=jnp.int32)
     first_hit = target[:, 0][None, :] == slot_iota[:, None]
     second_hit = target[:, 1][None, :] == slot_iota[:, None]

time: 131 us -> 130 us (level)
  no operation moved by 1% of the time
where the time goes in v10:
time: 130 us; the launch traced here: 128 us
  starting transfers between devices  43 us (33%)
  blocking collectives  37.6 us (29%)
  waiting for transfers between devices  34.5 us (27%)
  matrix products  8.68 us (7%)
  local copies, waits for them, and re-layouts  2.2 us (2%)
  other arithmetic  1.55 us (1%)
    all_to_all x1, blocking collectives, shards(): lax.all_to_all(outbound.reshape(experts, capacity, quarter), 'ep', split_...  37.6 us
    all_to_all x1, waiting for transfers between devices, shards(): lax.all_to_all(summed.reshape(experts, capacity, quarter), 'ep', split_ax...  19.4 us
    all_to_all x1, starting transfers between devices, shards(): lax.all_to_all(summed.reshape(experts, capacity, quarter), 'ep', split_ax...  16.5 us
    ppermute x1, waiting for transfers between devices, ring_all_gather(): from_lo = lax.ppermute(block, 'tp', up)  6.03 us
    ppermute x1, starting transfers between devices, ring_reduce_scatter(): from_hi = lax.ppermute(prev_dn.astype(jnp.bfloat16), 'tp', down)  4.68 us
    ppermute x1, starting transfers between devices, ring_all_gather(): far_b = lax.ppermute(from_hi[half:], 'tp', down)  4.57 us
    ppermute x1, starting transfers between devices, ring_reduce_scatter(): lax.ppermute(quarter_of(2, half, rows).astype(jnp.bfloat16), 'tp', down)  4.31 us
    dot_general x8, matrix products, project(): term = jnp.dot(piece, rows, preferred_element_type=jnp.float32)  4.25 us
  transfers between devices with their start and end apart: 9, of which 7 were waited for; matrix products, arithmetic and copies ran while one was open for 3% of the time, Pallas kernels for 0%

profile of v10, /device:TPU:1, one launch (start us, length us, event | category | flops | bytes accessed | tf_op | source)
XLA Modules:
  0.0 128.0 jit_solution(13802892865029327228)
XLA Ops:
  0.0 0.0 copy-start
  0.0 0.8 slice_bitcast_fusion.3
  0.8 0.2 select_reduce_fusion.1
  1.0 0.8 multiply_add_fusion
  1.8 1.2 convolution_convert_fusion.3
  3.0 0.1 reshape.103
  3.1 37.6 %all_to_all.10 = bf16[128,4,512]{2,1,0:T(4,128)(2,1)S(1)} all-to-all(bf16[128,4,512]{2,1,0:T(4,128)(2,1)S(1)} %reshape.103), channel_id=1, replica_groups=mesh['ep'=128,'tp'=4] {'ep'}, dimensions={0} | all-to-all | bytes 1048576 | tf_op jit(solution)/shard_map/all_to_all | solution.py:61
  40.7 0.1 reshape.104
  40.9 3.1 %collective-permute-start = (bf16[512,512]{1,0:T(8,128)(2,1)S(1)}, bf16[512,512]{1,0:T(8,128)(2,1)S(1)}, u32[]{:S(2)}, u32[]{:S(2)}) collective-permute-start(bf16[512,512]{1,0:T(8,128)(2,1)S(1)} %reshape.104), channel_id=1, source_target_pairs={{0,1},{1,2},{2,3},{3,0},{4,5},{5,6},{6,7},{7,4},{8,9},{9,10},{10,1... | collective-permute-start | bytes 1572872 | tf_op jit(solution)/shard_map/ppermute | solution.py:26
  44.0 3.4 %collective-permute-start.1 = (bf16[512,512]{1,0:T(8,128)(2,1)S(1)}, bf16[512,512]{1,0:T(8,128)(2,1)S(1)}, u32[]{:S(2)}, u32[]{:S(2)}) collective-permute-start(bf16[512,512]{1,0:T(8,128)(2,1)S(1)} %reshape.104), channel_id=1, source_target_pairs={{0,3},{1,0},{2,1},{3,2},{4,7},{5,4},{6,5},{7,6},{8,11},{9,8},{10,9... | collective-permute-start | bytes 1572872 | tf_op jit(solution)/shard_map/ppermute | solution.py:27
  47.4 0.0 copy-start.2
  47.4 1.5 %fusion.26 = f32[512,352]{0,1:T(8,128)S(1)} fusion(bf16[512,512]{1,0:T(8,128)(2,1)S(1)} %reshape.104, bf16[1,2048,352]{1,2,0:T(8,128)(2,1)} %param.13, s32[]{:T(128)S(6)} %select_n.63), kind=kOutput, calls=%fused_computation.40 | convolution fusion | flops 184549376 | bytes 1605636 | tf_op jit(solution)/shard_map/dot_general | solution.py:71
  48.9 0.0 copy-done.2
  48.9 0.0 copy-start.1
  48.9 0.4 fusion.20
  49.3 6.0 %collective-permute-done = bf16[512,512]{1,0:T(8,128)(2,1)S(1)} collective-permute-done((bf16[512,512]{1,0:T(8,128)(2,1)S(1)}, bf16[512,512]{1,0:T(8,128)(2,1)S(1)}, u32[]{:S(2)}, u32[]{:S(2)}) %collective-permute-start) | collective-permute-done | bytes 524320 | tf_op jit(solution)/shard_map/ppermute | solution.py:26
  55.4 1.9 %collective-permute-start.2 = (bf16[256,512]{1,0:T(8,128)(2,1)S(1)}, bf16[256,512]{1,0:T(8,128)(2,1)S(1)}, u32[]{:S(2)}, u32[]{:S(2)}) collective-permute-start(bf16[256,512]{1,0:T(8,128)(2,1)S(1)} %slice.72), channel_id=1, source_target_pairs={{0,1},{1,2},{2,3},{3,0},{4,5},{5,6},{6,7},{7,4},{8,9},{9,10},{10,1... | collective-permute-start | bytes 786440 | tf_op jit(solution)/shard_map/ppermute | solution.py:28
  57.3 0.0 collective-permute-done.1
  57.3 4.6 %collective-permute-start.3 = (bf16[256,512]{1,0:T(8,128)(2,1)S(1)}, bf16[256,512]{1,0:T(8,128)(2,1)S(1)}, u32[]{:S(2)}, u32[]{:S(2)}) collective-permute-start(bf16[256,512]{1,0:T(8,128)(2,1)S(1)} %slice.73), channel_id=1, source_target_pairs={{0,3},{1,0},{2,1},{3,2},{4,7},{5,4},{6,5},{7,6},{8,11},{9,8},{10,9... | collective-permute-start | bytes 786440 | tf_op jit(solution)/shard_map/ppermute | solution.py:29
  61.9 0.0 copy-done.1
  61.9 0.4 convolution_add_fusion.3
  62.3 0.4 convolution_add_fusion.1
  62.7 1.0 collective-permute-done.2
  63.7 1.5 %collective-permute-done.3 = bf16[256,512]{1,0:T(8,128)(2,1)S(1)} collective-permute-done((bf16[256,512]{1,0:T(8,128)(2,1)S(1)}, bf16[256,512]{1,0:T(8,128)(2,1)S(1)}, u32[]{:S(2)}, u32[]{:S(2)}) %collective-permute-start.3) | collective-permute-done | bytes 262176 | tf_op jit(solution)/shard_map/ppermute | solution.py:29
  65.2 0.4 fusion.22
  65.6 0.4 fusion.14
  66.0 0.4 fusion.3
  66.4 0.5 multiply_convert_fusion
  66.9 0.0 copy-done
  66.9 0.5 fusion.1
  67.4 0.3 convolution_convert_fusion.5
  67.7 2.6 %collective-permute-start.4 = (bf16[256,512]{1,0:T(8,128)(2,1)S(1)}, bf16[256,512]{1,0:T(8,128)(2,1)S(1)}, u32[]{:S(2)}, u32[]{:S(2)}) collective-permute-start(bf16[256,512]{1,0:T(8,128)(2,1)S(1)} %convolution_convert_fusion.5), channel_id=1, source_target_pairs={{0,1},{1,2},{2,3},{3,0},{4,5},{5,6},{6,7},{7,4},{8,9},{9,10},{10,1... | collective-permute-start | bytes 786440 | tf_op jit(solution)/shard_map/ppermute | solution.py:11
  70.4 0.3 convolution_convert_fusion.4
  70.7 4.3 %collective-permute-start.6 = (bf16[256,512]{1,0:T(8,128)(2,1)S(1)}, bf16[256,512]{1,0:T(8,128)(2,1)S(1)}, u32[]{:S(2)}, u32[]{:S(2)}) collective-permute-start(bf16[256,512]{1,0:T(8,128)(2,1)S(1)} %convolution_convert_fusion.4), channel_id=1, source_target_pairs={{0,3},{1,0},{2,1},{3,2},{4,7},{5,4},{6,5},{7,6},{8,11},{9,8},{10,9... | collective-permute-start | bytes 786440 | tf_op jit(solution)/shard_map/ppermute | solution.py:12
  75.0 0.5 fusion.2
  75.5 1.0 collective-permute-done.4
  76.5 0.1 fusion.8
  76.6 0.1 convert_element_type.97
  76.7 1.9 %collective-permute-start.5 = (bf16[512,512]{1,0:T(8,128)(2,1)S(1)}, bf16[512,512]{1,0:T(8,128)(2,1)S(1)}, u32[]{:S(2)}, u32[]{:S(2)}) collective-permute-start(bf16[512,512]{1,0:T(8,128)(2,1)S(1)} %convert_element_type.97), channel_id=1, source_target_pairs={{0,1},{1,2},{2,3},{3,0},{4,5},{5,6},{6,7},{7,4},{8,9},{9,10},{10,1... | collective-permute-start | bytes 1572872 | tf_op jit(solution)/shard_map/ppermute | solution.py:17
  78.6 0.0 collective-permute-done.6
  78.6 0.1 fusion.7
  78.8 0.1 convert_element_type.103
  78.8 4.7 %collective-permute-start.7 = (bf16[512,512]{1,0:T(8,128)(2,1)S(1)}, bf16[512,512]{1,0:T(8,128)(2,1)S(1)}, u32[]{:S(2)}, u32[]{:S(2)}) collective-permute-start(bf16[512,512]{1,0:T(8,128)(2,1)S(1)} %convert_element_type.103), channel_id=1, source_target_pairs={{0,3},{1,0},{2,1},{3,2},{4,7},{5,4},{6,5},{7,6},{8,11},{9,8},{10,9... | collective-permute-start | bytes 1572872 | tf_op jit(solution)/shard_map/ppermute | solution.py:18
  83.5 0.5 fusion
  84.0 3.8 %collective-permute-done.5 = bf16[512,512]{1,0:T(8,128)(2,1)S(1)} collective-permute-done((bf16[512,512]{1,0:T(8,128)(2,1)S(1)}, bf16[512,512]{1,0:T(8,128)(2,1)S(1)}, u32[]{:S(2)}, u32[]{:S(2)}) %collective-permute-start.5) | collective-permute-done | bytes 524320 | tf_op jit(solution)/shard_map/ppermute | solution.py:17
  87.8 1.8 %collective-permute-done.7 = bf16[512,512]{1,0:T(8,128)(2,1)S(1)} collective-permute-done((bf16[512,512]{1,0:T(8,128)(2,1)S(1)}, bf16[512,512]{1,0:T(8,128)(2,1)S(1)}, u32[]{:S(2)}, u32[]{:S(2)}) %collective-permute-start.7) | collective-permute-done | bytes 524320 | tf_op jit(solution)/shard_map/ppermute | solution.py:18
  89.6 0.2 add_convert_fusion
  89.8 0.0 copy-start.4
  89.9 0.0 copy-start.3
  89.9 0.9 reshape.105
  90.8 16.5 %all-to-all-start.1 = ((bf16[128,4,512]{2,1,0:T(4,128)(2,1)}), bf16[128,4,512]{2,1,0:T(4,128)(2,1)S(1)}, u32[]{:S(2)}, u32[]{:S(2)}) async-start(bf16[128,4,512]{2,1,0:T(4,128)(2,1)} %reshape.105), calls=%async_computation.1 | async-start | bytes 1048576 | tf_op jit(solution)/shard_map/all_to_all | solution.py:86
  107.3 0.0 copy-done.4
  107.3 0.0 copy-done.3
  107.3 19.4 %all-to-all-done.1 = bf16[128,4,512]{2,1,0:T(4,128)(2,1)S(1)} async-done(((bf16[128,4,512]{2,1,0:T(4,128)(2,1)}), bf16[128,4,512]{2,1,0:T(4,128)(2,1)S(1)}, u32[]{:S(2)}, u32[]{:S(2)}) %all-to-all-start.1) | async-done | bytes 524320 | tf_op jit(solution)/shard_map/all_to_all | solution.py:86
  126.7 0.1 reshape.106
  126.8 0.3 convolution_multiply_fusion.1
  127.1 0.9 fusion.6
  (6 shorter events, 0.1 us)
Async XLA Ops:
  0.0 66.9 %copy-start = (bf16[1,352,2048]{2,1,0:T(8,128)(2,1)S(1)}, bf16[1,352,2048]{2,1,0:T(8,128)(2,1)}, u32[]{:S(2)}) copy-start(bf16[1,352,2048]{2,1,0:T(8,128)(2,1)} %param.15) | copy-start | bytes 4325380
  40.9 14.5 %collective-permute-start = (bf16[512,512]{1,0:T(8,128)(2,1)S(1)}, bf16[512,512]{1,0:T(8,128)(2,1)S(1)}, u32[]{:S(2)}, u32[]{:S(2)}) collective-permute-start(bf16[512,512]{1,0:T(8,128)(2,1)S(1)} %reshape.104), channel_id=1, source_target_pairs={{0,1},{1,2},{2,3},{3,0},{4,5},{5,6},{6,7},{7,4},{8,9},{9,10},{10,1... | collective-permute-start | bytes 1572872 | tf_op jit(solution)/shard_map/ppermute | solution.py:26
  44.0 13.3 %collective-permute-start.1 = (bf16[512,512]{1,0:T(8,128)(2,1)S(1)}, bf16[512,512]{1,0:T(8,128)(2,1)S(1)}, u32[]{:S(2)}, u32[]{:S(2)}) collective-permute-start(bf16[512,512]{1,0:T(8,128)(2,1)S(1)} %reshape.104), channel_id=1, source_target_pairs={{0,3},{1,0},{2,1},{3,2},{4,7},{5,4},{6,5},{7,6},{8,11},{9,8},{10,9... | collective-permute-start | bytes 1572872 | tf_op jit(solution)/shard_map/ppermute | solution.py:27
  47.4 1.5 %copy-start.2 = (bf16[1,2048,352]{1,2,0:T(8,128)(2,1)S(1)}, bf16[1,2048,352]{1,2,0:T(8,128)(2,1)}, u32[]{:S(2)}) copy-start(bf16[1,2048,352]{1,2,0:T(8,128)(2,1)} %param.14) | copy-start | bytes 4325380
  48.9 13.0 %copy-start.1 = (bf16[1,2048,352]{1,2,0:T(8,128)(2,1)S(1)}, bf16[1,2048,352]{1,2,0:T(8,128)(2,1)}, u32[]{:S(2)}) copy-start(bf16[1,2048,352]{1,2,0:T(8,128)(2,1)} %param.13) | copy-start | bytes 4325380
  55.4 8.3 %collective-permute-start.2 = (bf16[256,512]{1,0:T(8,128)(2,1)S(1)}, bf16[256,512]{1,0:T(8,128)(2,1)S(1)}, u32[]{:S(2)}, u32[]{:S(2)}) collective-permute-start(bf16[256,512]{1,0:T(8,128)(2,1)S(1)} %slice.72), channel_id=1, source_target_pairs={{0,1},{1,2},{2,3},{3,0},{4,5},{5,6},{6,7},{7,4},{8,9},{9,10},{10,1... | collective-permute-start | bytes 786440 | tf_op jit(solution)/shard_map/ppermute | solution.py:28
  57.3 7.9 %collective-permute-start.3 = (bf16[256,512]{1,0:T(8,128)(2,1)S(1)}, bf16[256,512]{1,0:T(8,128)(2,1)S(1)}, u32[]{:S(2)}, u32[]{:S(2)}) collective-permute-start(bf16[256,512]{1,0:T(8,128)(2,1)S(1)} %slice.73), channel_id=1, source_target_pairs={{0,3},{1,0},{2,1},{3,2},{4,7},{5,4},{6,5},{7,6},{8,11},{9,8},{10,9... | collective-permute-start | bytes 786440 | tf_op jit(solution)/shard_map/ppermute | solution.py:29
  67.7 8.8 %collective-permute-start.4 = (bf16[256,512]{1,0:T(8,128)(2,1)S(1)}, bf16[256,512]{1,0:T(8,128)(2,1)S(1)}, u32[]{:S(2)}, u32[]{:S(2)}) collective-permute-start(bf16[256,512]{1,0:T(8,128)(2,1)S(1)} %convolution_convert_fusion.5), channel_id=1, source_target_pairs={{0,1},{1,2},{2,3},{3,0},{4,5},{5,6},{6,7},{7,4},{8,9},{9,10},{10,1... | collective-permute-start | bytes 786440 | tf_op jit(solution)/shard_map/ppermute | solution.py:11
  70.7 7.9 %collective-permute-start.6 = (bf16[256,512]{1,0:T(8,128)(2,1)S(1)}, bf16[256,512]{1,0:T(8,128)(2,1)S(1)}, u32[]{:S(2)}, u32[]{:S(2)}) collective-permute-start(bf16[256,512]{1,0:T(8,128)(2,1)S(1)} %convolution_convert_fusion.4), channel_id=1, source_target_pairs={{0,3},{1,0},{2,1},{3,2},{4,7},{5,4},{6,5},{7,6},{8,11},{9,8},{10,9... | collective-permute-start | bytes 786440 | tf_op jit(solution)/shard_map/ppermute | solution.py:12
  76.7 11.1 %collective-permute-start.5 = (bf16[512,512]{1,0:T(8,128)(2,1)S(1)}, bf16[512,512]{1,0:T(8,128)(2,1)S(1)}, u32[]{:S(2)}, u32[]{:S(2)}) collective-permute-start(bf16[512,512]{1,0:T(8,128)(2,1)S(1)} %convert_element_type.97), channel_id=1, source_target_pairs={{0,1},{1,2},{2,3},{3,0},{4,5},{5,6},{6,7},{7,4},{8,9},{9,10},{10,1... | collective-permute-start | bytes 1572872 | tf_op jit(solution)/shard_map/ppermute | solution.py:17
  78.8 10.8 %collective-permute-start.7 = (bf16[512,512]{1,0:T(8,128)(2,1)S(1)}, bf16[512,512]{1,0:T(8,128)(2,1)S(1)}, u32[]{:S(2)}, u32[]{:S(2)}) collective-permute-start(bf16[512,512]{1,0:T(8,128)(2,1)S(1)} %convert_element_type.103), channel_id=1, source_target_pairs={{0,3},{1,0},{2,1},{3,2},{4,7},{5,4},{6,5},{7,6},{8,11},{9,8},{10,9... | collective-permute-start | bytes 1572872 | tf_op jit(solution)/shard_map/ppermute | solution.py:18
  89.8 17.4 %copy-start.4 = (f32[128,2]{0,1:T(2,128)S(1)}, f32[128,2]{0,1:T(2,128)}, u32[]{:S(2)}) copy-start(f32[128,2]{0,1:T(2,128)} %param.12) | copy-start | bytes 3076
  89.9 17.4 %copy-start.3 = (s32[128,2]{0,1:T(2,128)S(1)}, s32[128,2]{0,1:T(2,128)}, u32[]{:S(2)}) copy-start(s32[128,2]{0,1:T(2,128)} %param.11) | copy-start | bytes 3076
  90.8 35.9 %all-to-all-start.1 = ((bf16[128,4,512]{2,1,0:T(4,128)(2,1)}), bf16[128,4,512]{2,1,0:T(4,128)(2,1)S(1)}, u32[]{:S(2)}, u32[]{:S(2)}) async-start(bf16[128,4,512]{2,1,0:T(4,128)(2,1)} %reshape.105), calls=%async_computation.1 | async-start | bytes 1048576 | tf_op jit(solution)/shard_map/all_to_all | solution.py:86

commit v11 on v10

--- a/solution.py
+++ b/solution.py
@@ -61,8 +61,9 @@
     arrived = lax.all_to_all(
         outbound.reshape(experts, capacity, quarter), "ep", split_axis=0, concat_axis=0, tiled=True
     )
-    arrived = arrived.reshape(row_count, quarter)
-    pieces = ring_all_gather(arrived, groups, row_count)
+    pieces = [
+        (k, piece.reshape(row_count, quarter)) for k, piece in ring_all_gather(arrived, groups, experts)
+    ]
 
     def project(weight):
         acc = None

time: 130 us -> 141 us (1.085)
  matrix products: 8.68 us -> 17.3 us
  local copies, waits for them, and re-layouts: 2.2 us -> 9.11 us
  waiting for transfers between devices: 34.5 us -> 30.6 us
  starting transfers between devices: 43 us -> 40.9 us
    dot_general x8, matrix products: 4.25 us -> 12.9 us  [project(): term = jnp.dot(piece, rows, preferred_element_type=jnp.float32)]
    reshape x1 -> x4, local copies, waits for them, and re-layouts: 0.12 us -> 3.62 us  [shards(): piece.reshape(row_count, quarter)]
    slice x1, local copies, waits for them, and re-layouts: 0.02 us -> 1.75 us  [ring_all_gather(): far_b = lax.ppermute(from_hi[half:], 'tp', down)]
    slice x1, local copies, waits for them, and re-layouts: 0.02 us -> 1.74 us  [ring_all_gather(): far_a = lax.ppermute(from_lo[:half], 'tp', up)]
    ppermute x1, waiting for transfers between devices: 6.03 us -> 4.33 us  [ring_all_gather(): from_lo = lax.ppermute(block, 'tp', up)]
    all_to_all x1, starting transfers between devices: 16.5 us -> 14.8 us  [shards(): lax.all_to_all(summed.reshape(experts, capacity, quarter), 'ep', split_ax...]
    ppermute x1, waiting for transfers between devices: 1.49 us -> 0.01 us  [ring_all_gather(): far_b = lax.ppermute(from_hi[half:], 'tp', down)]
  transfers between devices with their start and end apart: 9 -> 9, of which waited for: 7 -> 5; matrix products, arithmetic and copies ran while one was open for 3% -> 11% of each run, Pallas kernels for 0% -> 0%
where the time goes in v11:
time: 141 us; the launch traced here: 139 us
  starting transfers between devices  40.9 us (29%)
  blocking collectives  37.7 us (27%)
  waiting for transfers between devices  30.6 us (22%)
  matrix products  17.3 us (12%)
  local copies, waits for them, and re-layouts  9.11 us (6%)
  other arithmetic  2.93 us (2%)
    all_to_all x1, blocking collectives, shards(): lax.all_to_all(outbound.reshape(experts, capacity, quarter), 'ep', split_...  37.7 us
    all_to_all x1, waiting for transfers between devices, shards(): lax.all_to_all(summed.reshape(experts, capacity, quarter), 'ep', split_ax...  19.4 us
    all_to_all x1, starting transfers between devices, shards(): lax.all_to_all(summed.reshape(experts, capacity, quarter), 'ep', split_ax...  14.8 us
    dot_general x8, matrix products, project(): term = jnp.dot(piece, rows, preferred_element_type=jnp.float32)  12.9 us
    ppermute x1, starting transfers between devices, ring_reduce_scatter(): from_hi = lax.ppermute(prev_dn.astype(jnp.bfloat16), 'tp', down)  4.68 us
    ppermute x1, waiting for transfers between devices, ring_reduce_scatter(): from_lo = lax.ppermute(next_up.astype(jnp.bfloat16), 'tp', up)  4.64 us
    ppermute x1, starting transfers between devices, ring_reduce_scatter(): lax.ppermute(quarter_of(2, half, rows).astype(jnp.bfloat16), 'tp', down)  4.57 us
    ppermute x1, starting transfers between devices, ring_all_gather(): far_b = lax.ppermute(from_hi[half:], 'tp', down)  4.56 us
  transfers between devices with their start and end apart: 9, of which 5 were waited for; matrix products, arithmetic and copies ran while one was open for 11% of the time, Pallas kernels for 0%

profile of v11, /device:TPU:1, one launch (start us, length us, event | category | flops | bytes accessed | tf_op | source)
XLA Modules:
  0.0 139.0 jit_solution(14961957245380646672)
XLA Ops:
  0.0 0.0 copy-start
  0.0 0.8 slice_bitcast_fusion.3
  0.8 0.2 select_reduce_fusion.1
  1.0 0.8 multiply_add_fusion
  1.8 1.2 convolution_convert_fusion.3
  3.0 0.1 reshape.112
  3.1 37.7 %all_to_all.10 = bf16[128,4,512]{2,1,0:T(4,128)(2,1)} all-to-all(bf16[128,4,512]{2,1,0:T(4,128)(2,1)S(1)} %reshape.112), channel_id=1, replica_groups=mesh['ep'=128,'tp'=4] {'ep'}, dimensions={0} | all-to-all | bytes 1048576 | tf_op jit(solution)/shard_map/all_to_all | solution.py:61
  40.8 3.1 %collective-permute-start = (bf16[128,4,512]{2,1,0:T(4,128)(2,1)}, bf16[128,4,512]{2,1,0:T(4,128)(2,1)}, u32[]{:S(2)}, u32[]{:S(2)}) collective-permute-start(bf16[128,4,512]{2,1,0:T(4,128)(2,1)} %all_to_all.10), channel_id=1, source_target_pairs={{0,1},{1,2},{2,3},{3,0},{4,5},{5,6},{6,7},{7,4},{8,9},{9,10},{10,1... | collective-permute-start | bytes 1572872 | tf_op jit(solution)/shard_map/ppermute | solution.py:26
  44.0 3.4 %collective-permute-start.1 = (bf16[128,4,512]{2,1,0:T(4,128)(2,1)}, bf16[128,4,512]{2,1,0:T(4,128)(2,1)}, u32[]{:S(2)}, u32[]{:S(2)}) collective-permute-start(bf16[128,4,512]{2,1,0:T(4,128)(2,1)} %all_to_all.10), channel_id=1, source_target_pairs={{0,3},{1,0},{2,1},{3,2},{4,7},{5,4},{6,5},{7,6},{8,11},{9,8},{10,9... | collective-permute-start | bytes 1572872 | tf_op jit(solution)/shard_map/ppermute | solution.py:27
  47.4 1.2 reshape.113
  48.6 1.4 fusion.26
  49.9 1.4 fusion.20
  51.3 4.3 %collective-permute-done = bf16[128,4,512]{2,1,0:T(4,128)(2,1)} collective-permute-done((bf16[128,4,512]{2,1,0:T(4,128)(2,1)}, bf16[128,4,512]{2,1,0:T(4,128)(2,1)}, u32[]{:S(2)}, u32[]{:S(2)}) %collective-permute-start) | collective-permute-done | bytes 524320 | tf_op jit(solution)/shard_map/ppermute | solution.py:26
  55.6 1.7 %slice.72 = bf16[64,4,512]{2,1,0:T(4,128)(2,1)} slice(bf16[128,4,512]{2,1,0:T(4,128)(2,1)} %collective-permute-done), slice={[0:64], [0:4], [0:512]} | slice | bytes 524288 | tf_op jit(solution)/shard_map/slice | solution.py:28
  57.4 1.9 %collective-permute-start.2 = (bf16[64,4,512]{2,1,0:T(4,128)(2,1)}, bf16[64,4,512]{2,1,0:T(4,128)(2,1)}, u32[]{:S(2)}, u32[]{:S(2)}) collective-permute-start(bf16[64,4,512]{2,1,0:T(4,128)(2,1)} %slice.72), channel_id=1, source_target_pairs={{0,1},{1,2},{2,3},{3,0},{4,5},{5,6},{6,7},{7,4},{8,9},{9,10},{10,1... | collective-permute-start | bytes 786440 | tf_op jit(solution)/shard_map/ppermute | solution.py:28
  59.3 0.0 collective-permute-done.1
  59.3 1.7 %slice.73 = bf16[64,4,512]{2,1,0:T(4,128)(2,1)} slice(bf16[128,4,512]{2,1,0:T(4,128)(2,1)} %collective-permute-done.1), slice={[64:128], [0:4], [0:512]} | slice | bytes 524288 | tf_op jit(solution)/shard_map/slice | solution.py:29
  61.1 4.6 %collective-permute-start.3 = (bf16[64,4,512]{2,1,0:T(4,128)(2,1)}, bf16[64,4,512]{2,1,0:T(4,128)(2,1)}, u32[]{:S(2)}, u32[]{:S(2)}) collective-permute-start(bf16[64,4,512]{2,1,0:T(4,128)(2,1)} %slice.73), channel_id=1, source_target_pairs={{0,3},{1,0},{2,1},{3,2},{4,7},{5,4},{6,5},{7,6},{8,11},{9,8},{10,9... | collective-permute-start | bytes 786440 | tf_op jit(solution)/shard_map/ppermute | solution.py:29
  65.6 1.2 reshape.114
  66.8 2.2 %convolution_add_fusion.3 = f32[512,352]{0,1:T(8,128)} fusion(f32[512,352]{0,1:T(8,128)S(1)} %fusion.26, bf16[512,512]{1,0:T(8,128)(2,1)S(1)} %reshape.114, bf16[1,2048,352]{1,2,0:T(8,128)(2,1)} %param.13, s32[]{:T(128)S(6)} %select_n.65), kind=kOutput, calls=%fused_computation.10 | convolution fusion | flops 184729600 | bytes 2326532 | tf_op jit(solution)/shard_map/dot_general | solution.py:72
  69.0 1.2 reshape.115
  70.2 2.2 %convolution_add_fusion.1 = f32[512,352]{0,1:T(8,128)} fusion(f32[512,352]{0,1:T(8,128)S(1)} %fusion.20, bf16[512,512]{1,0:T(8,128)(2,1)S(1)} %reshape.114, bf16[1,2048,352]{1,2,0:T(8,128)(2,1)} %param.14, s32[]{:T(128)S(6)} %select_n.65), kind=kOutput, calls=%fused_computation.8 | convolution fusion | flops 184729600 | bytes 2326532 | tf_op jit(solution)/shard_map/dot_general | solution.py:72
  72.4 0.0 collective-permute-done.2
  72.5 0.0 collective-permute-done.3
  72.5 1.4 pad_maximum_fusion
  73.8 0.1 reshape.116
  74.0 0.0 copy-start.1
  74.0 1.4 %fusion.22 = f32[512,352]{0,1:T(8,128)S(1)} fusion(bf16[512,512]{1,0:T(8,128)(2,1)S(1)} %reshape.116, bf16[1,2048,352]{1,2,0:T(8,128)(2,1)} %param.13, s32[]{:T(128)S(6)} %select_n.69), kind=kOutput, calls=%fused_computation.37 | convolution fusion | flops 184549376 | bytes 1605636 | tf_op jit(solution)/shard_map/dot_general | solution.py:72
  75.4 1.4 fusion.14
  76.8 0.0 copy-done.1
  76.8 0.0 copy-start.2
  76.8 1.4 %fusion.3 = f32[512,352]{0,1:T(8,128)S(1)} fusion(f32[512,352]{0,1:T(8,128)S(1)} %fusion.22, f32[512,352]{0,1:T(8,128)S(1)} %copy-done.1, bf16[512,512]{1,0:T(8,128)(2,1)S(1)} %reshape.115, bf16[1,2048,352]{1,2,0:T(8,128)(2,1)} %param.13, s32[]{:T(128)S(6)} %select_n.67), kind=kOutput, calls=%fused_computation.11 | convolution fusion | flops 184909824 | bytes 3047428 | tf_op jit(solution)/shard_map/dot_general | solution.py:72
  78.3 0.0 copy-done.2
  78.3 1.4 %multiply_convert_fusion = bf16[512,352]{0,1:T(8,128)(2,1)S(1)} fusion(f32[512,352]{0,1:T(8,128)S(1)} %fusion.3, f32[512,352]{0,1:T(8,128)S(1)} %fusion.14, f32[512,352]{0,1:T(8,128)S(1)} %copy-done.2, bf16[512,512]{1,0:T(8,128)(2,1)S(1)} %reshape.115, bf16[1,2048,352]{1,2,0:T(8,128)(2,1)} %param.14, s32[]{:T(128)S(6)} %select_n.67), kind=kOutput, calls=%fused_computation.20 | convolution fusion | flops 185991168 | bytes 3407876 | tf_op jit(solution)/shard_map/dot_general | solution.py:72
  79.7 0.0 copy-done
  79.7 0.5 fusion.1
  80.2 0.3 convolution_convert_fusion.5
  80.5 1.9 %collective-permute-start.4 = (bf16[256,512]{1,0:T(8,128)(2,1)S(1)}, bf16[256,512]{1,0:T(8,128)(2,1)S(1)}, u32[]{:S(2)}, u32[]{:S(2)}) collective-permute-start(bf16[256,512]{1,0:T(8,128)(2,1)S(1)} %convolution_convert_fusion.5), channel_id=1, source_target_pairs={{0,1},{1,2},{2,3},{3,0},{4,5},{5,6},{6,7},{7,4},{8,9},{9,10},{10,1... | collective-permute-start | bytes 786440 | tf_op jit(solution)/shard_map/ppermute | solution.py:11
  82.5 0.3 convolution_convert_fusion.4
  82.8 4.6 %collective-permute-start.6 = (bf16[256,512]{1,0:T(8,128)(2,1)S(1)}, bf16[256,512]{1,0:T(8,128)(2,1)S(1)}, u32[]{:S(2)}, u32[]{:S(2)}) collective-permute-start(bf16[256,512]{1,0:T(8,128)(2,1)S(1)} %convolution_convert_fusion.4), channel_id=1, source_target_pairs={{0,3},{1,0},{2,1},{3,2},{4,7},{5,4},{6,5},{7,6},{8,11},{9,8},{10,9... | collective-permute-start | bytes 786440 | tf_op jit(solution)/shard_map/ppermute | solution.py:12
  87.4 0.5 fusion.2
  87.8 1.0 collective-permute-done.4
  88.8 0.1 fusion.8
  89.0 0.1 convert_element_type.97
  89.1 1.9 %collective-permute-start.5 = (bf16[512,512]{1,0:T(8,128)(2,1)S(1)}, bf16[512,512]{1,0:T(8,128)(2,1)S(1)}, u32[]{:S(2)}, u32[]{:S(2)}) collective-permute-start(bf16[512,512]{1,0:T(8,128)(2,1)S(1)} %convert_element_type.97), channel_id=1, source_target_pairs={{0,1},{1,2},{2,3},{3,0},{4,5},{5,6},{6,7},{7,4},{8,9},{9,10},{10,1... | collective-permute-start | bytes 1572872 | tf_op jit(solution)/shard_map/ppermute | solution.py:17
  91.0 0.0 collective-permute-done.6
  91.0 0.1 fusion.7
  91.1 0.1 convert_element_type.103
  91.2 4.7 %collective-permute-start.7 = (bf16[512,512]{1,0:T(8,128)(2,1)S(1)}, bf16[512,512]{1,0:T(8,128)(2,1)S(1)}, u32[]{:S(2)}, u32[]{:S(2)}) collective-permute-start(bf16[512,512]{1,0:T(8,128)(2,1)S(1)} %convert_element_type.103), channel_id=1, source_target_pairs={{0,3},{1,0},{2,1},{3,2},{4,7},{5,4},{6,5},{7,6},{8,11},{9,8},{10,9... | collective-permute-start | bytes 1572872 | tf_op jit(solution)/shard_map/ppermute | solution.py:18
  95.9 0.5 fusion
  96.4 4.6 %collective-permute-done.5 = bf16[512,512]{1,0:T(8,128)(2,1)S(1)} collective-permute-done((bf16[512,512]{1,0:T(8,128)(2,1)S(1)}, bf16[512,512]{1,0:T(8,128)(2,1)S(1)}, u32[]{:S(2)}, u32[]{:S(2)}) %collective-permute-start.5) | collective-permute-done | bytes 524320 | tf_op jit(solution)/shard_map/ppermute | solution.py:17
  101.0 1.2 collective-permute-done.7
  102.2 0.2 add_convert_fusion
  102.4 0.0 copy-start.4
  102.5 0.0 copy-start.3
  102.5 0.9 reshape.117
  103.4 14.8 %all-to-all-start.1 = ((bf16[128,4,512]{2,1,0:T(4,128)(2,1)}), bf16[128,4,512]{2,1,0:T(4,128)(2,1)S(1)}, u32[]{:S(2)}, u32[]{:S(2)}) async-start(bf16[128,4,512]{2,1,0:T(4,128)(2,1)} %reshape.117), calls=%async_computation.1 | async-start | bytes 1048576 | tf_op jit(solution)/shard_map/all_to_all | solution.py:87
  118.2 0.0 copy-done.4
  118.2 0.0 copy-done.3
  118.3 19.4 %all-to-all-done.1 = bf16[128,4,512]{2,1,0:T(4,128)(2,1)S(1)} async-done(((bf16[128,4,512]{2,1,0:T(4,128)(2,1)}), bf16[128,4,512]{2,1,0:T(4,128)(2,1)S(1)}, u32[]{:S(2)}, u32[]{:S(2)}) %all-to-all-start.1) | async-done | bytes 524320 | tf_op jit(solution)/shard_map/all_to_all | solution.py:87
  137.6 0.1 reshape.118
  137.8 0.3 convolution_multiply_fusion.1
  138.0 0.9 fusion.6
  (2 shorter events, 0.0 us)
Async XLA Ops:
  0.0 79.7 %copy-start = (bf16[1,352,2048]{2,1,0:T(8,128)(2,1)S(1)}, bf16[1,352,2048]{2,1,0:T(8,128)(2,1)}, u32[]{:S(2)}) copy-start(bf16[1,352,2048]{2,1,0:T(8,128)(2,1)} %param.15) | copy-start | bytes 4325380
  40.8 14.8 %collective-permute-start = (bf16[128,4,512]{2,1,0:T(4,128)(2,1)}, bf16[128,4,512]{2,1,0:T(4,128)(2,1)}, u32[]{:S(2)}, u32[]{:S(2)}) collective-permute-start(bf16[128,4,512]{2,1,0:T(4,128)(2,1)} %all_to_all.10), channel_id=1, source_target_pairs={{0,1},{1,2},{2,3},{3,0},{4,5},{5,6},{6,7},{7,4},{8,9},{9,10},{10,1... | collective-permute-start | bytes 1572872 | tf_op jit(solution)/shard_map/ppermute | solution.py:26
  44.0 15.4 %collective-permute-start.1 = (bf16[128,4,512]{2,1,0:T(4,128)(2,1)}, bf16[128,4,512]{2,1,0:T(4,128)(2,1)}, u32[]{:S(2)}, u32[]{:S(2)}) collective-permute-start(bf16[128,4,512]{2,1,0:T(4,128)(2,1)} %all_to_all.10), channel_id=1, source_target_pairs={{0,3},{1,0},{2,1},{3,2},{4,7},{5,4},{6,5},{7,6},{8,11},{9,8},{10,9... | collective-permute-start | bytes 1572872 | tf_op jit(solution)/shard_map/ppermute | solution.py:27
  57.4 15.1 %collective-permute-start.2 = (bf16[64,4,512]{2,1,0:T(4,128)(2,1)}, bf16[64,4,512]{2,1,0:T(4,128)(2,1)}, u32[]{:S(2)}, u32[]{:S(2)}) collective-permute-start(bf16[64,4,512]{2,1,0:T(4,128)(2,1)} %slice.72), channel_id=1, source_target_pairs={{0,1},{1,2},{2,3},{3,0},{4,5},{5,6},{6,7},{7,4},{8,9},{9,10},{10,1... | collective-permute-start | bytes 786440 | tf_op jit(solution)/shard_map/ppermute | solution.py:28
  61.1 11.4 %collective-permute-start.3 = (bf16[64,4,512]{2,1,0:T(4,128)(2,1)}, bf16[64,4,512]{2,1,0:T(4,128)(2,1)}, u32[]{:S(2)}, u32[]{:S(2)}) collective-permute-start(bf16[64,4,512]{2,1,0:T(4,128)(2,1)} %slice.73), channel_id=1, source_target_pairs={{0,3},{1,0},{2,1},{3,2},{4,7},{5,4},{6,5},{7,6},{8,11},{9,8},{10,9... | collective-permute-start | bytes 786440 | tf_op jit(solution)/shard_map/ppermute | solution.py:29
  74.0 2.8 %copy-start.1 = (f32[512,352]{0,1:T(8,128)S(1)}, f32[512,352]{0,1:T(8,128)}, u32[]{:S(2)}) copy-start(f32[512,352]{0,1:T(8,128)} %convolution_add_fusion.3) | copy-start | bytes 2162692
  76.8 1.5 %copy-start.2 = (f32[512,352]{0,1:T(8,128)S(1)}, f32[512,352]{0,1:T(8,128)}, u32[]{:S(2)}) copy-start(f32[512,352]{0,1:T(8,128)} %convolution_add_fusion.1) | copy-start | bytes 2162692
  80.5 8.3 %collective-permute-start.4 = (bf16[256,512]{1,0:T(8,128)(2,1)S(1)}, bf16[256,512]{1,0:T(8,128)(2,1)S(1)}, u32[]{:S(2)}, u32[]{:S(2)}) collective-permute-start(bf16[256,512]{1,0:T(8,128)(2,1)S(1)} %convolution_convert_fusion.5), channel_id=1, source_target_pairs={{0,1},{1,2},{2,3},{3,0},{4,5},{5,6},{6,7},{7,4},{8,9},{9,10},{10,1... | collective-permute-start | bytes 786440 | tf_op jit(solution)/shard_map/ppermute | solution.py:11
  82.8 8.2 %collective-permute-start.6 = (bf16[256,512]{1,0:T(8,128)(2,1)S(1)}, bf16[256,512]{1,0:T(8,128)(2,1)S(1)}, u32[]{:S(2)}, u32[]{:S(2)}) collective-permute-start(bf16[256,512]{1,0:T(8,128)(2,1)S(1)} %convolution_convert_fusion.4), channel_id=1, source_target_pairs={{0,3},{1,0},{2,1},{3,2},{4,7},{5,4},{6,5},{7,6},{8,11},{9,8},{10,9... | collective-permute-start | bytes 786440 | tf_op jit(solution)/shard_map/ppermute | solution.py:12
  89.1 11.9 %collective-permute-start.5 = (bf16[512,512]{1,0:T(8,128)(2,1)S(1)}, bf16[512,512]{1,0:T(8,128)(2,1)S(1)}, u32[]{:S(2)}, u32[]{:S(2)}) collective-permute-start(bf16[512,512]{1,0:T(8,128)(2,1)S(1)} %convert_element_type.97), channel_id=1, source_target_pairs={{0,1},{1,2},{2,3},{3,0},{4,5},{5,6},{6,7},{7,4},{8,9},{9,10},{10,1... | collective-permute-start | bytes 1572872 | tf_op jit(solution)/shard_map/ppermute | solution.py:17
  91.2 11.0 %collective-permute-start.7 = (bf16[512,512]{1,0:T(8,128)(2,1)S(1)}, bf16[512,512]{1,0:T(8,128)(2,1)S(1)}, u32[]{:S(2)}, u32[]{:S(2)}) collective-permute-start(bf16[512,512]{1,0:T(8,128)(2,1)S(1)} %convert_element_type.103), channel_id=1, source_target_pairs={{0,3},{1,0},{2,1},{3,2},{4,7},{5,4},{6,5},{7,6},{8,11},{9,8},{10,9... | collective-permute-start | bytes 1572872 | tf_op jit(solution)/shard_map/ppermute | solution.py:18
  102.4 15.8 %copy-start.4 = (f32[128,2]{0,1:T(2,128)S(1)}, f32[128,2]{0,1:T(2,128)}, u32[]{:S(2)}) copy-start(f32[128,2]{0,1:T(2,128)} %param.12) | copy-start | bytes 3076
  102.5 15.8 %copy-start.3 = (s32[128,2]{0,1:T(2,128)S(1)}, s32[128,2]{0,1:T(2,128)}, u32[]{:S(2)}) copy-start(s32[128,2]{0,1:T(2,128)} %param.11) | copy-start | bytes 3076
  103.4 34.2 %all-to-all-start.1 = ((bf16[128,4,512]{2,1,0:T(4,128)(2,1)}), bf16[128,4,512]{2,1,0:T(4,128)(2,1)S(1)}, u32[]{:S(2)}, u32[]{:S(2)}) async-start(bf16[128,4,512]{2,1,0:T(4,128)(2,1)} %reshape.117), calls=%async_computation.1 | async-start | bytes 1048576 | tf_op jit(solution)/shard_map/all_to_all | solution.py:87
